TPU v7x, 128 devices: a whole 4x4x4 slice. The times are simulated.
128 devices in a mesh: seq: 128 (over z, x, y, core).
Axes of the slice: x: 4, y: 4, z: 4, core: 2. Of those that a mesh axis runs over, the one named last changes fastest.
Arguments:
- tokens: bfloat16 [65536, 1536], P('seq'), may hold values from -6 to 6
- norm_gain: float32 [1536], replicated, may hold values from 0.5 to 1.5
- w_query: bfloat16 [1536, 1536], replicated
- w_key_value: bfloat16 [1536, 256], replicated
- w_out: bfloat16 [1536, 1536], replicated, may hold values from -1.75 to 1.75
- segment_ids: int32 [65536], P('seq'), may hold values from 0 to 63, as said below
- page_owner: int32 [4096], P('seq'), may hold values from 0 to 127, as said below
- page_slot: int32 [4096], P('seq'), may hold values from 0 to 127, as said below
Outputs:
- attn_out: bfloat16 [65536, 1536], P('seq')
- kv_cache: bfloat16 [262144, 256], P('seq')
Inputs may be any that keep to these rules, and one draw needn't show every extreme that they name: `segment_ids`: segments are contiguous runs of the stream, never falling, each of 1 to 4096 tokens; one has exactly 4096. `page_owner`: the 32 pages of one device go to different owners; some owner keeps a page of every device. `page_slot`: two pages with the same owner have different slots.
All inputs are finite; a program needn't handle non-finite values.
Results may differ from a plain program's by a relative error of at most 0.0086.
Values may be sent and summed in bfloat16 or wider, within the bound.
No kernel may reach another device: no remote copies, remote signals or barrier semaphores. Data moves between devices by JAX's collectives and lax.ppermute only.
A program may use at most 256 MiB of HBM per device.

v0:
```python
import jax
import jax.numpy as jnp
from jax import lax
from jax.sharding import PartitionSpec as P

WINDOW = 1024
PAGE = 16


EPS = 1e-06
ROPE_BASE = 10000.0


def carried_in(part, axis, combine, identity):
    place = lax.axis_index(axis)
    gathered = jax.tree.map(lambda a: lax.all_gather(a, axis), part)
    state = jax.tree.map(lambda a, e: jnp.zeros_like(a) + jnp.asarray(e, a.dtype), part, identity)

    def one(hop, state):
        return combine(
            state, jax.tree.map(lambda a: lax.dynamic_index_in_dim(a, hop, 0, False), gathered)
        )

    return lax.fori_loop(0, place, one, state)


def passed_along(value, axis, by):
    size = lax.axis_size(axis)
    pairs = [(i, i + by) for i in range(size) if 0 <= i + by < size]
    return lax.ppermute(value, axis, pairs)


def rotate(vectors, positions):
    width = vectors.shape[-1]
    half_dim = width // 2
    pair_index = jnp.arange(half_dim, dtype=jnp.float32)
    frequency = ROPE_BASE ** (-2.0 * pair_index / width)
    angles = positions.astype(jnp.float32)[:, None] * frequency[None, :]
    if vectors.ndim == 3:
        angles = angles[:, None, :]
    cosine = jnp.cos(angles)
    sine_part = jnp.sin(angles)
    first_half = vectors[..., :half_dim]
    second_half = vectors[..., half_dim:]
    return jnp.concatenate(
        [
            first_half * cosine - second_half * sine_part,
            second_half * cosine + first_half * sine_part,
        ],
        -1,
    )


def combine_runs(earlier, later):
    same_run = later[0] == earlier[0]
    missing = later[0] < 0
    run_id = jnp.where(missing, earlier[0], later[0])
    run_first = jnp.where(missing | same_run, earlier[1], later[1])
    return (run_id, run_first)


def body(tokens, norm_gain, w_query, w_key_value, w_out, segment_ids, page_owner, page_slot):
    row_count = tokens.shape[0]
    devices = lax.axis_size("seq")
    offset = lax.axis_index("seq") * row_count
    head_dim = w_key_value.shape[1] // 2
    head_count = w_query.shape[1] // head_dim
    local_index = jnp.arange(row_count, dtype=jnp.int32)
    global_index = offset + local_index
    change = jnp.concatenate([jnp.ones((1,), dtype=jnp.bool_), segment_ids[1:] != segment_ids[:-1]])
    local_start = lax.cummax(jnp.where(change, local_index, 0))
    last_run = (segment_ids[-1:], offset + local_start[-1:])
    empty_run = (jnp.full((1,), -1, jnp.int32), jnp.zeros((1,), jnp.int32))
    prior_id, prior_first = carried_in(last_run, "seq", combine_runs, empty_run)
    starts = jnp.where(segment_ids == prior_id, prior_first, offset + local_start)
    positions = global_index - starts
    wide = tokens.astype(jnp.float32)
    mean_square = jnp.mean(wide * wide, -1, keepdims=True)
    normed = (wide * lax.rsqrt(mean_square + EPS) * norm_gain).astype(jnp.bfloat16)
    queries = jnp.dot(normed, w_query, preferred_element_type=jnp.float32).reshape(
        row_count, head_count, head_dim
    )
    queries = (rotate(queries, positions) * head_dim ** (-0.5)).astype(jnp.bfloat16)
    projected = jnp.dot(normed, w_key_value, preferred_element_type=jnp.float32)
    keyval = jnp.concatenate(
        [rotate(projected[:, :head_dim], positions), projected[:, head_dim:]], 1
    ).astype(jnp.bfloat16)
    reach = WINDOW // row_count
    blocks = [keyval]
    moving = keyval
    for hop_step in range(reach):
        moving = passed_along(moving, "seq", 1)
        blocks.append(moving)
    ordered = blocks[::-1]
    block_firsts = [offset - (reach - place) * row_count for place in range(reach + 1)]

    def block_scores(block_rows, block_first):
        key_index = block_first + local_index
        valid = (
            (key_index[None, :] >= starts[:, None])
            & (key_index[None, :] <= global_index[:, None])
            & (global_index[:, None] - key_index[None, :] < WINDOW)
        )
        scores = jnp.einsum(
            "thd,kd->thk", queries, block_rows[:, :head_dim], preferred_element_type=jnp.float32
        )
        return jnp.where(valid[:, None, :], scores, -1e30)

    pieces = [block_scores(ordered[place], block_firsts[place]) for place in range(reach + 1)]
    scores = jnp.concatenate(pieces, 2)
    row_peak = jnp.max(scores, 2, keepdims=True)
    exponent = jnp.exp(scores - row_peak)
    probs = (exponent / jnp.sum(exponent, 2, keepdims=True)).astype(jnp.bfloat16)
    all_values = jnp.concatenate([block_rows[:, head_dim:] for block_rows in ordered], 0)
    context = jnp.einsum("thk,kd->thd", probs, all_values, preferred_element_type=jnp.float32)
    context = context.astype(jnp.bfloat16).reshape(row_count, head_count * head_dim)
    attn_out = jnp.dot(context, w_out, preferred_element_type=jnp.float32).astype(jnp.bfloat16)
    page_rows = keyval.reshape(row_count // PAGE, PAGE * 2 * head_dim)
    owner_hits = page_owner[:, None] == jnp.arange(devices, dtype=jnp.int32)[None, :]
    send_rows = jnp.einsum(
        "po,pc->oc", owner_hits.astype(jnp.bfloat16), page_rows, preferred_element_type=jnp.float32
    ).astype(jnp.bfloat16)
    send_slots = jnp.sum(jnp.where(owner_hits, page_slot[:, None] + 1, 0), 0) - 1
    got_rows, got_slots = (
        lax.all_to_all(send_rows, "seq", split_axis=0, concat_axis=0, tiled=True),
        lax.all_to_all(send_slots, "seq", split_axis=0, concat_axis=0, tiled=True),
    )
    placed = got_slots[None, :] == jnp.arange(devices, dtype=jnp.int32)[:, None]
    cache = jnp.dot(
        placed.astype(jnp.bfloat16), got_rows, preferred_element_type=jnp.float32
    ).astype(jnp.bfloat16)
    return (attn_out, cache.reshape(devices * PAGE, 2 * head_dim))


def solution(mesh):
    placed = (P("seq", None), P(), P(), P(), P(), P("seq"), P("seq"), P("seq"))
    return jax.shard_map(
        body,
        mesh=mesh,
        in_specs=placed,
        out_specs=(P("seq", None), P("seq", None)),
        check_vma=False,
    )
```

profile of v0, /device:TPU:32, one launch (start us, length us, event | category | flops | bytes accessed | tf_op | source)
XLA Modules:
  0.0 631.9 jit_solution(3704880574740571800)
XLA Ops:
  0.7 0.8 slice_compare_fusion
  2.2 0.8 slice_dynamic-update-slice_fusion
  3.2 65.7 %all-reduce.2 = (s32[128]{0:T(128)S(1)}, s32[128]{0:T(128)S(1)}) all-reduce(s32[128]{0:T(128)S(1)} %slice_dynamic-update-slice_fusion, s32[128]{0:T(128)S(1)} %add_dynamic-update-slice_fusion), channel_id=2, replica_groups=mesh['seq'=128] {'seq'}, use_global_device_ids=true, to_apply=%add | all-reduce | flops 256 | bytes 2048
  69.0 108.9 %while.12 = (s32[]{:T(128)}, s32[1]{0:T(128)}, s32[1]{0:T(128)}, s32[]{:T(128)}, s32[128,1]{0,1:T(1,128)S(1)}, /*index=5*/s32[128,1]{0,1:T(1,128)S(1)}, s32[]{:T(128)}, s32[]{:T(128)}, s32[]{:T(128)}, s32[1]{0:T(128)}) while((s32[]{:T(128)}, s32[1]{0:T(128)}, s32[1]{0:T(128)}, s32[]{:T(128)}, s32[128,1]{0,1:T(1,128)S(1)}, ...), condition=%wide.region_3.4_spmd, body=%wide.region_2.3_spmd.sunk | while | flops 10 | bytes 202 | solution.py:24
  177.9 1.8 fusion.4
  179.7 2.3 fusion.14
  182.7 5.2 collective-permute-start
  188.7 326.0 %all-to-all-start = ((s32[128,1,1]{2,1,0:T(1,128)}), s32[128,1,1]{2,1,0:T(1,128)S(1)}, u32[]{:S(2)}, u32[]{:S(2)}) async-start(s32[128,1,1]{2,1,0:T(1,128)} %copy.61), calls=%async_computation | async-start | bytes 131072 | tf_op jit(solution)/shard_map/all_to_all | solution.py:126
  515.5 4.7 fusion.16
  520.3 1.4 fusion.26
  521.7 3.3 copy.73
  525.0 2.3 copy.74
  527.3 4.1 multiply_subtract_fusion
  531.4 0.9 fusion.7
  532.2 1.1 fusion.11
  533.4 6.5 %fusion.27 = (f32[512,12]{0,1:T(8,128)S(1)}, f32[512,12,512]{0,2,1:T(8,128)}) fusion(bf16[512,12,128]{2,0,1:T(8,128)(2,1)S(1)} %fusion.7, bf16[512,256]{0,1:T(8,128)(2,1)S(1)} %maximum_convert_fusion, pred[512,512]{0,1:T(8,128)(4,1)S(1)} %get-tuple-element.63), kind=kOutput, calls=%fused_computation.72 | convolution fusion | flops 811591680 | bytes 14573568 | tf_op jit(solution)/shard_map/thd,kd->thk/dot_general | solution.py:104
  540.8 1.5 fusion.3
  543.5 2.0 reduce.6
  545.6 2.6 reshape.363
  548.2 10.2 %all-to-all-start.1 = ((bf16[128,2,2048]{2,1,0:T(2,128)(2,1)}), bf16[128,2,2048]{2,1,0:T(2,128)(2,1)}, u32[]{:S(2)}, u32[]{:S(2)}) async-start(bf16[128,2,2048]{2,1,0:T(2,128)(2,1)} %reshape.363), calls=%async_computation.1 | async-start | bytes 2097152 | tf_op jit(solution)/shard_map/all_to_all | solution.py:125
  558.4 2.4 reduce.4
  560.8 2.3 collective-permute-start.1
  563.0 7.3 %fusion.29 = (f32[512,12]{0,1:T(8,128)S(1)}, f32[512,12,512]{0,2,1:T(8,128)}) fusion(bf16[512,12,128]{2,0,1:T(8,128)(2,1)S(1)} %fusion.7, bf16[512,256]{0,1:T(8,128)(2,1)} %collective-permute-done, pred[512,512]{0,1:T(8,128)(4,1)S(1)} %get-tuple-element.64), kind=kOutput, calls=%fused_computation.74 | convolution fusion | flops 811591680 | bytes 14573568 | tf_op jit(solution)/shard_map/thd,kd->thk/dot_general | solution.py:104
  570.3 0.9 slice.76
  571.3 5.8 collective-permute-done.1
  577.1 6.5 %fusion.28 = (f32[512,12]{0,1:T(8,128)S(1)}, f32[512,12,512]{0,2,1:T(8,128)}) fusion(bf16[512,12,128]{2,0,1:T(8,128)(2,1)S(1)} %fusion.7, bf16[512,256]{0,1:T(8,128)(2,1)S(1)} %collective-permute-done.1, pred[512,512]{0,1:T(8,128)(4,1)S(1)} %get-tuple-element.62), kind=kOutput, calls=%fused_computation.73 | convolution fusion | flops 811591680 | bytes 14573568 | tf_op jit(solution)/shard_map/thd,kd->thk/dot_general | solution.py:104
  583.6 16.3 %fusion.1 = f32[512,12]{0,1:T(8,128)S(1)} fusion(f32[512,12,512]{0,2,1:T(8,128)} %get-tuple-element.68, f32[512,12,512]{0,2,1:T(8,128)} %get-tuple-element.72, f32[512,12,512]{0,2,1:T(8,128)} %get-tuple-element.70, f32[512,12]{0,1:T(8,128)S(1)} %maximum_maximum_fusion), kind=kLoop, calls=%fused_computation.5 | loop fusion | flops 37742592 | bytes 37797888 | tf_op jit(solution)/shard_map/reduce_sum | solution.py:113
  600.0 14.5 %fusion.8 = bf16[512,12,128]{0,2,1:T(8,128)(2,1)S(1)} fusion(f32[512,12,512]{0,2,1:T(8,128)} %get-tuple-element.68, f32[512,12,512]{0,2,1:T(8,128)} %get-tuple-element.72, f32[512,12,512]{0,2,1:T(8,128)} %get-tuple-element.70, f32[512,12]{0,1:T(8,128)S(1)} %fusion.1, f32[512,12]{0,1:T(8,128)S(1)} %maximum_maximum_fusion, ...), kind=kOutput, calls=%fused_computation.23 | convolution fusion | flops 2465071104 | bytes 39763968 | tf_op jit(solution)/shard_map/thk,kd->thd/dot_general | solution.py:115
  614.5 6.1 convolution_convert_fusion.2
  620.7 6.5 %reshape.364 = bf16[128,1,4096]{2,1,0:T(2,128)(2,1)S(1)} reshape(bf16[128,2,2048]{2,1,0:T(2,128)(2,1)} %all-to-all-done.1) | data formatting | bytes 2097152
  627.2 2.4 convolution_convert_fusion
  629.6 2.3 reshape.350
  (81 shorter events, 26.8 us)
Async XLA Ops:
  0.6 179.1 %copy-start = (bf16[1536,256]{1,0:T(8,128)(2,1)S(1)}, bf16[1536,256]{1,0:T(8,128)(2,1)}, u32[]{:S(2)}) copy-start(bf16[1536,256]{1,0:T(8,128)(2,1)} %param.13) | copy-start | bytes 2359300
  0.6 181.4 %copy-start.4 = (s32[512]{0:T(512)S(1)}, s32[512]{0:T(512)}, u32[]{:S(2)}) copy-start(s32[512]{0:T(512)} %param.15) | copy-start | bytes 6148
  177.9 10.0 %copy-start.7 = (s32[32]{0:T(128)S(1)}, s32[32]{0:T(128)}, u32[]{:S(2)}) copy-start(s32[32]{0:T(128)} %param.17) | copy-start | bytes 388
  177.9 10.0 %copy-start.5 = (s32[32]{0:T(128)S(1)}, s32[32]{0:T(128)}, u32[]{:S(2)}) copy-start(s32[32]{0:T(128)} %param.16) | copy-start | bytes 388
  179.7 335.8 %copy-start.2 = (bf16[512,1536]{1,0:T(8,128)(2,1)S(1)}, bf16[512,1536]{1,0:T(8,128)(2,1)}, u32[]{:S(2)}) copy-start(bf16[512,1536]{1,0:T(8,128)(2,1)} %param.10) | copy-start | bytes 4718596
  179.7 335.8 %copy-start.6 = (f32[1536]{0:T(1024)S(1)}, f32[1536]{0:T(1024)}, u32[]{:S(2)}) copy-start(f32[1536]{0:T(1024)} %param.11) | copy-start | bytes 18436
  182.7 378.1 %collective-permute-start = (bf16[512,256]{0,1:T(8,128)(2,1)S(1)}, bf16[512,256]{0,1:T(8,128)(2,1)}, u32[]{:S(2)}, u32[]{:S(2)}) collective-permute-start(bf16[512,256]{0,1:T(8,128)(2,1)S(1)} %maximum_convert_fusion), channel_id=1, source_target_pairs={{0,1},{1,2},{2,3},{3,4},{4,5},{5,6},{6,7},{7,8},{8,9},{9,10},{10,1... | collective-permute-start | bytes 786440 | tf_op jit(solution)/shard_map/ppermute | solution.py:30
  188.7 359.5 %all-to-all-start = ((s32[128,1,1]{2,1,0:T(1,128)}), s32[128,1,1]{2,1,0:T(1,128)S(1)}, u32[]{:S(2)}, u32[]{:S(2)}) async-start(s32[128,1,1]{2,1,0:T(1,128)} %copy.61), calls=%async_computation | async-start | bytes 131072 | tf_op jit(solution)/shard_map/all_to_all | solution.py:126
  548.2 72.5 %all-to-all-start.1 = ((bf16[128,2,2048]{2,1,0:T(2,128)(2,1)}), bf16[128,2,2048]{2,1,0:T(2,128)(2,1)}, u32[]{:S(2)}, u32[]{:S(2)}) async-start(bf16[128,2,2048]{2,1,0:T(2,128)(2,1)} %reshape.363), calls=%async_computation.1 | async-start | bytes 2097152 | tf_op jit(solution)/shard_map/all_to_all | solution.py:125
  560.8 16.3 %collective-permute-start.1 = (bf16[512,256]{0,1:T(8,128)(2,1)}, bf16[512,256]{0,1:T(8,128)(2,1)S(1)}, u32[]{:S(2)}, u32[]{:S(2)}) collective-permute-start(bf16[512,256]{0,1:T(8,128)(2,1)} %collective-permute-done), channel_id=1, source_target_pairs={{0,1},{1,2},{2,3},{3,4},{4,5},{5,6},{6,7},{7,8},{8,9},{9,10},{10,1... | collective-permute-start | bytes 786440 | tf_op jit(solution)/shard_map/ppermute | solution.py:30
  583.6 16.3 %copy-start.3 = (bf16[512,128]{0,1:T(8,128)(2,1)S(1)}, bf16[512,128]{0,1:T(8,128)(2,1)}, u32[]{:S(2)}) copy-start(bf16[512,128]{0,1:T(8,128)(2,1)} %slice.77) | copy-start | bytes 393220
  614.5 17.4 %copy-start.1 = (bf16[1536,256]{1,0:T(8,128)(2,1)S(1)}, bf16[1536,256]{1,0:T(8,128)(2,1)}, u32[]{:S(2)}) copy-start(bf16[1536,256]{1,0:T(8,128)(2,1)} %param.13) | copy-start | bytes 2359300
where the time goes:
time: 637 us; the launch traced here: 632 us
  starting transfers between devices  344 us (54%)
  loops' own time  87.5 us (14%)
  blocking collectives  65.7 us (10%)
  matrix products  51.9 us (8%)
  local copies, waits for them, and re-layouts  45.1 us (7%)
  other arithmetic  31.3 us (5%)
    all_to_all x1, starting transfers between devices, body(): lax.all_to_all(send_slots, 'seq', split_axis=0, concat_axis=0, tiled=True)  326 us
    another operation x1, loops' own time, carried_in(): return lax.fori_loop(0, place, one, state)  87.5 us
    unnamed x1, blocking collectives  65.7 us
    dynamic_slice x32, local copies, waits for them, and re-layouts, one(): lax.dynamic_index_in_dim(a, hop, 0, False)  21.4 us
    dot_general x3, matrix products, block_scores(): jnp.einsum('thd,kd->thk', queries, block_rows[:, :head_dim], preferred_el...  20.3 us
    reduce_sum x1, other arithmetic, body(): jnp.sum(exponent, 2, keepdims=True)  16.3 us
    unnamed x23, local copies, waits for them, and re-layouts  15.6 us
    dot_general x1, matrix products, body(): jnp.einsum('thk,kd->thd', probs, all_values, preferred_element_type=jnp.f...  14.5 us
  transfers between devices with their start and end apart: 4, of which 1 were waited for; matrix products, arithmetic and copies ran while one was open for 14% of the time, Pallas kernels for 0%

commit v1 on v0

--- a/solution.py
+++ b/solution.py
@@ -5,23 +5,11 @@
 
 WINDOW = 1024
 PAGE = 16
+MAXLEN = 4096
 
 
 EPS = 1e-06
 ROPE_BASE = 10000.0
-
-
-def carried_in(part, axis, combine, identity):
-    place = lax.axis_index(axis)
-    gathered = jax.tree.map(lambda a: lax.all_gather(a, axis), part)
-    state = jax.tree.map(lambda a, e: jnp.zeros_like(a) + jnp.asarray(e, a.dtype), part, identity)
-
-    def one(hop, state):
-        return combine(
-            state, jax.tree.map(lambda a: lax.dynamic_index_in_dim(a, hop, 0, False), gathered)
-        )
-
-    return lax.fori_loop(0, place, one, state)
 
 
 def passed_along(value, axis, by):
@@ -51,14 +39,6 @@
     )
 
 
-def combine_runs(earlier, later):
-    same_run = later[0] == earlier[0]
-    missing = later[0] < 0
-    run_id = jnp.where(missing, earlier[0], later[0])
-    run_first = jnp.where(missing | same_run, earlier[1], later[1])
-    return (run_id, run_first)
-
-
 def body(tokens, norm_gain, w_query, w_key_value, w_out, segment_ids, page_owner, page_slot):
     row_count = tokens.shape[0]
     devices = lax.axis_size("seq")
@@ -69,9 +49,15 @@
     global_index = offset + local_index
     change = jnp.concatenate([jnp.ones((1,), dtype=jnp.bool_), segment_ids[1:] != segment_ids[:-1]])
     local_start = lax.cummax(jnp.where(change, local_index, 0))
-    last_run = (segment_ids[-1:], offset + local_start[-1:])
-    empty_run = (jnp.full((1,), -1, jnp.int32), jnp.zeros((1,), jnp.int32))
-    prior_id, prior_first = carried_in(last_run, "seq", combine_runs, empty_run)
+    place = lax.axis_index("seq")
+    run_info = jnp.stack([segment_ids[-1], offset + local_start[-1]])
+    hops = min(devices - 1, -(-MAXLEN // row_count))
+    heard = [passed_along(run_info, "seq", hop) for hop in range(1, hops + 1)]
+    prior_id = jnp.where(place >= 1, heard[0][0], -1)
+    prior_first = offset
+    for hop in range(hops, 0, -1):
+        same = (place >= hop) & (heard[hop - 1][0] == prior_id)
+        prior_first = jnp.where(same, jnp.minimum(prior_first, heard[hop - 1][1]), prior_first)
     starts = jnp.where(segment_ids == prior_id, prior_first, offset + local_start)
     positions = global_index - starts
     wide = tokens.astype(jnp.float32)
@@ -116,18 +102,20 @@
     context = context.astype(jnp.bfloat16).reshape(row_count, head_count * head_dim)
     attn_out = jnp.dot(context, w_out, preferred_element_type=jnp.float32).astype(jnp.bfloat16)
     page_rows = keyval.reshape(row_count // PAGE, PAGE * 2 * head_dim)
+    width = page_rows.shape[1]
+    slot_tag = jnp.zeros((page_rows.shape[0], 128), jnp.bfloat16).at[:, 0].set(
+        (page_slot + 1).astype(jnp.bfloat16)
+    )
+    payload = jnp.concatenate([page_rows, slot_tag], 1)
     owner_hits = page_owner[:, None] == jnp.arange(devices, dtype=jnp.int32)[None, :]
     send_rows = jnp.einsum(
-        "po,pc->oc", owner_hits.astype(jnp.bfloat16), page_rows, preferred_element_type=jnp.float32
+        "po,pc->oc", owner_hits.astype(jnp.bfloat16), payload, preferred_element_type=jnp.float32
     ).astype(jnp.bfloat16)
-    send_slots = jnp.sum(jnp.where(owner_hits, page_slot[:, None] + 1, 0), 0) - 1
-    got_rows, got_slots = (
-        lax.all_to_all(send_rows, "seq", split_axis=0, concat_axis=0, tiled=True),
-        lax.all_to_all(send_slots, "seq", split_axis=0, concat_axis=0, tiled=True),
-    )
+    got = lax.all_to_all(send_rows, "seq", split_axis=0, concat_axis=0, tiled=True)
+    got_slots = got[:, width].astype(jnp.float32).astype(jnp.int32) - 1
     placed = got_slots[None, :] == jnp.arange(devices, dtype=jnp.int32)[:, None]
     cache = jnp.dot(
-        placed.astype(jnp.bfloat16), got_rows, preferred_element_type=jnp.float32
+        placed.astype(jnp.bfloat16), got[:, :width], preferred_element_type=jnp.float32
     ).astype(jnp.bfloat16)
     return (attn_out, cache.reshape(devices * PAGE, 2 * head_dim))
 

time: 637 us -> 163 us (0.26)
  starting transfers between devices: 344 us -> 42.2 us
  loops' own time: 87.5 us -> 0 us
  blocking collectives: 65.7 us -> 0 us
  local copies, waits for them, and re-layouts: 45.1 us -> 25 us
  between operations: 0.97 us -> 12.7 us
    all_to_all x1 -> x0, starting transfers between devices: 326 us -> none  [body(): lax.all_to_all(send_slots, 'seq', split_axis=0, concat_axis=0, tiled=True)]
    another operation x1 -> x0, loops' own time: 87.5 us -> none  [carried_in(): return lax.fori_loop(0, place, one, state)]
    unnamed x1 -> x0, blocking collectives: 65.7 us -> none
    ppermute x2 -> x10, starting transfers between devices: 7.42 us -> 31.7 us  [passed_along(): return lax.ppermute(value, axis, pairs)]
    dynamic_slice x32 -> x0, local copies, waits for them, and re-layouts: 21.4 us -> none  [one(): lax.dynamic_index_in_dim(a, hop, 0, False)]
    slice x1 -> x10, local copies, waits for them, and re-layouts: 0.07 us -> 6.67 us  [the longest x8 4.82 us: body(): heard[hop - 1][1]]
    unnamed x23 -> x19, local copies, waits for them, and re-layouts: 15.6 us -> 14.2 us
  transfers between devices with their start and end apart: 4 -> 11, of which waited for: 1 -> 1; matrix products, arithmetic and copies ran while one was open for 14% -> 55% of each run, Pallas kernels for 0% -> 0%
where the time goes in v1:
time: 163 us; the launch traced here: 162 us
  matrix products  48.1 us (30%)
  starting transfers between devices  42.2 us (26%)
  other arithmetic  30.2 us (19%)
  local copies, waits for them, and re-layouts  25 us (15%)
  between operations  12.7 us (8%)
  waiting for transfers between devices  3.44 us (2%)
    ppermute x10, starting transfers between devices, passed_along(): return lax.ppermute(value, axis, pairs)  31.7 us
    dot_general x3, matrix products, block_scores(): jnp.einsum('thd,kd->thk', queries, block_rows[:, :head_dim], preferred_el...  19.5 us
    reduce_sum x1, other arithmetic, body(): jnp.sum(exponent, 2, keepdims=True)  16.3 us
    dot_general x1, matrix products, body(): jnp.einsum('thk,kd->thd', probs, all_values, preferred_element_type=jnp.f...  14.5 us
    unnamed x19, local copies, waits for them, and re-layouts  14.2 us
    all_to_all x1, starting transfers between devices, body(): lax.all_to_all(send_rows, 'seq', split_axis=0, concat_axis=0, tiled=True)  10.6 us
    dot_general x1, matrix products, body(): jnp.dot(context, w_out, preferred_element_type=jnp.float32)  6.07 us
    slice x8, local copies, waits for them, and re-layouts, body(): heard[hop - 1][1]  4.82 us
  transfers between devices with their start and end apart: 11, of which 1 were waited for; matrix products, arithmetic and copies ran while one was open for 55% of the time, Pallas kernels for 0%

profile of v1, /device:TPU:32, one launch (start us, length us, event | category | flops | bytes accessed | tf_op | source)
XLA Modules:
  0.0 161.7 jit_solution(3038702940392767058)
XLA Ops:
  0.7 0.9 slice_compare_fusion
  1.6 1.3 slice.124
  5.5 1.9 %collective-permute-start = (s32[2]{0:T(128)S(1)}, s32[2]{0:T(128)S(1)}, u32[]{:S(2)}, u32[]{:S(2)}) collective-permute-start(s32[2]{0:T(128)S(1)} %pad_add_fusion), channel_id=1, source_target_pairs={{0,1},{1,2},{2,3},{3,4},{4,5},{5,6},{6,7},{7,8},{8,9},{9,10},{10,1... | collective-permute-start | bytes 32 | tf_op jit(solution)/shard_map/ppermute | solution.py:18
  7.4 3.4 %collective-permute-start.7 = (s32[2]{0:T(128)S(1)}, s32[2]{0:T(128)S(1)}, u32[]{:S(2)}, u32[]{:S(2)}) collective-permute-start(s32[2]{0:T(128)S(1)} %pad_add_fusion), channel_id=1, source_target_pairs={{0,8},{1,9},{2,10},{3,11},{4,12},{5,13},{6,14},{7,15},{8,16},{9,17... | collective-permute-start | bytes 32 | tf_op jit(solution)/shard_map/ppermute | solution.py:18
  10.8 5.5 %collective-permute-start.6 = (s32[2]{0:T(128)S(1)}, s32[2]{0:T(128)S(1)}, u32[]{:S(2)}, u32[]{:S(2)}) collective-permute-start(s32[2]{0:T(128)S(1)} %pad_add_fusion), channel_id=1, source_target_pairs={{0,7},{1,8},{2,9},{3,10},{4,11},{5,12},{6,13},{7,14},{8,15},{9,16}... | collective-permute-start | bytes 32 | tf_op jit(solution)/shard_map/ppermute | solution.py:18
  16.3 3.7 %collective-permute-start.5 = (s32[2]{0:T(128)S(1)}, s32[2]{0:T(128)S(1)}, u32[]{:S(2)}, u32[]{:S(2)}) collective-permute-start(s32[2]{0:T(128)S(1)} %pad_add_fusion), channel_id=1, source_target_pairs={{0,6},{1,7},{2,8},{3,9},{4,10},{5,11},{6,12},{7,13},{8,14},{9,15},... | collective-permute-start | bytes 32 | tf_op jit(solution)/shard_map/ppermute | solution.py:18
  20.1 1.9 %collective-permute-start.4 = (s32[2]{0:T(128)S(1)}, s32[2]{0:T(128)S(1)}, u32[]{:S(2)}, u32[]{:S(2)}) collective-permute-start(s32[2]{0:T(128)S(1)} %pad_add_fusion), channel_id=1, source_target_pairs={{0,5},{1,6},{2,7},{3,8},{4,9},{5,10},{6,11},{7,12},{8,13},{9,14},{... | collective-permute-start | bytes 32 | tf_op jit(solution)/shard_map/ppermute | solution.py:18
  22.6 1.8 %fusion.4 = f32[512]{0:T(512)S(1)} fusion(bf16[512,1536]{1,0:T(8,128)(2,1)} %param.10), kind=kLoop, calls=%fused_computation.13 | loop fusion | flops 2358784 | bytes 1574912 | tf_op jit(solution)/shard_map/reduce_sum | solution.py:64
  24.5 2.2 %fusion.14 = f32[512,256]{0,1:T(8,128)S(1)} fusion(bf16[1536,256]{1,0:T(8,128)(2,1)S(1)} %copy-done, bf16[512,1536]{1,0:T(8,128)(2,1)} %param.10, f32[1536]{0:T(1024)} %param.11, f32[512]{0:T(512)S(1)} %add_rsqrt_fusion), kind=kOutput, calls=%fused_computation.33 | convolution fusion | flops 405798912 | bytes 2891776 | tf_op jit(solution)/shard_map/dot_general | solution.py:70
  26.7 4.8 %fusion.16 = f32[512,1536]{0,1:T(8,128)S(1)} fusion(bf16[1536,1536]{1,0:T(8,128)(2,1)} %param.12, bf16[512,1536]{1,0:T(8,128)(2,1)S(1)} %copy-done.2, f32[1536]{0:T(1024)S(1)} %copy-done.5, f32[512]{0:T(512)S(1)} %add_rsqrt_fusion), kind=kOutput, calls=%fused_computation.34 | convolution fusion | flops 2419064832 | bytes 9445376 | tf_op jit(solution)/shard_map/dot_general | solution.py:66
  31.4 1.4 fusion.36
  32.9 3.3 %copy.63 = f32[512,12,64]{2,0,1:T(8,128)} copy(f32[512,12,64]{0,2,1:T(8,128)} %get-tuple-element.19) | data formatting | bytes 3145728
  36.2 2.2 %copy.64 = f32[512,12,64]{2,0,1:T(8,128)} copy(f32[512,12,64]{0,2,1:T(8,128)S(1)} %get-tuple-element.18) | data formatting | bytes 3145728
  39.2 4.6 %collective-permute-start.3 = (s32[2]{0:T(128)S(1)}, s32[2]{0:T(128)S(1)}, u32[]{:S(2)}, u32[]{:S(2)}) collective-permute-start(s32[2]{0:T(128)S(1)} %pad_add_fusion), channel_id=1, source_target_pairs={{0,4},{1,5},{2,6},{3,7},{4,8},{5,9},{6,10},{7,11},{8,12},{9,13},{1... | collective-permute-start | bytes 32 | tf_op jit(solution)/shard_map/ppermute | solution.py:18
  45.7 2.6 %collective-permute-start.2 = (s32[2]{0:T(128)S(1)}, s32[2]{0:T(128)S(1)}, u32[]{:S(2)}, u32[]{:S(2)}) collective-permute-start(s32[2]{0:T(128)S(1)} %pad_add_fusion), channel_id=1, source_target_pairs={{0,3},{1,4},{2,5},{3,6},{4,7},{5,8},{6,9},{7,10},{8,11},{9,12},{10... | collective-permute-start | bytes 32 | tf_op jit(solution)/shard_map/ppermute | solution.py:18
  50.2 4.1 %collective-permute-start.1 = (s32[2]{0:T(128)S(1)}, s32[2]{0:T(128)S(1)}, u32[]{:S(2)}, u32[]{:S(2)}) collective-permute-start(s32[2]{0:T(128)S(1)} %pad_add_fusion), channel_id=1, source_target_pairs={{0,2},{1,3},{2,4},{3,5},{4,6},{5,7},{6,8},{7,9},{8,10},{9,11},{10,... | collective-permute-start | bytes 32 | tf_op jit(solution)/shard_map/ppermute | solution.py:18
  67.6 1.9 %collective-permute-start.8 = (bf16[512,256]{0,1:T(8,128)(2,1)S(1)}, bf16[512,256]{0,1:T(8,128)(2,1)S(1)}, u32[]{:S(2)}, u32[]{:S(2)}) collective-permute-start(bf16[512,256]{0,1:T(8,128)(2,1)S(1)} %maximum_convert_fusion), channel_id=1, source_target_pairs={{0,1},{1,2},{2,3},{3,4},{4,5},{5,6},{6,7},{7,8},{8,9},{9,10},{10,1... | collective-permute-start | bytes 786440 | tf_op jit(solution)/shard_map/ppermute | solution.py:18
  71.1 1.4 reduce.15
  72.5 1.6 reshape.382
  74.1 10.6 %all-to-all-start = ((bf16[128,2,2112]{2,1,0:T(2,128)(2,1)}), bf16[128,2,2112]{2,1,0:T(2,128)(2,1)}, u32[]{:S(2)}, u32[]{:S(2)}) async-start(bf16[128,2,2112]{2,1,0:T(2,128)(2,1)} %reshape.382), calls=%async_computation | async-start | bytes 2228224 | tf_op jit(solution)/shard_map/all_to_all | solution.py:114
  84.7 4.1 %multiply_subtract_fusion = (f32[512,12,64]{2,0,1:T(8,128)S(1)}, f32[512,12,64]{2,0,1:T(8,128)S(1)}) fusion(f32[512,12,64]{2,0,1:T(8,128)} %copy.64, f32[512,12,64]{2,0,1:T(8,128)} %copy.63, f32[512,64]{1,0:T(8,128)S(1)} %copy.46, f32[512,64]{1,0:T(8,128)S(1)} %copy.44), kind=kLoop, calls=%fused_computation.19 | loop fusion | flops 2359296 | bytes 6553600 | tf_op jit(solution)/shard_map/sub | solution.py:35
  89.6 1.1 fusion.10
  90.8 6.5 %fusion.45 = (f32[512,12]{0,1:T(8,128)S(1)}, f32[512,12,512]{0,2,1:T(8,128)}) fusion(bf16[512,12,128]{2,0,1:T(8,128)(2,1)S(1)} %fusion.7, bf16[512,256]{0,1:T(8,128)(2,1)S(1)} %maximum_convert_fusion, pred[512,512]{0,1:T(8,128)(4,1)S(1)} %get-tuple-element.23), kind=kOutput, calls=%fused_computation.88 | convolution fusion | flops 811591680 | bytes 14573568 | tf_op jit(solution)/shard_map/thd,kd->thk/dot_general | solution.py:90
  97.3 2.0 %collective-permute-start.9 = (bf16[512,256]{0,1:T(8,128)(2,1)S(1)}, bf16[512,256]{0,1:T(8,128)(2,1)S(1)}, u32[]{:S(2)}, u32[]{:S(2)}) collective-permute-start(bf16[512,256]{0,1:T(8,128)(2,1)S(1)} %collective-permute-done.8), channel_id=1, source_target_pairs={{0,1},{1,2},{2,3},{3,4},{4,5},{5,6},{6,7},{7,8},{8,9},{9,10},{10,1... | collective-permute-start | bytes 786440 | tf_op jit(solution)/shard_map/ppermute | solution.py:18
  99.3 6.4 %fusion.47 = (f32[512,12]{0,1:T(8,128)S(1)}, f32[512,12,512]{0,2,1:T(8,128)}) fusion(bf16[512,12,128]{2,0,1:T(8,128)(2,1)S(1)} %fusion.7, bf16[512,256]{0,1:T(8,128)(2,1)S(1)} %collective-permute-done.8, pred[512,512]{0,1:T(8,128)(4,1)S(1)} %get-tuple-element.24), kind=kOutput, calls=%fused_computation.90 | convolution fusion | flops 811591680 | bytes 14573568 | tf_op jit(solution)/shard_map/thd,kd->thk/dot_general | solution.py:90
  105.8 3.4 %collective-permute-done.9 = bf16[512,256]{0,1:T(8,128)(2,1)S(1)} collective-permute-done((bf16[512,256]{0,1:T(8,128)(2,1)S(1)}, bf16[512,256]{0,1:T(8,128)(2,1)S(1)}, u32[]{:S(2)}, u32[]{:S(2)}) %collective-permute-start.9) | collective-permute-done | bytes 262176 | tf_op jit(solution)/shard_map/ppermute | solution.py:18
  109.2 6.6 %fusion.46 = (f32[512,12]{0,1:T(8,128)S(1)}, f32[512,12,512]{0,2,1:T(8,128)}) fusion(bf16[512,12,128]{2,0,1:T(8,128)(2,1)S(1)} %fusion.7, bf16[512,256]{0,1:T(8,128)(2,1)S(1)} %collective-permute-done.9, pred[512,512]{0,1:T(8,128)(4,1)S(1)} %get-tuple-element.22), kind=kOutput, calls=%fused_computation.89 | convolution fusion | flops 811591680 | bytes 14573568 | tf_op jit(solution)/shard_map/thd,kd->thk/dot_general | solution.py:90
  115.8 16.3 %fusion.1 = f32[512,12]{0,1:T(8,128)S(1)} fusion(f32[512,12,512]{0,2,1:T(8,128)} %get-tuple-element.44, f32[512,12,512]{0,2,1:T(8,128)} %get-tuple-element.48, f32[512,12,512]{0,2,1:T(8,128)} %get-tuple-element.46, f32[512,12]{0,1:T(8,128)S(1)} %maximum_maximum_fusion), kind=kLoop, calls=%fused_computation.3 | loop fusion | flops 37742592 | bytes 37797888 | tf_op jit(solution)/shard_map/reduce_sum | solution.py:99
  132.1 14.5 %fusion.8 = bf16[512,12,128]{0,2,1:T(8,128)(2,1)S(1)} fusion(f32[512,12,512]{0,2,1:T(8,128)} %get-tuple-element.44, f32[512,12,512]{0,2,1:T(8,128)} %get-tuple-element.48, f32[512,12,512]{0,2,1:T(8,128)} %get-tuple-element.46, f32[512,12]{0,1:T(8,128)S(1)} %fusion.1, f32[512,12]{0,1:T(8,128)S(1)} %maximum_maximum_fusion, bf16[512,128]{0,1:T(8,128)(2,1)S(1)} %slice.164, ...), kind=kOutput, calls=%fused_computation.21 | convolution fusion | flops 2465071104 | bytes 39763968 | tf_op jit(solution)/shard_map/thk,kd->thd/dot_general | solution.py:101
  146.7 6.1 %convolution_convert_fusion.2 = bf16[512,1536]{1,0:T(8,128)(2,1)} fusion(bf16[512,1536]{0,1:T(8,128)(2,1)S(1)} %bitcast.61, bf16[1536,1536]{1,0:T(8,128)(2,1)} %param.14), kind=kOutput, calls=%fused_computation.20 | convolution fusion | flops 2416705536 | bytes 7864320 | tf_op jit(solution)/shard_map/dot_general | solution.py:103
  152.8 7.0 %reshape.383 = bf16[128,1,4224]{2,1,0:T(2,128)(2,1)S(1)} reshape(bf16[128,2,2112]{2,1,0:T(2,128)(2,1)} %all-to-all-done) | data formatting | bytes 2162688
  160.4 1.3 reshape.375
  (65 shorter events, 12.6 us)
Async XLA Ops:
  0.6 23.8 %copy-start = (bf16[1536,256]{1,0:T(8,128)(2,1)S(1)}, bf16[1536,256]{1,0:T(8,128)(2,1)}, u32[]{:S(2)}) copy-start(bf16[1536,256]{1,0:T(8,128)(2,1)} %param.13) | copy-start | bytes 2359300
  0.6 26.0 %copy-start.2 = (bf16[512,1536]{1,0:T(8,128)(2,1)S(1)}, bf16[512,1536]{1,0:T(8,128)(2,1)}, u32[]{:S(2)}) copy-start(bf16[512,1536]{1,0:T(8,128)(2,1)} %param.10) | copy-start | bytes 4718596
  0.7 26.0 %copy-start.5 = (f32[1536]{0:T(1024)S(1)}, f32[1536]{0:T(1024)}, u32[]{:S(2)}) copy-start(f32[1536]{0:T(1024)} %param.11) | copy-start | bytes 18436
  5.5 33.7 %collective-permute-start = (s32[2]{0:T(128)S(1)}, s32[2]{0:T(128)S(1)}, u32[]{:S(2)}, u32[]{:S(2)}) collective-permute-start(s32[2]{0:T(128)S(1)} %pad_add_fusion), channel_id=1, source_target_pairs={{0,1},{1,2},{2,3},{3,4},{4,5},{5,6},{6,7},{7,8},{8,9},{9,10},{10,1... | collective-permute-start | bytes 32 | tf_op jit(solution)/shard_map/ppermute | solution.py:18
  7.4 38.3 %collective-permute-start.7 = (s32[2]{0:T(128)S(1)}, s32[2]{0:T(128)S(1)}, u32[]{:S(2)}, u32[]{:S(2)}) collective-permute-start(s32[2]{0:T(128)S(1)} %pad_add_fusion), channel_id=1, source_target_pairs={{0,8},{1,9},{2,10},{3,11},{4,12},{5,13},{6,14},{7,15},{8,16},{9,17... | collective-permute-start | bytes 32 | tf_op jit(solution)/shard_map/ppermute | solution.py:18
  10.8 39.4 %collective-permute-start.6 = (s32[2]{0:T(128)S(1)}, s32[2]{0:T(128)S(1)}, u32[]{:S(2)}, u32[]{:S(2)}) collective-permute-start(s32[2]{0:T(128)S(1)} %pad_add_fusion), channel_id=1, source_target_pairs={{0,7},{1,8},{2,9},{3,10},{4,11},{5,12},{6,13},{7,14},{8,15},{9,16}... | collective-permute-start | bytes 32 | tf_op jit(solution)/shard_map/ppermute | solution.py:18
  16.3 39.3 %collective-permute-start.5 = (s32[2]{0:T(128)S(1)}, s32[2]{0:T(128)S(1)}, u32[]{:S(2)}, u32[]{:S(2)}) collective-permute-start(s32[2]{0:T(128)S(1)} %pad_add_fusion), channel_id=1, source_target_pairs={{0,6},{1,7},{2,8},{3,9},{4,10},{5,11},{6,12},{7,13},{8,14},{9,15},... | collective-permute-start | bytes 32 | tf_op jit(solution)/shard_map/ppermute | solution.py:18
  20.1 36.8 %collective-permute-start.4 = (s32[2]{0:T(128)S(1)}, s32[2]{0:T(128)S(1)}, u32[]{:S(2)}, u32[]{:S(2)}) collective-permute-start(s32[2]{0:T(128)S(1)} %pad_add_fusion), channel_id=1, source_target_pairs={{0,5},{1,6},{2,7},{3,8},{4,9},{5,10},{6,11},{7,12},{8,13},{9,14},{... | collective-permute-start | bytes 32 | tf_op jit(solution)/shard_map/ppermute | solution.py:18
  36.2 2.3 %copy-start.6 = (s32[32]{0:T(128)S(1)}, s32[32]{0:T(128)}, u32[]{:S(2)}) copy-start(s32[32]{0:T(128)} %param.17) | copy-start | bytes 388
  36.2 30.2 %copy-start.3 = (s32[512]{0:T(512)S(1)}, s32[512]{0:T(512)}, u32[]{:S(2)}) copy-start(s32[512]{0:T(512)} %param.15) | copy-start | bytes 6148
  36.2 33.9 %copy-start.4 = (s32[32]{0:T(128)S(1)}, s32[32]{0:T(128)}, u32[]{:S(2)}) copy-start(s32[32]{0:T(128)} %param.16) | copy-start | bytes 388
  39.2 18.9 %collective-permute-start.3 = (s32[2]{0:T(128)S(1)}, s32[2]{0:T(128)S(1)}, u32[]{:S(2)}, u32[]{:S(2)}) collective-permute-start(s32[2]{0:T(128)S(1)} %pad_add_fusion), channel_id=1, source_target_pairs={{0,4},{1,5},{2,6},{3,7},{4,8},{5,9},{6,10},{7,11},{8,12},{9,13},{1... | collective-permute-start | bytes 32 | tf_op jit(solution)/shard_map/ppermute | solution.py:18
  45.7 13.7 %collective-permute-start.2 = (s32[2]{0:T(128)S(1)}, s32[2]{0:T(128)S(1)}, u32[]{:S(2)}, u32[]{:S(2)}) collective-permute-start(s32[2]{0:T(128)S(1)} %pad_add_fusion), channel_id=1, source_target_pairs={{0,3},{1,4},{2,5},{3,6},{4,7},{5,8},{6,9},{7,10},{8,11},{9,12},{10... | collective-permute-start | bytes 32 | tf_op jit(solution)/shard_map/ppermute | solution.py:18
  50.2 10.5 %collective-permute-start.1 = (s32[2]{0:T(128)S(1)}, s32[2]{0:T(128)S(1)}, u32[]{:S(2)}, u32[]{:S(2)}) collective-permute-start(s32[2]{0:T(128)S(1)} %pad_add_fusion), channel_id=1, source_target_pairs={{0,2},{1,3},{2,4},{3,5},{4,6},{5,7},{6,8},{7,9},{8,10},{9,11},{10,... | collective-permute-start | bytes 32 | tf_op jit(solution)/shard_map/ppermute | solution.py:18
  67.6 29.7 %collective-permute-start.8 = (bf16[512,256]{0,1:T(8,128)(2,1)S(1)}, bf16[512,256]{0,1:T(8,128)(2,1)S(1)}, u32[]{:S(2)}, u32[]{:S(2)}) collective-permute-start(bf16[512,256]{0,1:T(8,128)(2,1)S(1)} %maximum_convert_fusion), channel_id=1, source_target_pairs={{0,1},{1,2},{2,3},{3,4},{4,5},{5,6},{6,7},{7,8},{8,9},{9,10},{10,1... | collective-permute-start | bytes 786440 | tf_op jit(solution)/shard_map/ppermute | solution.py:18
  74.1 78.6 %all-to-all-start = ((bf16[128,2,2112]{2,1,0:T(2,128)(2,1)}), bf16[128,2,2112]{2,1,0:T(2,128)(2,1)}, u32[]{:S(2)}, u32[]{:S(2)}) async-start(bf16[128,2,2112]{2,1,0:T(2,128)(2,1)} %reshape.382), calls=%async_computation | async-start | bytes 2228224 | tf_op jit(solution)/shard_map/all_to_all | solution.py:114
  97.3 11.9 %collective-permute-start.9 = (bf16[512,256]{0,1:T(8,128)(2,1)S(1)}, bf16[512,256]{0,1:T(8,128)(2,1)S(1)}, u32[]{:S(2)}, u32[]{:S(2)}) collective-permute-start(bf16[512,256]{0,1:T(8,128)(2,1)S(1)} %collective-permute-done.8), channel_id=1, source_target_pairs={{0,1},{1,2},{2,3},{3,4},{4,5},{5,6},{6,7},{7,8},{8,9},{9,10},{10,1... | collective-permute-start | bytes 786440 | tf_op jit(solution)/shard_map/ppermute | solution.py:18
  152.7 8.9 %copy-start.1 = (bf16[1536,256]{1,0:T(8,128)(2,1)S(1)}, bf16[1536,256]{1,0:T(8,128)(2,1)}, u32[]{:S(2)}) copy-start(bf16[1536,256]{1,0:T(8,128)(2,1)} %param.13) | copy-start | bytes 2359300

commit v2 on v1

--- a/solution.py
+++ b/solution.py
@@ -1,7 +1,11 @@
+import functools
+
 import jax
 import jax.numpy as jnp
 from jax import lax
 from jax.sharding import PartitionSpec as P
+from jax.experimental import pallas as pl
+from jax.experimental.pallas import tpu as pltpu
 
 WINDOW = 1024
 PAGE = 16
@@ -37,6 +41,48 @@
         ],
         -1,
     )
+
+
+def attend_kernel(query_ref, keyval_ref, first_ref, out_ref, *, tile, back, head_count, head_dim):
+    step = pl.program_id(0)
+    span = tile + WINDOW
+    key_first = pl.multiple_of(step * tile + back - WINDOW, tile)
+    rows = keyval_ref[pl.ds(key_first, span), :]
+    keys = rows[:, :head_dim]
+    values = rows[:, head_dim:]
+    query_at = step * tile + lax.broadcasted_iota(jnp.int32, (tile, span), 0)
+    key_at = key_first - back + lax.broadcasted_iota(jnp.int32, (tile, span), 1)
+    valid = (key_at >= first_ref[...]) & (key_at <= query_at) & (query_at - key_at < WINDOW)
+    for head in range(head_count):
+        lanes = slice(head * head_dim, (head + 1) * head_dim)
+        scores = lax.dot_general(
+            query_ref[:, lanes], keys, (((1,), (1,)), ((), ())), preferred_element_type=jnp.float32
+        )
+        scores = jnp.where(valid, scores, -1e30)
+        peak = jnp.max(scores, 1, keepdims=True)
+        exponent = jnp.exp(scores - peak)
+        probs = (exponent / jnp.sum(exponent, 1, keepdims=True)).astype(jnp.bfloat16)
+        context = jnp.dot(probs, values, preferred_element_type=jnp.float32)
+        out_ref[:, lanes] = context.astype(out_ref.dtype)
+
+
+def attend(queries, keyval_rows, first_rel, back, tile=128):
+    row_count, width = queries.shape
+    head_dim = keyval_rows.shape[1] // 2
+    kernel = functools.partial(
+        attend_kernel, tile=tile, back=back, head_count=width // head_dim, head_dim=head_dim
+    )
+    return pl.pallas_call(
+        kernel,
+        grid=(row_count // tile,),
+        in_specs=[
+            pl.BlockSpec((tile, width), lambda i: (i, 0)),
+            pl.BlockSpec(keyval_rows.shape, lambda i: (0, 0)),
+            pl.BlockSpec((tile, 1), lambda i: (i, 0)),
+        ],
+        out_specs=pl.BlockSpec((tile, width), lambda i: (i, 0)),
+        out_shape=jax.ShapeDtypeStruct((row_count, width), jnp.bfloat16),
+    )(queries, keyval_rows, first_rel)
 
 
 def body(tokens, norm_gain, w_query, w_key_value, w_out, segment_ids, page_owner, page_slot):
@@ -78,28 +124,13 @@
         moving = passed_along(moving, "seq", 1)
         blocks.append(moving)
     ordered = blocks[::-1]
-    block_firsts = [offset - (reach - place) * row_count for place in range(reach + 1)]
-
-    def block_scores(block_rows, block_first):
-        key_index = block_first + local_index
-        valid = (
-            (key_index[None, :] >= starts[:, None])
-            & (key_index[None, :] <= global_index[:, None])
-            & (global_index[:, None] - key_index[None, :] < WINDOW)
-        )
-        scores = jnp.einsum(
-            "thd,kd->thk", queries, block_rows[:, :head_dim], preferred_element_type=jnp.float32
-        )
-        return jnp.where(valid[:, None, :], scores, -1e30)
-
-    pieces = [block_scores(ordered[place], block_firsts[place]) for place in range(reach + 1)]
-    scores = jnp.concatenate(pieces, 2)
-    row_peak = jnp.max(scores, 2, keepdims=True)
-    exponent = jnp.exp(scores - row_peak)
-    probs = (exponent / jnp.sum(exponent, 2, keepdims=True)).astype(jnp.bfloat16)
-    all_values = jnp.concatenate([block_rows[:, head_dim:] for block_rows in ordered], 0)
-    context = jnp.einsum("thk,kd->thd", probs, all_values, preferred_element_type=jnp.float32)
-    context = context.astype(jnp.bfloat16).reshape(row_count, head_count * head_dim)
+    back = reach * row_count
+    context = attend(
+        queries.reshape(row_count, head_count * head_dim),
+        jnp.concatenate(ordered, 0),
+        (starts - offset)[:, None],
+        back,
+    )
     attn_out = jnp.dot(context, w_out, preferred_element_type=jnp.float32).astype(jnp.bfloat16)
     page_rows = keyval.reshape(row_count // PAGE, PAGE * 2 * head_dim)
     width = page_rows.shape[1]

time: 163 us -> 144 us (0.88)
  matrix products: 48.1 us -> 14.9 us
  Pallas kernels: 0 us -> 27 us
  other arithmetic: 30.2 us -> 13.8 us
  waiting for transfers between devices: 3.44 us -> 12 us
  local copies, waits for them, and re-layouts: 25 us -> 20.3 us
    dot_general x4 -> x0, matrix products: 34.1 us -> none  [the longest x3 19.5 us: block_scores(): jnp.einsum('thd,kd->thk', queries, block_rows[:, :head_dim], preferred_el...]
    pallas_call x0 -> x1, Pallas kernels: none -> 27 us  [attend(): pl.pallas_call(kernel, grid=(row_count // tile,), in_specs=[pl.BlockSpec(...]
    reduce_sum x1 -> x0, other arithmetic: 16.3 us -> none  [body(): jnp.sum(exponent, 2, keepdims=True)]
    ppermute x10, waiting for transfers between devices: 3.44 us -> 12 us  [passed_along(): return lax.ppermute(value, axis, pairs)]
    unnamed x19 -> x16, local copies, waits for them, and re-layouts: 14.2 us -> 8.74 us
    dot_general x1, matrix products: 4.75 us -> 6.72 us  [body(): jnp.dot(normed, w_query, preferred_element_type=jnp.float32)]
    concatenate x0 -> x1, other arithmetic: none -> 1.88 us  [body(): jnp.concatenate(ordered, 0)]
  transfers between devices with their start and end apart: 11 -> 11, of which waited for: 1 -> 1; matrix products, arithmetic and copies ran while one was open for 55% -> 24% of each run, Pallas kernels for 0% -> 19%
where the time goes in v2:
time: 144 us; the launch traced here: 143 us
  starting transfers between devices  43 us (30%)
  Pallas kernels  27 us (19%)
  local copies, waits for them, and re-layouts  20.3 us (14%)
  matrix products  14.9 us (10%)
  other arithmetic  13.8 us (10%)
  between operations  12.3 us (9%)
  waiting for transfers between devices  12 us (8%)
    ppermute x10, starting transfers between devices, passed_along(): return lax.ppermute(value, axis, pairs)  32.9 us
    pallas_call x1, Pallas kernels, attend(): pl.pallas_call(kernel, grid=(row_count // tile,), in_specs=[pl.BlockSpec(...  27 us
    ppermute x10, waiting for transfers between devices, passed_along(): return lax.ppermute(value, axis, pairs)  12 us
    all_to_all x1, starting transfers between devices, body(): lax.all_to_all(send_rows, 'seq', split_axis=0, concat_axis=0, tiled=True)  10.1 us
    unnamed x16, local copies, waits for them, and re-layouts  8.74 us
    dot_general x1, matrix products, body(): jnp.dot(normed, w_query, preferred_element_type=jnp.float32)  6.72 us
    dot_general x1, matrix products, body(): jnp.dot(context, w_out, preferred_element_type=jnp.float32)  6.56 us
    slice x8, local copies, waits for them, and re-layouts, body(): heard[hop - 1][1]  4.88 us
  transfers between devices with their start and end apart: 11, of which 1 were waited for; matrix products, arithmetic and copies ran while one was open for 24% of the time, Pallas kernels for 19%

profile of v2, /device:TPU:32, one launch (start us, length us, event | category | flops | bytes accessed | tf_op | source)
XLA Modules:
  0.0 143.3 jit_solution(6021393608407227856)
XLA Ops:
  0.7 0.9 slice_compare_fusion
  1.6 1.3 slice.107
  4.8 0.7 pad_add_fusion
  5.5 1.9 %collective-permute-start = (s32[2]{0:T(128)S(1)}, s32[2]{0:T(128)S(1)}, u32[]{:S(2)}, u32[]{:S(2)}) collective-permute-start(s32[2]{0:T(128)S(1)} %pad_add_fusion), channel_id=1, source_target_pairs={{0,1},{1,2},{2,3},{3,4},{4,5},{5,6},{6,7},{7,8},{8,9},{9,10},{10,1... | collective-permute-start | bytes 32 | tf_op jit(solution)/shard_map/ppermute | solution.py:22
  7.4 3.5 %collective-permute-start.1 = (s32[2]{0:T(128)S(1)}, s32[2]{0:T(128)S(1)}, u32[]{:S(2)}, u32[]{:S(2)}) collective-permute-start(s32[2]{0:T(128)S(1)} %pad_add_fusion), channel_id=1, source_target_pairs={{0,2},{1,3},{2,4},{3,5},{4,6},{5,7},{6,8},{7,9},{8,10},{9,11},{10,... | collective-permute-start | bytes 32 | tf_op jit(solution)/shard_map/ppermute | solution.py:22
  10.9 4.2 %collective-permute-start.2 = (s32[2]{0:T(128)S(1)}, s32[2]{0:T(128)S(1)}, u32[]{:S(2)}, u32[]{:S(2)}) collective-permute-start(s32[2]{0:T(128)S(1)} %pad_add_fusion), channel_id=1, source_target_pairs={{0,3},{1,4},{2,5},{3,6},{4,7},{5,8},{6,9},{7,10},{8,11},{9,12},{10... | collective-permute-start | bytes 32 | tf_op jit(solution)/shard_map/ppermute | solution.py:22
  15.1 4.7 %collective-permute-start.3 = (s32[2]{0:T(128)S(1)}, s32[2]{0:T(128)S(1)}, u32[]{:S(2)}, u32[]{:S(2)}) collective-permute-start(s32[2]{0:T(128)S(1)} %pad_add_fusion), channel_id=1, source_target_pairs={{0,4},{1,5},{2,6},{3,7},{4,8},{5,9},{6,10},{7,11},{8,12},{9,13},{1... | collective-permute-start | bytes 32 | tf_op jit(solution)/shard_map/ppermute | solution.py:22
  19.8 3.7 %collective-permute-start.4 = (s32[2]{0:T(128)S(1)}, s32[2]{0:T(128)S(1)}, u32[]{:S(2)}, u32[]{:S(2)}) collective-permute-start(s32[2]{0:T(128)S(1)} %pad_add_fusion), channel_id=1, source_target_pairs={{0,5},{1,6},{2,7},{3,8},{4,9},{5,10},{6,11},{7,12},{8,13},{9,14},{... | collective-permute-start | bytes 32 | tf_op jit(solution)/shard_map/ppermute | solution.py:22
  23.5 0.6 compare_reduce_fusion
  24.1 1.8 %fusion.1 = f32[512]{0:T(512)S(1)} fusion(bf16[512,1536]{1,0:T(8,128)(2,1)} %param.10), kind=kLoop, calls=%fused_computation.5 | loop fusion | flops 2358784 | bytes 1574912 | tf_op jit(solution)/shard_map/reduce_sum | solution.py:110
  26.0 6.7 %fusion.9 = f32[512,1536]{0,1:T(8,128)} fusion(bf16[1536,1536]{1,0:T(8,128)(2,1)} %param.12, bf16[512,1536]{1,0:T(8,128)(2,1)S(1)} %copy-done.1, f32[1536]{0:T(1024)S(1)} %copy-done.4, f32[512]{0:T(512)S(1)} %add_rsqrt_fusion), kind=kOutput, calls=%fused_computation.20 | convolution fusion | flops 2419064832 | bytes 9445376 | tf_op jit(solution)/shard_map/dot_general | solution.py:112
  33.4 0.7 fusion.19
  34.1 4.2 %collective-permute-start.5 = (s32[2]{0:T(128)S(1)}, s32[2]{0:T(128)S(1)}, u32[]{:S(2)}, u32[]{:S(2)}) collective-permute-start(s32[2]{0:T(128)S(1)} %pad_add_fusion), channel_id=1, source_target_pairs={{0,6},{1,7},{2,8},{3,9},{4,10},{5,11},{6,12},{7,13},{8,14},{9,15},... | collective-permute-start | bytes 32 | tf_op jit(solution)/shard_map/ppermute | solution.py:22
  40.2 2.5 %collective-permute-start.6 = (s32[2]{0:T(128)S(1)}, s32[2]{0:T(128)S(1)}, u32[]{:S(2)}, u32[]{:S(2)}) collective-permute-start(s32[2]{0:T(128)S(1)} %pad_add_fusion), channel_id=1, source_target_pairs={{0,7},{1,8},{2,9},{3,10},{4,11},{5,12},{6,13},{7,14},{8,15},{9,16}... | collective-permute-start | bytes 32 | tf_op jit(solution)/shard_map/ppermute | solution.py:22
  43.9 3.7 %collective-permute-start.7 = (s32[2]{0:T(128)S(1)}, s32[2]{0:T(128)S(1)}, u32[]{:S(2)}, u32[]{:S(2)}) collective-permute-start(s32[2]{0:T(128)S(1)} %pad_add_fusion), channel_id=1, source_target_pairs={{0,8},{1,9},{2,10},{3,11},{4,12},{5,13},{6,14},{7,15},{8,16},{9,17... | collective-permute-start | bytes 32 | tf_op jit(solution)/shard_map/ppermute | solution.py:22
  50.1 0.6 fusion.27
  60.2 1.2 multiply_subtract_fusion.1
  61.6 2.4 %collective-permute-start.8 = (bf16[512,256]{1,0:T(8,128)(2,1)S(1)}, bf16[512,256]{1,0:T(8,128)(2,1)}, u32[]{:S(2)}, u32[]{:S(2)}) collective-permute-start(bf16[512,256]{1,0:T(8,128)(2,1)S(1)} %maximum_convert_fusion), channel_id=1, source_target_pairs={{0,1},{1,2},{2,3},{3,4},{4,5},{5,6},{6,7},{7,8},{8,9},{9,10},{10,1... | collective-permute-start | bytes 786440 | tf_op jit(solution)/shard_map/ppermute | solution.py:22
  64.1 1.0 multiply_cosine_fusion
  66.4 1.4 reduce.12
  67.8 1.6 %reshape.142 = bf16[128,2,2112]{2,1,0:T(2,128)(2,1)} reshape(bf16[128,4224]{1,0:T(8,128)(2,1)S(1)} %reduce.12) | data formatting | bytes 2162688
  69.4 10.1 %all-to-all-start = ((bf16[128,2,2112]{2,1,0:T(2,128)(2,1)}), bf16[128,2,2112]{2,1,0:T(2,128)(2,1)}, u32[]{:S(2)}, u32[]{:S(2)}) async-start(bf16[128,2,2112]{2,1,0:T(2,128)(2,1)} %reshape.142), calls=%async_computation | async-start | bytes 2228224 | tf_op jit(solution)/shard_map/all_to_all | solution.py:145
  79.5 2.2 %collective-permute-start.9 = (bf16[512,256]{1,0:T(8,128)(2,1)}, bf16[512,256]{1,0:T(8,128)(2,1)S(1)}, u32[]{:S(2)}, u32[]{:S(2)}) collective-permute-start(bf16[512,256]{1,0:T(8,128)(2,1)} %collective-permute-done.8), channel_id=1, source_target_pairs={{0,1},{1,2},{2,3},{3,4},{4,5},{5,6},{6,7},{7,8},{8,9},{9,10},{10,1... | collective-permute-start | bytes 786440 | tf_op jit(solution)/shard_map/ppermute | solution.py:22
  81.7 2.3 %multiply_subtract_fusion = (f32[512,12,64]{0,2,1:T(8,128)S(1)}, f32[512,12,64]{0,2,1:T(8,128)S(1)}) fusion(f32[512,12,128]{0,2,1:T(8,128)} %bitcast.41, f32[512,64]{0,1:T(8,128)S(1)} %copy.46, f32[512,64]{0,1:T(8,128)S(1)} %copy.45), kind=kLoop, calls=%fused_computation.12 | loop fusion | flops 2359296 | bytes 6553600 | tf_op jit(solution)/shard_map/sub | solution.py:39
  84.6 1.6 %copy.50.query_ref = bf16[512,1536]{1,0:T(8,128)(2,1)} copy(bf16[512,1536]{0,1:T(8,128)(2,1)S(1)} %bitcast.38) | data formatting | bytes 3145728 | tf_op jit(solution)/shard_map/convert_element_type | solution.py:115
  86.1 0.8 copy.51.first_ref
  87.0 11.9 %collective-permute-done.9 = bf16[512,256]{1,0:T(8,128)(2,1)S(1)} collective-permute-done((bf16[512,256]{1,0:T(8,128)(2,1)}, bf16[512,256]{1,0:T(8,128)(2,1)S(1)}, u32[]{:S(2)}, u32[]{:S(2)}) %collective-permute-start.9) | collective-permute-done | bytes 262176 | tf_op jit(solution)/shard_map/ppermute | solution.py:22
  98.9 1.9 %pad_maximum_fusion.keyval_ref = bf16[1536,256]{1,0:T(8,128)(2,1)} fusion(bf16[512,256]{1,0:T(8,128)(2,1)S(1)} %maximum_convert_fusion, bf16[512,256]{1,0:T(8,128)(2,1)} %collective-permute-done.8, bf16[512,256]{1,0:T(8,128)(2,1)S(1)} %collective-permute-done.9), kind=kLoop, calls=%fused_computation.15 | loop fusion | flops 2359296 | bytes 1572864 | tf_op jit(solution)/shard_map/concatenate | solution.py:130
  100.8 27.0 %shard_map.95 = bf16[512,1536]{1,0:T(8,128)(2,1)} custom-call(bf16[512,1536]{1,0:T(8,128)(2,1)} %copy.50.query_ref, bf16[1536,256]{1,0:T(8,128)(2,1)} %pad_maximum_fusion.keyval_ref, s32[512,1]{1,0:T(8,128)} %copy.51.first_ref), custom_call_target="tpu_custom_call" | custom-call | tf_op jit(solution)/shard_map/pallas_call | solution.py:75
  127.9 6.6 %convolution_convert_fusion.2 = bf16[512,1536]{1,0:T(8,128)(2,1)} fusion(bf16[512,1536]{1,0:T(8,128)(2,1)} %shard_map.95, bf16[1536,1536]{1,0:T(8,128)(2,1)} %param.14), kind=kOutput, calls=%fused_computation.10 | convolution fusion | flops 2416705536 | bytes 7864320 | tf_op jit(solution)/shard_map/dot_general | solution.py:134
  134.4 6.9 %reshape.143 = bf16[128,1,4224]{2,1,0:T(2,128)(2,1)S(1)} reshape(bf16[128,2,2112]{2,1,0:T(2,128)(2,1)} %all-to-all-done) | data formatting | bytes 2162688
  142.0 1.3 reshape.139
  (52 shorter events, 9.0 us)
Async XLA Ops:
  0.6 32.0 %copy-start = (bf16[1536,256]{1,0:T(8,128)(2,1)S(1)}, bf16[1536,256]{1,0:T(8,128)(2,1)}, u32[]{:S(2)}) copy-start(bf16[1536,256]{1,0:T(8,128)(2,1)} %param.13) | copy-start | bytes 2359300
  0.6 25.3 %copy-start.1 = (bf16[512,1536]{1,0:T(8,128)(2,1)S(1)}, bf16[512,1536]{1,0:T(8,128)(2,1)}, u32[]{:S(2)}) copy-start(bf16[512,1536]{1,0:T(8,128)(2,1)} %param.10) | copy-start | bytes 4718596
  0.7 25.3 %copy-start.4 = (f32[1536]{0:T(1024)S(1)}, f32[1536]{0:T(1024)}, u32[]{:S(2)}) copy-start(f32[1536]{0:T(1024)} %param.11) | copy-start | bytes 18436
  5.5 28.6 %collective-permute-start = (s32[2]{0:T(128)S(1)}, s32[2]{0:T(128)S(1)}, u32[]{:S(2)}, u32[]{:S(2)}) collective-permute-start(s32[2]{0:T(128)S(1)} %pad_add_fusion), channel_id=1, source_target_pairs={{0,1},{1,2},{2,3},{3,4},{4,5},{5,6},{6,7},{7,8},{8,9},{9,10},{10,1... | collective-permute-start | bytes 32 | tf_op jit(solution)/shard_map/ppermute | solution.py:22
  7.4 32.8 %collective-permute-start.1 = (s32[2]{0:T(128)S(1)}, s32[2]{0:T(128)S(1)}, u32[]{:S(2)}, u32[]{:S(2)}) collective-permute-start(s32[2]{0:T(128)S(1)} %pad_add_fusion), channel_id=1, source_target_pairs={{0,2},{1,3},{2,4},{3,5},{4,6},{5,7},{6,8},{7,9},{8,10},{9,11},{10,... | collective-permute-start | bytes 32 | tf_op jit(solution)/shard_map/ppermute | solution.py:22
  10.9 33.0 %collective-permute-start.2 = (s32[2]{0:T(128)S(1)}, s32[2]{0:T(128)S(1)}, u32[]{:S(2)}, u32[]{:S(2)}) collective-permute-start(s32[2]{0:T(128)S(1)} %pad_add_fusion), channel_id=1, source_target_pairs={{0,3},{1,4},{2,5},{3,6},{4,7},{5,8},{6,9},{7,10},{8,11},{9,12},{10... | collective-permute-start | bytes 32 | tf_op jit(solution)/shard_map/ppermute | solution.py:22
  15.1 33.8 %collective-permute-start.3 = (s32[2]{0:T(128)S(1)}, s32[2]{0:T(128)S(1)}, u32[]{:S(2)}, u32[]{:S(2)}) collective-permute-start(s32[2]{0:T(128)S(1)} %pad_add_fusion), channel_id=1, source_target_pairs={{0,4},{1,5},{2,6},{3,7},{4,8},{5,9},{6,10},{7,11},{8,12},{9,13},{1... | collective-permute-start | bytes 32 | tf_op jit(solution)/shard_map/ppermute | solution.py:22
  19.8 30.3 %collective-permute-start.4 = (s32[2]{0:T(128)S(1)}, s32[2]{0:T(128)S(1)}, u32[]{:S(2)}, u32[]{:S(2)}) collective-permute-start(s32[2]{0:T(128)S(1)} %pad_add_fusion), channel_id=1, source_target_pairs={{0,5},{1,6},{2,7},{3,8},{4,9},{5,10},{6,11},{7,12},{8,13},{9,14},{... | collective-permute-start | bytes 32 | tf_op jit(solution)/shard_map/ppermute | solution.py:22
  32.7 0.7 copy-start.5
  32.7 27.5 %copy-start.2 = (s32[512]{0:T(512)S(1)}, s32[512]{0:T(512)}, u32[]{:S(2)}) copy-start(s32[512]{0:T(512)} %param.15) | copy-start | bytes 6148
  34.1 17.3 %collective-permute-start.5 = (s32[2]{0:T(128)S(1)}, s32[2]{0:T(128)S(1)}, u32[]{:S(2)}, u32[]{:S(2)}) collective-permute-start(s32[2]{0:T(128)S(1)} %pad_add_fusion), channel_id=1, source_target_pairs={{0,6},{1,7},{2,8},{3,9},{4,10},{5,11},{6,12},{7,13},{8,14},{9,15},... | collective-permute-start | bytes 32 | tf_op jit(solution)/shard_map/ppermute | solution.py:22
  40.2 12.5 %collective-permute-start.6 = (s32[2]{0:T(128)S(1)}, s32[2]{0:T(128)S(1)}, u32[]{:S(2)}, u32[]{:S(2)}) collective-permute-start(s32[2]{0:T(128)S(1)} %pad_add_fusion), channel_id=1, source_target_pairs={{0,7},{1,8},{2,9},{3,10},{4,11},{5,12},{6,13},{7,14},{8,15},{9,16}... | collective-permute-start | bytes 32 | tf_op jit(solution)/shard_map/ppermute | solution.py:22
  43.9 10.0 %collective-permute-start.7 = (s32[2]{0:T(128)S(1)}, s32[2]{0:T(128)S(1)}, u32[]{:S(2)}, u32[]{:S(2)}) collective-permute-start(s32[2]{0:T(128)S(1)} %pad_add_fusion), channel_id=1, source_target_pairs={{0,8},{1,9},{2,10},{3,11},{4,12},{5,13},{6,14},{7,15},{8,16},{9,17... | collective-permute-start | bytes 32 | tf_op jit(solution)/shard_map/ppermute | solution.py:22
  60.2 5.1 %copy-start.3 = (s32[32]{0:T(128)S(1)}, s32[32]{0:T(128)}, u32[]{:S(2)}) copy-start(s32[32]{0:T(128)} %param.16) | copy-start | bytes 388
  61.6 18.0 %collective-permute-start.8 = (bf16[512,256]{1,0:T(8,128)(2,1)S(1)}, bf16[512,256]{1,0:T(8,128)(2,1)}, u32[]{:S(2)}, u32[]{:S(2)}) collective-permute-start(bf16[512,256]{1,0:T(8,128)(2,1)S(1)} %maximum_convert_fusion), channel_id=1, source_target_pairs={{0,1},{1,2},{2,3},{3,4},{4,5},{5,6},{6,7},{7,8},{8,9},{9,10},{10,1... | collective-permute-start | bytes 786440 | tf_op jit(solution)/shard_map/ppermute | solution.py:22
  69.4 65.0 %all-to-all-start = ((bf16[128,2,2112]{2,1,0:T(2,128)(2,1)}), bf16[128,2,2112]{2,1,0:T(2,128)(2,1)}, u32[]{:S(2)}, u32[]{:S(2)}) async-start(bf16[128,2,2112]{2,1,0:T(2,128)(2,1)} %reshape.142), calls=%async_computation | async-start | bytes 2228224 | tf_op jit(solution)/shard_map/all_to_all | solution.py:145
  79.5 19.4 %collective-permute-start.9 = (bf16[512,256]{1,0:T(8,128)(2,1)}, bf16[512,256]{1,0:T(8,128)(2,1)S(1)}, u32[]{:S(2)}, u32[]{:S(2)}) collective-permute-start(bf16[512,256]{1,0:T(8,128)(2,1)} %collective-permute-done.8), channel_id=1, source_target_pairs={{0,1},{1,2},{2,3},{3,4},{4,5},{5,6},{6,7},{7,8},{8,9},{9,10},{10,1... | collective-permute-start | bytes 786440 | tf_op jit(solution)/shard_map/ppermute | solution.py:22

commit v3 on v2

--- a/solution.py
+++ b/solution.py
@@ -9,7 +9,6 @@
 
 WINDOW = 1024
 PAGE = 16
-MAXLEN = 4096
 
 
 EPS = 1e-06
@@ -96,14 +95,15 @@
     change = jnp.concatenate([jnp.ones((1,), dtype=jnp.bool_), segment_ids[1:] != segment_ids[:-1]])
     local_start = lax.cummax(jnp.where(change, local_index, 0))
     place = lax.axis_index("seq")
-    run_info = jnp.stack([segment_ids[-1], offset + local_start[-1]])
-    hops = min(devices - 1, -(-MAXLEN // row_count))
-    heard = [passed_along(run_info, "seq", hop) for hop in range(1, hops + 1)]
-    prior_id = jnp.where(place >= 1, heard[0][0], -1)
-    prior_first = offset
-    for hop in range(hops, 0, -1):
-        same = (place >= hop) & (heard[hop - 1][0] == prior_id)
-        prior_first = jnp.where(same, jnp.minimum(prior_first, heard[hop - 1][1]), prior_first)
+    owner_hits = page_owner[:, None] == jnp.arange(devices, dtype=jnp.int32)[None, :]
+    slot_to = jnp.sum(jnp.where(owner_hits, page_slot[:, None] + 1, 0), 0)
+    notes = jnp.zeros((devices, 128), jnp.int32)
+    notes = notes.at[:, 0].set(segment_ids[-1]).at[:, 1].set(offset + local_start[-1]).at[:, 2].set(slot_to)
+    heard = lax.all_to_all(notes, "seq", split_axis=0, concat_axis=0, tiled=True)
+    source = jnp.arange(devices, dtype=jnp.int32)
+    prior_id = jnp.where(place >= 1, heard[jnp.maximum(place - 1, 0), 0], -1)
+    earlier_same = (source < place) & (heard[:, 0] == prior_id)
+    prior_first = jnp.min(jnp.where(earlier_same, heard[:, 1], offset))
     starts = jnp.where(segment_ids == prior_id, prior_first, offset + local_start)
     positions = global_index - starts
     wide = tokens.astype(jnp.float32)
@@ -118,11 +118,7 @@
         [rotate(projected[:, :head_dim], positions), projected[:, head_dim:]], 1
     ).astype(jnp.bfloat16)
     reach = WINDOW // row_count
-    blocks = [keyval]
-    moving = keyval
-    for hop_step in range(reach):
-        moving = passed_along(moving, "seq", 1)
-        blocks.append(moving)
+    blocks = [keyval] + [passed_along(keyval, "seq", hop) for hop in range(1, reach + 1)]
     ordered = blocks[::-1]
     back = reach * row_count
     context = attend(
@@ -132,22 +128,18 @@
         back,
     )
     attn_out = jnp.dot(context, w_out, preferred_element_type=jnp.float32).astype(jnp.bfloat16)
-    page_rows = keyval.reshape(row_count // PAGE, PAGE * 2 * head_dim)
-    width = page_rows.shape[1]
-    slot_tag = jnp.zeros((page_rows.shape[0], 128), jnp.bfloat16).at[:, 0].set(
-        (page_slot + 1).astype(jnp.bfloat16)
-    )
-    payload = jnp.concatenate([page_rows, slot_tag], 1)
-    owner_hits = page_owner[:, None] == jnp.arange(devices, dtype=jnp.int32)[None, :]
-    send_rows = jnp.einsum(
-        "po,pc->oc", owner_hits.astype(jnp.bfloat16), payload, preferred_element_type=jnp.float32
-    ).astype(jnp.bfloat16)
-    got = lax.all_to_all(send_rows, "seq", split_axis=0, concat_axis=0, tiled=True)
-    got_slots = got[:, width].astype(jnp.float32).astype(jnp.int32) - 1
-    placed = got_slots[None, :] == jnp.arange(devices, dtype=jnp.int32)[:, None]
-    cache = jnp.dot(
-        placed.astype(jnp.bfloat16), got[:, :width], preferred_element_type=jnp.float32
-    ).astype(jnp.bfloat16)
+    page_count = row_count // PAGE
+    pages = keyval.reshape(page_count, PAGE, 2 * head_dim)
+    pages = jnp.concatenate([pages, jnp.zeros((1, PAGE, 2 * head_dim), pages.dtype)], 0)
+    page_index = jnp.arange(page_count, dtype=jnp.int32)[:, None]
+    pick = jnp.sum(jnp.where(owner_hits, page_index, 0), 0)
+    pick = jnp.where(jnp.any(owner_hits, 0), pick, page_count)
+    got = lax.all_to_all(pages[pick], "seq", split_axis=0, concat_axis=0, tiled=True)
+    got = jnp.concatenate([got, jnp.zeros((1, PAGE, 2 * head_dim), got.dtype)], 0)
+    landed = heard[:, 2][None, :] == source[:, None] + 1
+    from_source = jnp.sum(jnp.where(landed, source[None, :], 0), 1)
+    from_source = jnp.where(jnp.any(landed, 1), from_source, devices)
+    cache = got[from_source]
     return (attn_out, cache.reshape(devices * PAGE, 2 * head_dim))
 
 

time: 144 us -> 97.1 us (0.67)
  starting transfers between devices: 43 us -> 25.5 us
  waiting for transfers between devices: 12 us -> 0.01 us
  local copies, waits for them, and re-layouts: 20.3 us -> 9.62 us
  between operations: 12.3 us -> 4.21 us
    ppermute x10 -> x2, starting transfers between devices: 32.9 us -> 5.47 us  [passed_along(): return lax.ppermute(value, axis, pairs)]
    ppermute x10 -> x2, waiting for transfers between devices: 12 us -> 0.01 us  [passed_along(): return lax.ppermute(value, axis, pairs)]
    all_to_all x1 -> x2, starting transfers between devices: 10.1 us -> 20.1 us  [the longest x1 10.2 us: body(): lax.all_to_all(notes, 'seq', split_axis=0, concat_axis=0, tiled=True)]
    unnamed x16 -> x8, local copies, waits for them, and re-layouts: 8.74 us -> 0.02 us
    slice x10 -> x3, local copies, waits for them, and re-layouts: 6.72 us -> 2.02 us  [the longest x1 1.26 us: body(): segment_ids[-1]]
    gather x0 -> x2, local copies, waits for them, and re-layouts: none -> 3.23 us  [the longest x1 1.61 us: body(): cache = got[from_source]]
    sub x2 -> x1, other arithmetic: 3.57 us -> 2.35 us  [rotate(): first_half * cosine - second_half * sine_part]
    another operation x5 -> x6, other arithmetic: 2.36 us -> 3.56 us
  transfers between devices with their start and end apart: 11 -> 4, of which waited for: 1 -> 0; matrix products, arithmetic and copies ran while one was open for 24% -> 26% of each run, Pallas kernels for 19% -> 28%
where the time goes in v3:
time: 97.1 us; the launch traced here: 95.3 us
  Pallas kernels  27 us (28%)
  starting transfers between devices  25.5 us (26%)
  other arithmetic  15 us (15%)
  matrix products  13.9 us (14%)
  local copies, waits for them, and re-layouts  9.62 us (10%)
  between operations  4.21 us (4%)
    pallas_call x1, Pallas kernels, attend(): pl.pallas_call(kernel, grid=(row_count // tile,), in_specs=[pl.BlockSpec(...  27 us
    all_to_all x1, starting transfers between devices, body(): lax.all_to_all(notes, 'seq', split_axis=0, concat_axis=0, tiled=True)  10.2 us
    all_to_all x1, starting transfers between devices, body(): lax.all_to_all(pages[pick], 'seq', split_axis=0, concat_axis=0, tiled=True)  9.84 us
    dot_general x1, matrix products, body(): jnp.dot(normed, w_query, preferred_element_type=jnp.float32)  6.75 us
    dot_general x1, matrix products, body(): jnp.dot(context, w_out, preferred_element_type=jnp.float32)  6.56 us
    ppermute x2, starting transfers between devices, passed_along(): return lax.ppermute(value, axis, pairs)  5.47 us
    another operation x6, other arithmetic  3.56 us
    sub x1, other arithmetic, rotate(): first_half * cosine - second_half * sine_part  2.35 us
  transfers between devices with their start and end apart: 4, of which 0 were waited for; matrix products, arithmetic and copies ran while one was open for 26% of the time, Pallas kernels for 28%

profile of v3, /device:TPU:32, one launch (start us, length us, event | category | flops | bytes accessed | tf_op | source)
XLA Modules:
  0.0 95.3 jit_solution(9942240081840668829)
XLA Ops:
  0.7 0.6 compare_reduce_fusion.3
  1.3 0.8 slice_compare_fusion.1
  2.1 1.3 %slice.93 = s32[1]{0:T(128)} slice(s32[512]{0:T(512)} %param.19), slice={[511:512]} | slice | bytes 8 | tf_op jit(solution)/shard_map/slice | solution.py:101
  3.4 0.7 compare_reduce_fusion.2
  4.1 0.6 compare_reduce_fusion.1
  4.8 0.3 reduce-window.9
  6.8 0.6 slice.98
  7.3 0.7 broadcast_add_fusion
  9.3 0.7 select_reduce_fusion
  10.2 0.6 fusion.16
  10.8 0.7 copy.40
  11.5 10.2 %all-to-all-start = ((s32[128,1,128]{2,1,0:T(1,128)}), s32[128,1,128]{2,1,0:T(1,128)S(1)}, u32[]{:S(2)}, u32[]{:S(2)}) async-start(s32[128,1,128]{2,1,0:T(1,128)} %copy.40), calls=%async_computation | async-start | bytes 131072 | tf_op jit(solution)/shard_map/all_to_all | solution.py:102
  21.8 0.7 fusion.15
  22.5 1.8 %fusion = f32[512]{0:T(512)S(1)} fusion(bf16[512,1536]{1,0:T(8,128)(2,1)} %param.14), kind=kLoop, calls=%fused_computation.4 | loop fusion | flops 2358784 | bytes 1574912 | tf_op jit(solution)/shard_map/reduce_sum | solution.py:110
  24.4 6.8 %fusion.9 = f32[512,1536]{0,1:T(8,128)} fusion(bf16[1536,1536]{1,0:T(8,128)(2,1)} %param.16, bf16[512,1536]{1,0:T(8,128)(2,1)S(1)} %copy-done.1, f32[1536]{0:T(1024)S(1)} %copy-done.3, f32[512]{0:T(512)S(1)} %add_rsqrt_fusion), kind=kOutput, calls=%fused_computation.18 | convolution fusion | flops 2419064832 | bytes 9445376 | tf_op jit(solution)/shard_map/dot_general | solution.py:112
  31.1 0.6 fusion.7
  32.0 0.5 constant_dynamic-slice_fusion
  33.3 0.6 fusion.19
  33.9 0.7 broadcast_subtract_fusion
  34.6 1.2 %subtract_convert_fusion = (bf16[512,64]{1,0:T(8,128)(2,1)S(1)}, bf16[512,64]{1,0:T(8,128)(2,1)S(1)}, f32[512,64]{1,0:T(8,128)S(1)}, f32[512,64]{1,0:T(8,128)S(1)}) fusion(f32[512,256]{1,0:T(8,128)S(1)} %fusion.7, f32[64]{0:T(128)S(1)} %multiply_power_fusion, f32[512]{0:T(512)S(1)} %get-tuple-element.47), kind=kLoop, calls=%fused_computation.26 | loop fusion | flops 294912 | bytes 657664 | tf_op jit(solution)/shard_map/convert.6
  36.0 2.0 %collective-permute-start.1 = (bf16[512,256]{1,0:T(8,128)(2,1)S(1)}, bf16[512,256]{1,0:T(8,128)(2,1)S(1)}, u32[]{:S(2)}, u32[]{:S(2)}) collective-permute-start(bf16[512,256]{1,0:T(8,128)(2,1)S(1)} %pad_maximum_fusion), channel_id=1, source_target_pairs={{0,1},{1,2},{2,3},{3,4},{4,5},{5,6},{6,7},{7,8},{8,9},{9,10},{10,1... | collective-permute-start | bytes 786440 | tf_op jit(solution)/shard_map/ppermute | solution.py:21
  38.0 3.4 %collective-permute-start = (bf16[512,256]{1,0:T(8,128)(2,1)S(1)}, bf16[512,256]{1,0:T(8,128)(2,1)S(1)}, u32[]{:S(2)}, u32[]{:S(2)}) collective-permute-start(bf16[512,256]{1,0:T(8,128)(2,1)S(1)} %pad_maximum_fusion), channel_id=1, source_target_pairs={{0,2},{1,3},{2,4},{3,5},{4,6},{5,7},{6,8},{7,9},{8,10},{9,11},{10,... | collective-permute-start | bytes 786440 | tf_op jit(solution)/shard_map/ppermute | solution.py:21
  42.1 2.3 %multiply_subtract_fusion = (f32[512,12,64]{0,2,1:T(8,128)S(1)}, f32[512,12,64]{0,2,1:T(8,128)S(1)}) fusion(f32[512,12,128]{0,2,1:T(8,128)} %bitcast.36, f32[512,64]{0,1:T(8,128)S(1)} %copy.42, f32[512,64]{0,1:T(8,128)S(1)} %copy.41), kind=kLoop, calls=%fused_computation.11 | loop fusion | flops 2359296 | bytes 6553600 | tf_op jit(solution)/shard_map/sub | solution.py:38
  44.4 0.5 fusion.3
  44.9 1.6 %copy.46.query_ref = bf16[512,1536]{1,0:T(8,128)(2,1)} copy(bf16[512,1536]{0,1:T(8,128)(2,1)S(1)} %bitcast.35) | data formatting | bytes 3145728 | tf_op jit(solution)/shard_map/convert_element_type | solution.py:115
  46.5 0.9 copy.47.first_ref
  47.5 1.6 %gather_fusion = bf16[128,16,256]{2,1,0:T(8,128)(2,1)} fusion(bf16[33,16,256]{2,1,0:T(8,128)(2,1)S(1)} %fusion.12, s32[1024]{0:T(1024)S(1)} %pad_clamp_fusion.1), kind=kCustom, calls=%fused_computation | custom fusion | bytes 2097664 | tf_op jit(solution)/shard_map/gather | solution.py:137
  49.1 9.8 %all-to-all-start.1 = ((bf16[128,16,256]{2,1,0:T(8,128)(2,1)}), bf16[128,16,256]{2,1,0:T(8,128)(2,1)S(1)}, u32[]{:S(2)}, u32[]{:S(2)}) async-start(bf16[128,16,256]{2,1,0:T(8,128)(2,1)} %gather_fusion), calls=%async_computation.1 | async-start | bytes 2097152 | tf_op jit(solution)/shard_map/all_to_all | solution.py:137
  59.0 1.0 %maximum_maximum_fusion.keyval_ref = bf16[1536,256]{1,0:T(8,128)(2,1)} fusion(bf16[512,128]{1,0:T(8,128)(2,1)S(1)} %slice.138, bf16[512,64]{1,0:T(8,128)(2,1)S(1)} %get-tuple-element.45, bf16[512,64]{1,0:T(8,128)(2,1)S(1)} %get-tuple-element.44, bf16[512,256]{1,0:T(8,128)(2,1)S(1)} %collective-permute-done.1, bf16[512,256]{1,0:T(8,128)(2,1)S(1)} %collective-permute-done), kind=kLoop, calls=%fused_computation.12 | loop fusion | flops 3932160 | bytes 1572864 | tf_op jit(solution)/shard_map/concatenate | solution.py:126
  60.0 27.0 %shard_map.95 = bf16[512,1536]{1,0:T(8,128)(2,1)} custom-call(bf16[512,1536]{1,0:T(8,128)(2,1)} %copy.46.query_ref, bf16[1536,256]{1,0:T(8,128)(2,1)} %maximum_maximum_fusion.keyval_ref, s32[512,1]{1,0:T(8,128)} %copy.47.first_ref), custom_call_target="tpu_custom_call" | custom-call | tf_op jit(solution)/shard_map/pallas_call | solution.py:74
  87.1 6.6 %convolution_convert_fusion = bf16[512,1536]{1,0:T(8,128)(2,1)} fusion(bf16[512,1536]{1,0:T(8,128)(2,1)} %shard_map.95, bf16[1536,1536]{1,0:T(8,128)(2,1)} %param.18), kind=kOutput, calls=%fused_computation.9 | convolution fusion | flops 2416705536 | bytes 7864320 | tf_op jit(solution)/shard_map/dot_general | solution.py:130
  93.7 1.6 %gather_fusion.1 = bf16[128,16,256]{2,1,0:T(8,128)(2,1)} fusion(bf16[129,16,256]{2,1,0:T(8,128)(2,1)S(1)} %concatenate.47, s32[1024]{0:T(1024)S(1)} %pad_clamp_fusion), kind=kCustom, calls=%fused_computation.1 | custom fusion | bytes 2097664 | tf_op jit(solution)/shard_map/gather | solution.py:142
  (39 shorter events, 1.8 us)
Async XLA Ops:
  0.6 30.5 %copy-start = (bf16[1536,256]{1,0:T(8,128)(2,1)S(1)}, bf16[1536,256]{1,0:T(8,128)(2,1)}, u32[]{:S(2)}) copy-start(bf16[1536,256]{1,0:T(8,128)(2,1)} %param.17) | copy-start | bytes 2359300
  0.6 23.7 %copy-start.1 = (bf16[512,1536]{1,0:T(8,128)(2,1)S(1)}, bf16[512,1536]{1,0:T(8,128)(2,1)}, u32[]{:S(2)}) copy-start(bf16[512,1536]{1,0:T(8,128)(2,1)} %param.14) | copy-start | bytes 4718596
  0.7 23.7 %copy-start.3 = (f32[1536]{0:T(1024)S(1)}, f32[1536]{0:T(1024)}, u32[]{:S(2)}) copy-start(f32[1536]{0:T(1024)} %param.15) | copy-start | bytes 18436
  11.5 20.3 %all-to-all-start = ((s32[128,1,128]{2,1,0:T(1,128)}), s32[128,1,128]{2,1,0:T(1,128)S(1)}, u32[]{:S(2)}, u32[]{:S(2)}) async-start(s32[128,1,128]{2,1,0:T(1,128)} %copy.40), calls=%async_computation | async-start | bytes 131072 | tf_op jit(solution)/shard_map/all_to_all | solution.py:102
  31.1 2.8 %copy-start.2 = (s32[512]{0:T(512)S(1)}, s32[512]{0:T(512)}, u32[]{:S(2)}) copy-start(s32[512]{0:T(512)} %param.19) | copy-start | bytes 6148
  36.0 23.0 %collective-permute-start.1 = (bf16[512,256]{1,0:T(8,128)(2,1)S(1)}, bf16[512,256]{1,0:T(8,128)(2,1)S(1)}, u32[]{:S(2)}, u32[]{:S(2)}) collective-permute-start(bf16[512,256]{1,0:T(8,128)(2,1)S(1)} %pad_maximum_fusion), channel_id=1, source_target_pairs={{0,1},{1,2},{2,3},{3,4},{4,5},{5,6},{6,7},{7,8},{8,9},{9,10},{10,1... | collective-permute-start | bytes 786440 | tf_op jit(solution)/shard_map/ppermute | solution.py:21
  38.0 21.0 %collective-permute-start = (bf16[512,256]{1,0:T(8,128)(2,1)S(1)}, bf16[512,256]{1,0:T(8,128)(2,1)S(1)}, u32[]{:S(2)}, u32[]{:S(2)}) collective-permute-start(bf16[512,256]{1,0:T(8,128)(2,1)S(1)} %pad_maximum_fusion), channel_id=1, source_target_pairs={{0,2},{1,3},{2,4},{3,5},{4,6},{5,7},{6,8},{7,9},{8,10},{9,11},{10,... | collective-permute-start | bytes 786440 | tf_op jit(solution)/shard_map/ppermute | solution.py:21
  49.1 44.5 %all-to-all-start.1 = ((bf16[128,16,256]{2,1,0:T(8,128)(2,1)}), bf16[128,16,256]{2,1,0:T(8,128)(2,1)S(1)}, u32[]{:S(2)}, u32[]{:S(2)}) async-start(bf16[128,16,256]{2,1,0:T(8,128)(2,1)} %gather_fusion), calls=%async_computation.1 | async-start | bytes 2097152 | tf_op jit(solution)/shard_map/all_to_all | solution.py:137

commit v4 on v3

--- a/solution.py
+++ b/solution.py
@@ -42,25 +42,22 @@
     )
 
 
-def attend_kernel(query_ref, keyval_ref, first_ref, out_ref, *, tile, back, head_count, head_dim):
+def attend_kernel(query_ref, keys_ref, values_ref, first_ref, out_ref, *, tile, back, head_count, head_dim):
     step = pl.program_id(0)
     span = tile + WINDOW
     key_first = pl.multiple_of(step * tile + back - WINDOW, tile)
-    rows = keyval_ref[pl.ds(key_first, span), :]
-    keys = rows[:, :head_dim]
-    values = rows[:, head_dim:]
+    keys = keys_ref[:, pl.ds(key_first, span)]
+    values = values_ref[pl.ds(key_first, span), :]
     query_at = step * tile + lax.broadcasted_iota(jnp.int32, (tile, span), 0)
     key_at = key_first - back + lax.broadcasted_iota(jnp.int32, (tile, span), 1)
     valid = (key_at >= first_ref[...]) & (key_at <= query_at) & (query_at - key_at < WINDOW)
     for head in range(head_count):
         lanes = slice(head * head_dim, (head + 1) * head_dim)
-        scores = lax.dot_general(
-            query_ref[:, lanes], keys, (((1,), (1,)), ((), ())), preferred_element_type=jnp.float32
-        )
+        scores = jnp.dot(query_ref[:, lanes], keys, preferred_element_type=jnp.float32)
         scores = jnp.where(valid, scores, -1e30)
         peak = jnp.max(scores, 1, keepdims=True)
         exponent = jnp.exp(scores - peak)
-        probs = (exponent / jnp.sum(exponent, 1, keepdims=True)).astype(jnp.bfloat16)
+        probs = (exponent * (1.0 / jnp.sum(exponent, 1, keepdims=True))).astype(jnp.bfloat16)
         context = jnp.dot(probs, values, preferred_element_type=jnp.float32)
         out_ref[:, lanes] = context.astype(out_ref.dtype)
 
@@ -76,12 +73,13 @@
         grid=(row_count // tile,),
         in_specs=[
             pl.BlockSpec((tile, width), lambda i: (i, 0)),
-            pl.BlockSpec(keyval_rows.shape, lambda i: (0, 0)),
+            pl.BlockSpec((head_dim, keyval_rows.shape[0]), lambda i: (0, 0)),
+            pl.BlockSpec((keyval_rows.shape[0], head_dim), lambda i: (0, 0)),
             pl.BlockSpec((tile, 1), lambda i: (i, 0)),
         ],
         out_specs=pl.BlockSpec((tile, width), lambda i: (i, 0)),
         out_shape=jax.ShapeDtypeStruct((row_count, width), jnp.bfloat16),
-    )(queries, keyval_rows, first_rel)
+    )(queries, keyval_rows[:, :head_dim].T, keyval_rows[:, head_dim:], first_rel)
 
 
 def body(tokens, norm_gain, w_query, w_key_value, w_out, segment_ids, page_owner, page_slot):

time: 97.1 us -> 98.4 us (1.013)
  local copies, waits for them, and re-layouts: 9.62 us -> 11.4 us
  transfers between devices with their start and end apart: 4 -> 4, of which waited for: 0 -> 0; matrix products, arithmetic and copies ran while one was open for 26% -> 27% of each run, Pallas kernels for 28% -> 28%
where the time goes in v4:
time: 98.4 us; the launch traced here: 96.7 us
  Pallas kernels  27.5 us (28%)
  starting transfers between devices  25.5 us (26%)
  other arithmetic  14.1 us (14%)
  matrix products  13.9 us (14%)
  local copies, waits for them, and re-layouts  11.4 us (12%)
  between operations  4.22 us (4%)
    pallas_call x1, Pallas kernels, attend(): pl.pallas_call(kernel, grid=(row_count // tile,), in_specs=[pl.BlockSpec(...  27.5 us
    all_to_all x1, starting transfers between devices, body(): lax.all_to_all(notes, 'seq', split_axis=0, concat_axis=0, tiled=True)  10.2 us
    all_to_all x1, starting transfers between devices, body(): lax.all_to_all(pages[pick], 'seq', split_axis=0, concat_axis=0, tiled=True)  9.84 us
    dot_general x1, matrix products, body(): jnp.dot(normed, w_query, preferred_element_type=jnp.float32)  6.75 us
    dot_general x1, matrix products, body(): jnp.dot(context, w_out, preferred_element_type=jnp.float32)  6.56 us
    ppermute x2, starting transfers between devices, passed_along(): return lax.ppermute(value, axis, pairs)  5.47 us
    another operation x6, other arithmetic  3.56 us
    sub x1, other arithmetic, rotate(): first_half * cosine - second_half * sine_part  2.35 us
  transfers between devices with their start and end apart: 4, of which 0 were waited for; matrix products, arithmetic and copies ran while one was open for 27% of the time, Pallas kernels for 28%

profile of v4, /device:TPU:32, one launch (start us, length us, event | category | flops | bytes accessed | tf_op | source)
XLA Modules:
  0.0 96.7 jit_solution(5746047465960397230)
XLA Ops:
  0.7 0.6 compare_reduce_fusion.3
  1.3 0.8 slice_compare_fusion.1
  2.1 1.3 %slice.99 = s32[1]{0:T(128)} slice(s32[512]{0:T(512)} %param.19), slice={[511:512]} | slice | bytes 8 | tf_op jit(solution)/shard_map/slice | solution.py:99
  3.4 0.7 compare_reduce_fusion.2
  4.1 0.6 compare_reduce_fusion.1
  6.8 0.6 slice.104
  7.3 0.7 broadcast_add_fusion
  9.3 0.7 select_reduce_fusion
  10.2 0.6 fusion.16
  10.8 0.7 copy.44
  11.5 10.2 %all-to-all-start = ((s32[128,1,128]{2,1,0:T(1,128)}), s32[128,1,128]{2,1,0:T(1,128)S(1)}, u32[]{:S(2)}, u32[]{:S(2)}) async-start(s32[128,1,128]{2,1,0:T(1,128)} %copy.44), calls=%async_computation | async-start | bytes 131072 | tf_op jit(solution)/shard_map/all_to_all | solution.py:100
  21.8 0.7 fusion.15
  22.5 1.8 %fusion = f32[512]{0:T(512)S(1)} fusion(bf16[512,1536]{1,0:T(8,128)(2,1)} %param.14), kind=kLoop, calls=%fused_computation.4 | loop fusion | flops 2358784 | bytes 1574912 | tf_op jit(solution)/shard_map/reduce_sum | solution.py:108
  24.4 6.8 %fusion.9 = f32[512,1536]{0,1:T(8,128)} fusion(bf16[1536,1536]{1,0:T(8,128)(2,1)} %param.16, bf16[512,1536]{1,0:T(8,128)(2,1)S(1)} %copy-done.1, f32[1536]{0:T(1024)S(1)} %copy-done.3, f32[512]{0:T(512)S(1)} %add_rsqrt_fusion), kind=kOutput, calls=%fused_computation.18 | convolution fusion | flops 2419064832 | bytes 9445376 | tf_op jit(solution)/shard_map/dot_general | solution.py:110
  31.1 0.6 fusion.7
  32.0 0.5 constant_dynamic-slice_fusion
  33.3 0.6 fusion.19
  33.9 0.7 broadcast_subtract_fusion
  34.6 1.2 %subtract_convert_fusion = (bf16[512,64]{1,0:T(8,128)(2,1)S(1)}, bf16[512,64]{1,0:T(8,128)(2,1)S(1)}, f32[512,64]{1,0:T(8,128)S(1)}, f32[512,64]{1,0:T(8,128)S(1)}) fusion(f32[512,256]{1,0:T(8,128)S(1)} %fusion.7, f32[64]{0:T(128)S(1)} %multiply_power_fusion, f32[512]{0:T(512)S(1)} %get-tuple-element.49), kind=kLoop, calls=%fused_computation.27 | loop fusion | flops 294912 | bytes 657664 | tf_op jit(solution)/shard_map/convert.6
  36.0 2.0 %collective-permute-start.1 = (bf16[512,256]{1,0:T(8,128)(2,1)S(1)}, bf16[512,256]{1,0:T(8,128)(2,1)S(1)}, u32[]{:S(2)}, u32[]{:S(2)}) collective-permute-start(bf16[512,256]{1,0:T(8,128)(2,1)S(1)} %pad_maximum_fusion), channel_id=1, source_target_pairs={{0,1},{1,2},{2,3},{3,4},{4,5},{5,6},{6,7},{7,8},{8,9},{9,10},{10,1... | collective-permute-start | bytes 786440 | tf_op jit(solution)/shard_map/ppermute | solution.py:21
  38.0 3.4 %collective-permute-start = (bf16[512,256]{1,0:T(8,128)(2,1)S(1)}, bf16[512,256]{1,0:T(8,128)(2,1)S(1)}, u32[]{:S(2)}, u32[]{:S(2)}) collective-permute-start(bf16[512,256]{1,0:T(8,128)(2,1)S(1)} %pad_maximum_fusion), channel_id=1, source_target_pairs={{0,2},{1,3},{2,4},{3,5},{4,6},{5,7},{6,8},{7,9},{8,10},{9,11},{10,... | collective-permute-start | bytes 786440 | tf_op jit(solution)/shard_map/ppermute | solution.py:21
  42.1 2.3 %multiply_subtract_fusion = (f32[512,12,64]{0,2,1:T(8,128)S(1)}, f32[512,12,64]{0,2,1:T(8,128)S(1)}) fusion(f32[512,12,128]{0,2,1:T(8,128)} %bitcast.38, f32[512,64]{0,1:T(8,128)S(1)} %copy.46, f32[512,64]{0,1:T(8,128)S(1)} %copy.45), kind=kLoop, calls=%fused_computation.11 | loop fusion | flops 2359296 | bytes 6553600 | tf_op jit(solution)/shard_map/sub | solution.py:38
  44.4 0.5 fusion.3
  44.9 1.6 %copy.50.query_ref = bf16[512,1536]{1,0:T(8,128)(2,1)} copy(bf16[512,1536]{0,1:T(8,128)(2,1)S(1)} %bitcast.37) | data formatting | bytes 3145728 | tf_op jit(solution)/shard_map/convert_element_type | solution.py:113
  46.5 0.9 copy.52.first_ref
  47.5 1.6 %gather_fusion = bf16[128,16,256]{2,1,0:T(8,128)(2,1)} fusion(bf16[33,16,256]{2,1,0:T(8,128)(2,1)S(1)} %fusion.12, s32[1024]{0:T(1024)S(1)} %pad_clamp_fusion.1), kind=kCustom, calls=%fused_computation | custom fusion | bytes 2097664 | tf_op jit(solution)/shard_map/gather | solution.py:135
  49.1 9.8 %all-to-all-start.1 = ((bf16[128,16,256]{2,1,0:T(8,128)(2,1)}), bf16[128,16,256]{2,1,0:T(8,128)(2,1)S(1)}, u32[]{:S(2)}, u32[]{:S(2)}) async-start(bf16[128,16,256]{2,1,0:T(8,128)(2,1)} %gather_fusion), calls=%async_computation.1 | async-start | bytes 2097152 | tf_op jit(solution)/shard_map/all_to_all | solution.py:135
  59.2 0.8 fusion.20
  59.9 1.0 copy.51.keys_ref
  60.9 27.5 %shard_map.95 = bf16[512,1536]{1,0:T(8,128)(2,1)} custom-call(bf16[512,1536]{1,0:T(8,128)(2,1)} %copy.50.query_ref, bf16[128,1536]{1,0:T(8,128)(2,1)} %copy.51.keys_ref, bf16[1536,128]{1,0:T(8,128)(2,1)} %get-tuple-element.44.values_ref, s32[512,1]{1,0:T(8,128)} %copy.52.first_ref), custom_call_target="tpu_custom_call" | custom-call | tf_op jit(solution)/shard_map/pallas_call | solution.py:71
  88.4 6.6 %convolution_convert_fusion = bf16[512,1536]{1,0:T(8,128)(2,1)} fusion(bf16[512,1536]{1,0:T(8,128)(2,1)} %shard_map.95, bf16[1536,1536]{1,0:T(8,128)(2,1)} %param.18), kind=kOutput, calls=%fused_computation.9 | convolution fusion | flops 2416705536 | bytes 7864320 | tf_op jit(solution)/shard_map/dot_general | solution.py:128
  95.1 1.6 %gather_fusion.1 = bf16[128,16,256]{2,1,0:T(8,128)(2,1)} fusion(bf16[129,16,256]{2,1,0:T(8,128)(2,1)S(1)} %concatenate.47, s32[1024]{0:T(1024)S(1)} %pad_clamp_fusion), kind=kCustom, calls=%fused_computation.1 | custom fusion | bytes 2097664 | tf_op jit(solution)/shard_map/gather | solution.py:140
  (41 shorter events, 2.3 us)
Async XLA Ops:
  0.6 30.5 %copy-start = (bf16[1536,256]{1,0:T(8,128)(2,1)S(1)}, bf16[1536,256]{1,0:T(8,128)(2,1)}, u32[]{:S(2)}) copy-start(bf16[1536,256]{1,0:T(8,128)(2,1)} %param.17) | copy-start | bytes 2359300
  0.6 23.7 %copy-start.1 = (bf16[512,1536]{1,0:T(8,128)(2,1)S(1)}, bf16[512,1536]{1,0:T(8,128)(2,1)}, u32[]{:S(2)}) copy-start(bf16[512,1536]{1,0:T(8,128)(2,1)} %param.14) | copy-start | bytes 4718596
  0.7 23.7 %copy-start.3 = (f32[1536]{0:T(1024)S(1)}, f32[1536]{0:T(1024)}, u32[]{:S(2)}) copy-start(f32[1536]{0:T(1024)} %param.15) | copy-start | bytes 18436
  11.5 20.3 %all-to-all-start = ((s32[128,1,128]{2,1,0:T(1,128)}), s32[128,1,128]{2,1,0:T(1,128)S(1)}, u32[]{:S(2)}, u32[]{:S(2)}) async-start(s32[128,1,128]{2,1,0:T(1,128)} %copy.44), calls=%async_computation | async-start | bytes 131072 | tf_op jit(solution)/shard_map/all_to_all | solution.py:100
  31.1 2.8 %copy-start.2 = (s32[512]{0:T(512)S(1)}, s32[512]{0:T(512)}, u32[]{:S(2)}) copy-start(s32[512]{0:T(512)} %param.19) | copy-start | bytes 6148
  36.0 23.0 %collective-permute-start.1 = (bf16[512,256]{1,0:T(8,128)(2,1)S(1)}, bf16[512,256]{1,0:T(8,128)(2,1)S(1)}, u32[]{:S(2)}, u32[]{:S(2)}) collective-permute-start(bf16[512,256]{1,0:T(8,128)(2,1)S(1)} %pad_maximum_fusion), channel_id=1, source_target_pairs={{0,1},{1,2},{2,3},{3,4},{4,5},{5,6},{6,7},{7,8},{8,9},{9,10},{10,1... | collective-permute-start | bytes 786440 | tf_op jit(solution)/shard_map/ppermute | solution.py:21
  38.0 21.0 %collective-permute-start = (bf16[512,256]{1,0:T(8,128)(2,1)S(1)}, bf16[512,256]{1,0:T(8,128)(2,1)S(1)}, u32[]{:S(2)}, u32[]{:S(2)}) collective-permute-start(bf16[512,256]{1,0:T(8,128)(2,1)S(1)} %pad_maximum_fusion), channel_id=1, source_target_pairs={{0,2},{1,3},{2,4},{3,5},{4,6},{5,7},{6,8},{7,9},{8,10},{9,11},{10,... | collective-permute-start | bytes 786440 | tf_op jit(solution)/shard_map/ppermute | solution.py:21
  49.1 45.9 %all-to-all-start.1 = ((bf16[128,16,256]{2,1,0:T(8,128)(2,1)}), bf16[128,16,256]{2,1,0:T(8,128)(2,1)S(1)}, u32[]{:S(2)}, u32[]{:S(2)}) async-start(bf16[128,16,256]{2,1,0:T(8,128)(2,1)} %gather_fusion), calls=%async_computation.1 | async-start | bytes 2097152 | tf_op jit(solution)/shard_map/all_to_all | solution.py:135

commit v5 on v3

--- a/solution.py
+++ b/solution.py
@@ -52,24 +52,34 @@
     query_at = step * tile + lax.broadcasted_iota(jnp.int32, (tile, span), 0)
     key_at = key_first - back + lax.broadcasted_iota(jnp.int32, (tile, span), 1)
     valid = (key_at >= first_ref[...]) & (key_at <= query_at) & (query_at - key_at < WINDOW)
+    stacked = jnp.concatenate(
+        [query_ref[:, head * head_dim : (head + 1) * head_dim] for head in range(head_count)], 0
+    )
+    scores = lax.dot_general(
+        stacked, keys, (((1,), (1,)), ((), ())), preferred_element_type=jnp.float32
+    ).reshape(head_count, tile, span)
+    scores = jnp.where(valid[None], scores, -1e30)
+    peak = jnp.max(scores, 2, keepdims=True)
+    exponent = jnp.exp(scores - peak)
+    probs = (exponent / jnp.sum(exponent, 2, keepdims=True)).astype(jnp.bfloat16)
+    context = jnp.dot(
+        probs.reshape(head_count * tile, span), values, preferred_element_type=jnp.float32
+    )
     for head in range(head_count):
-        lanes = slice(head * head_dim, (head + 1) * head_dim)
-        scores = lax.dot_general(
-            query_ref[:, lanes], keys, (((1,), (1,)), ((), ())), preferred_element_type=jnp.float32
-        )
-        scores = jnp.where(valid, scores, -1e30)
-        peak = jnp.max(scores, 1, keepdims=True)
-        exponent = jnp.exp(scores - peak)
-        probs = (exponent / jnp.sum(exponent, 1, keepdims=True)).astype(jnp.bfloat16)
-        context = jnp.dot(probs, values, preferred_element_type=jnp.float32)
-        out_ref[:, lanes] = context.astype(out_ref.dtype)
+        out_ref[:, head * head_dim : (head + 1) * head_dim] = context[
+            head * tile : (head + 1) * tile
+        ].astype(out_ref.dtype)
 
 
 def attend(queries, keyval_rows, first_rel, back, tile=128):
     row_count, width = queries.shape
     head_dim = keyval_rows.shape[1] // 2
     kernel = functools.partial(
-        attend_kernel, tile=tile, back=back, head_count=width // head_dim, head_dim=head_dim
+        attend_kernel,
+        tile=tile,
+        back=back,
+        head_count=width // head_dim,
+        head_dim=head_dim,
     )
     return pl.pallas_call(
         kernel,
@@ -81,6 +91,7 @@
         ],
         out_specs=pl.BlockSpec((tile, width), lambda i: (i, 0)),
         out_shape=jax.ShapeDtypeStruct((row_count, width), jnp.bfloat16),
+        compiler_params=pltpu.CompilerParams(vmem_limit_bytes=60 * 1024 * 1024),
     )(queries, keyval_rows, first_rel)
 
 

time: 97.1 us -> 91.9 us (0.946)
  Pallas kernels: 27 us -> 21.8 us
    pallas_call x1, Pallas kernels: 27 us -> 21.8 us  [attend(): pl.pallas_call(kernel, grid=(row_count // tile,), in_specs=[pl.BlockSpec(...]
  transfers between devices with their start and end apart: 4 -> 4, of which waited for: 0 -> 0; matrix products, arithmetic and copies ran while one was open for 26% -> 28% of each run, Pallas kernels for 28% -> 24%
where the time goes in v5:
time: 91.9 us; the launch traced here: 90.1 us
  starting transfers between devices  25.5 us (28%)
  Pallas kernels  21.8 us (24%)
  other arithmetic  15 us (16%)
  matrix products  13.9 us (15%)
  local copies, waits for them, and re-layouts  9.62 us (10%)
  between operations  4.21 us (5%)
    pallas_call x1, Pallas kernels, attend(): pl.pallas_call(kernel, grid=(row_count // tile,), in_specs=[pl.BlockSpec(...  21.8 us
    all_to_all x1, starting transfers between devices, body(): lax.all_to_all(notes, 'seq', split_axis=0, concat_axis=0, tiled=True)  10.2 us
    all_to_all x1, starting transfers between devices, body(): lax.all_to_all(pages[pick], 'seq', split_axis=0, concat_axis=0, tiled=True)  9.84 us
    dot_general x1, matrix products, body(): jnp.dot(normed, w_query, preferred_element_type=jnp.float32)  6.75 us
    dot_general x1, matrix products, body(): jnp.dot(context, w_out, preferred_element_type=jnp.float32)  6.56 us
    ppermute x2, starting transfers between devices, passed_along(): return lax.ppermute(value, axis, pairs)  5.47 us
    another operation x6, other arithmetic  3.56 us
    sub x1, other arithmetic, rotate(): first_half * cosine - second_half * sine_part  2.35 us
  transfers between devices with their start and end apart: 4, of which 0 were waited for; matrix products, arithmetic and copies ran while one was open for 28% of the time, Pallas kernels for 24%

profile of v5, /device:TPU:32, one launch (start us, length us, event | category | flops | bytes accessed | tf_op | source)
XLA Modules:
  0.0 90.1 jit_solution(15984826956258844774)
XLA Ops:
  0.7 0.6 compare_reduce_fusion.3
  1.3 0.8 slice_compare_fusion.1
  2.1 1.3 %slice.93 = s32[1]{0:T(128)} slice(s32[512]{0:T(512)} %param.19), slice={[511:512]} | slice | bytes 8 | tf_op jit(solution)/shard_map/slice | solution.py:112
  3.4 0.7 compare_reduce_fusion.2
  4.1 0.6 compare_reduce_fusion.1
  4.8 0.3 reduce-window.9
  6.8 0.6 slice.98
  7.3 0.7 broadcast_add_fusion
  9.3 0.7 select_reduce_fusion
  10.2 0.6 fusion.16
  10.8 0.7 copy.40
  11.5 10.2 %all-to-all-start = ((s32[128,1,128]{2,1,0:T(1,128)}), s32[128,1,128]{2,1,0:T(1,128)S(1)}, u32[]{:S(2)}, u32[]{:S(2)}) async-start(s32[128,1,128]{2,1,0:T(1,128)} %copy.40), calls=%async_computation | async-start | bytes 131072 | tf_op jit(solution)/shard_map/all_to_all | solution.py:113
  21.8 0.7 fusion.15
  22.5 1.8 %fusion = f32[512]{0:T(512)S(1)} fusion(bf16[512,1536]{1,0:T(8,128)(2,1)} %param.14), kind=kLoop, calls=%fused_computation.4 | loop fusion | flops 2358784 | bytes 1574912 | tf_op jit(solution)/shard_map/reduce_sum | solution.py:121
  24.4 6.8 %fusion.9 = f32[512,1536]{0,1:T(8,128)} fusion(bf16[1536,1536]{1,0:T(8,128)(2,1)} %param.16, bf16[512,1536]{1,0:T(8,128)(2,1)S(1)} %copy-done.1, f32[1536]{0:T(1024)S(1)} %copy-done.3, f32[512]{0:T(512)S(1)} %add_rsqrt_fusion), kind=kOutput, calls=%fused_computation.18 | convolution fusion | flops 2419064832 | bytes 9445376 | tf_op jit(solution)/shard_map/dot_general | solution.py:123
  31.1 0.6 fusion.7
  32.0 0.5 constant_dynamic-slice_fusion
  33.3 0.6 fusion.19
  33.9 0.7 broadcast_subtract_fusion
  34.6 1.2 %subtract_convert_fusion = (bf16[512,64]{1,0:T(8,128)(2,1)S(1)}, bf16[512,64]{1,0:T(8,128)(2,1)S(1)}, f32[512,64]{1,0:T(8,128)S(1)}, f32[512,64]{1,0:T(8,128)S(1)}) fusion(f32[512,256]{1,0:T(8,128)S(1)} %fusion.7, f32[64]{0:T(128)S(1)} %multiply_power_fusion, f32[512]{0:T(512)S(1)} %get-tuple-element.47), kind=kLoop, calls=%fused_computation.26 | loop fusion | flops 294912 | bytes 657664 | tf_op jit(solution)/shard_map/convert.6
  36.0 2.0 %collective-permute-start.1 = (bf16[512,256]{1,0:T(8,128)(2,1)S(1)}, bf16[512,256]{1,0:T(8,128)(2,1)S(1)}, u32[]{:S(2)}, u32[]{:S(2)}) collective-permute-start(bf16[512,256]{1,0:T(8,128)(2,1)S(1)} %pad_maximum_fusion), channel_id=1, source_target_pairs={{0,1},{1,2},{2,3},{3,4},{4,5},{5,6},{6,7},{7,8},{8,9},{9,10},{10,1... | collective-permute-start | bytes 786440 | tf_op jit(solution)/shard_map/ppermute | solution.py:21
  38.0 3.4 %collective-permute-start = (bf16[512,256]{1,0:T(8,128)(2,1)S(1)}, bf16[512,256]{1,0:T(8,128)(2,1)S(1)}, u32[]{:S(2)}, u32[]{:S(2)}) collective-permute-start(bf16[512,256]{1,0:T(8,128)(2,1)S(1)} %pad_maximum_fusion), channel_id=1, source_target_pairs={{0,2},{1,3},{2,4},{3,5},{4,6},{5,7},{6,8},{7,9},{8,10},{9,11},{10,... | collective-permute-start | bytes 786440 | tf_op jit(solution)/shard_map/ppermute | solution.py:21
  42.1 2.3 %multiply_subtract_fusion = (f32[512,12,64]{0,2,1:T(8,128)S(1)}, f32[512,12,64]{0,2,1:T(8,128)S(1)}) fusion(f32[512,12,128]{0,2,1:T(8,128)} %bitcast.36, f32[512,64]{0,1:T(8,128)S(1)} %copy.42, f32[512,64]{0,1:T(8,128)S(1)} %copy.41), kind=kLoop, calls=%fused_computation.11 | loop fusion | flops 2359296 | bytes 6553600 | tf_op jit(solution)/shard_map/sub | solution.py:38
  44.4 0.5 fusion.3
  44.9 1.6 %copy.46.query_ref = bf16[512,1536]{1,0:T(8,128)(2,1)} copy(bf16[512,1536]{0,1:T(8,128)(2,1)S(1)} %bitcast.35) | data formatting | bytes 3145728 | tf_op jit(solution)/shard_map/convert_element_type | solution.py:126
  46.5 0.9 copy.47.first_ref
  47.5 1.6 %gather_fusion = bf16[128,16,256]{2,1,0:T(8,128)(2,1)} fusion(bf16[33,16,256]{2,1,0:T(8,128)(2,1)S(1)} %fusion.12, s32[1024]{0:T(1024)S(1)} %pad_clamp_fusion.1), kind=kCustom, calls=%fused_computation | custom fusion | bytes 2097664 | tf_op jit(solution)/shard_map/gather | solution.py:148
  49.1 9.8 %all-to-all-start.1 = ((bf16[128,16,256]{2,1,0:T(8,128)(2,1)}), bf16[128,16,256]{2,1,0:T(8,128)(2,1)S(1)}, u32[]{:S(2)}, u32[]{:S(2)}) async-start(bf16[128,16,256]{2,1,0:T(8,128)(2,1)} %gather_fusion), calls=%async_computation.1 | async-start | bytes 2097152 | tf_op jit(solution)/shard_map/all_to_all | solution.py:148
  59.0 1.0 %maximum_maximum_fusion.keyval_ref = bf16[1536,256]{1,0:T(8,128)(2,1)} fusion(bf16[512,128]{1,0:T(8,128)(2,1)S(1)} %slice.138, bf16[512,64]{1,0:T(8,128)(2,1)S(1)} %get-tuple-element.45, bf16[512,64]{1,0:T(8,128)(2,1)S(1)} %get-tuple-element.44, bf16[512,256]{1,0:T(8,128)(2,1)S(1)} %collective-permute-done.1, bf16[512,256]{1,0:T(8,128)(2,1)S(1)} %collective-permute-done), kind=kLoop, calls=%fused_computation.12 | loop fusion | flops 3932160 | bytes 1572864 | tf_op jit(solution)/shard_map/concatenate | solution.py:137
  60.0 21.8 %shard_map.95 = bf16[512,1536]{1,0:T(8,128)(2,1)} custom-call(bf16[512,1536]{1,0:T(8,128)(2,1)} %copy.46.query_ref, bf16[1536,256]{1,0:T(8,128)(2,1)} %maximum_maximum_fusion.keyval_ref, s32[512,1]{1,0:T(8,128)} %copy.47.first_ref), custom_call_target="tpu_custom_call" | custom-call | tf_op jit(solution)/shard_map/pallas_call | solution.py:84
  81.9 6.6 %convolution_convert_fusion = bf16[512,1536]{1,0:T(8,128)(2,1)} fusion(bf16[512,1536]{1,0:T(8,128)(2,1)} %shard_map.95, bf16[1536,1536]{1,0:T(8,128)(2,1)} %param.18), kind=kOutput, calls=%fused_computation.9 | convolution fusion | flops 2416705536 | bytes 7864320 | tf_op jit(solution)/shard_map/dot_general | solution.py:141
  88.5 1.6 %gather_fusion.1 = bf16[128,16,256]{2,1,0:T(8,128)(2,1)} fusion(bf16[129,16,256]{2,1,0:T(8,128)(2,1)S(1)} %concatenate.47, s32[1024]{0:T(1024)S(1)} %pad_clamp_fusion), kind=kCustom, calls=%fused_computation.1 | custom fusion | bytes 2097664 | tf_op jit(solution)/shard_map/gather | solution.py:153
  (39 shorter events, 1.8 us)
Async XLA Ops:
  0.6 30.5 %copy-start = (bf16[1536,256]{1,0:T(8,128)(2,1)S(1)}, bf16[1536,256]{1,0:T(8,128)(2,1)}, u32[]{:S(2)}) copy-start(bf16[1536,256]{1,0:T(8,128)(2,1)} %param.17) | copy-start | bytes 2359300
  0.6 23.7 %copy-start.1 = (bf16[512,1536]{1,0:T(8,128)(2,1)S(1)}, bf16[512,1536]{1,0:T(8,128)(2,1)}, u32[]{:S(2)}) copy-start(bf16[512,1536]{1,0:T(8,128)(2,1)} %param.14) | copy-start | bytes 4718596
  0.7 23.7 %copy-start.3 = (f32[1536]{0:T(1024)S(1)}, f32[1536]{0:T(1024)}, u32[]{:S(2)}) copy-start(f32[1536]{0:T(1024)} %param.15) | copy-start | bytes 18436
  11.5 20.3 %all-to-all-start = ((s32[128,1,128]{2,1,0:T(1,128)}), s32[128,1,128]{2,1,0:T(1,128)S(1)}, u32[]{:S(2)}, u32[]{:S(2)}) async-start(s32[128,1,128]{2,1,0:T(1,128)} %copy.40), calls=%async_computation | async-start | bytes 131072 | tf_op jit(solution)/shard_map/all_to_all | solution.py:113
  31.1 2.8 %copy-start.2 = (s32[512]{0:T(512)S(1)}, s32[512]{0:T(512)}, u32[]{:S(2)}) copy-start(s32[512]{0:T(512)} %param.19) | copy-start | bytes 6148
  36.0 23.0 %collective-permute-start.1 = (bf16[512,256]{1,0:T(8,128)(2,1)S(1)}, bf16[512,256]{1,0:T(8,128)(2,1)S(1)}, u32[]{:S(2)}, u32[]{:S(2)}) collective-permute-start(bf16[512,256]{1,0:T(8,128)(2,1)S(1)} %pad_maximum_fusion), channel_id=1, source_target_pairs={{0,1},{1,2},{2,3},{3,4},{4,5},{5,6},{6,7},{7,8},{8,9},{9,10},{10,1... | collective-permute-start | bytes 786440 | tf_op jit(solution)/shard_map/ppermute | solution.py:21
  38.0 21.0 %collective-permute-start = (bf16[512,256]{1,0:T(8,128)(2,1)S(1)}, bf16[512,256]{1,0:T(8,128)(2,1)S(1)}, u32[]{:S(2)}, u32[]{:S(2)}) collective-permute-start(bf16[512,256]{1,0:T(8,128)(2,1)S(1)} %pad_maximum_fusion), channel_id=1, source_target_pairs={{0,2},{1,3},{2,4},{3,5},{4,6},{5,7},{6,8},{7,9},{8,10},{9,11},{10,... | collective-permute-start | bytes 786440 | tf_op jit(solution)/shard_map/ppermute | solution.py:21
  49.1 39.3 %all-to-all-start.1 = ((bf16[128,16,256]{2,1,0:T(8,128)(2,1)}), bf16[128,16,256]{2,1,0:T(8,128)(2,1)S(1)}, u32[]{:S(2)}, u32[]{:S(2)}) async-start(bf16[128,16,256]{2,1,0:T(8,128)(2,1)} %gather_fusion), calls=%async_computation.1 | async-start | bytes 2097152 | tf_op jit(solution)/shard_map/all_to_all | solution.py:148

commit v6 on v5

--- a/solution.py
+++ b/solution.py
@@ -42,6 +42,23 @@
     )
 
 
+def rotate_lanes(vectors, positions, width):
+    half_dim = width // 2
+    pair_index = jnp.arange(half_dim, dtype=jnp.float32)
+    frequency = ROPE_BASE ** (-2.0 * pair_index / width)
+    angles = positions.astype(jnp.float32)[:, None] * frequency[None, :]
+    cosine = jnp.cos(angles)
+    sine_part = jnp.sin(angles)
+    repeats = vectors.shape[1] // width
+    cosine = jnp.tile(jnp.concatenate([cosine, cosine], 1), (1, repeats))
+    sine_part = jnp.tile(jnp.concatenate([-sine_part, sine_part], 1), (1, repeats))
+    lane = lax.broadcasted_iota(jnp.int32, vectors.shape, 1) % width
+    swapped = jnp.where(
+        lane < half_dim, jnp.roll(vectors, -half_dim, 1), jnp.roll(vectors, half_dim, 1)
+    )
+    return vectors * cosine + swapped * sine_part
+
+
 def attend_kernel(query_ref, keyval_ref, first_ref, out_ref, *, tile, back, head_count, head_dim):
     step = pl.program_id(0)
     span = tile + WINDOW
@@ -61,7 +78,7 @@
     scores = jnp.where(valid[None], scores, -1e30)
     peak = jnp.max(scores, 2, keepdims=True)
     exponent = jnp.exp(scores - peak)
-    probs = (exponent / jnp.sum(exponent, 2, keepdims=True)).astype(jnp.bfloat16)
+    probs = (exponent * (1.0 / jnp.sum(exponent, 2, keepdims=True))).astype(jnp.bfloat16)
     context = jnp.dot(
         probs.reshape(head_count * tile, span), values, preferred_element_type=jnp.float32
     )
@@ -103,13 +120,17 @@
     head_count = w_query.shape[1] // head_dim
     local_index = jnp.arange(row_count, dtype=jnp.int32)
     global_index = offset + local_index
-    change = jnp.concatenate([jnp.ones((1,), dtype=jnp.bool_), segment_ids[1:] != segment_ids[:-1]])
-    local_start = lax.cummax(jnp.where(change, local_index, 0))
+    local_start = jnp.sum((segment_ids[None, :] < segment_ids[:, None]).astype(jnp.int32), 1)
+    last_first = offset + jnp.sum((segment_ids < segment_ids[-1]).astype(jnp.int32))
     place = lax.axis_index("seq")
     owner_hits = page_owner[:, None] == jnp.arange(devices, dtype=jnp.int32)[None, :]
     slot_to = jnp.sum(jnp.where(owner_hits, page_slot[:, None] + 1, 0), 0)
-    notes = jnp.zeros((devices, 128), jnp.int32)
-    notes = notes.at[:, 0].set(segment_ids[-1]).at[:, 1].set(offset + local_start[-1]).at[:, 2].set(slot_to)
+    column = lax.broadcasted_iota(jnp.int32, (devices, 128), 1)
+    notes = jnp.where(
+        column == 0,
+        segment_ids[-1],
+        jnp.where(column == 1, last_first, jnp.where(column == 2, slot_to[:, None], 0)),
+    )
     heard = lax.all_to_all(notes, "seq", split_axis=0, concat_axis=0, tiled=True)
     source = jnp.arange(devices, dtype=jnp.int32)
     prior_id = jnp.where(place >= 1, heard[jnp.maximum(place - 1, 0), 0], -1)
@@ -120,10 +141,8 @@
     wide = tokens.astype(jnp.float32)
     mean_square = jnp.mean(wide * wide, -1, keepdims=True)
     normed = (wide * lax.rsqrt(mean_square + EPS) * norm_gain).astype(jnp.bfloat16)
-    queries = jnp.dot(normed, w_query, preferred_element_type=jnp.float32).reshape(
-        row_count, head_count, head_dim
-    )
-    queries = (rotate(queries, positions) * head_dim ** (-0.5)).astype(jnp.bfloat16)
+    queries = jnp.dot(normed, w_query, preferred_element_type=jnp.float32)
+    queries = (rotate_lanes(queries, positions, head_dim) * head_dim ** (-0.5)).astype(jnp.bfloat16)
     projected = jnp.dot(normed, w_key_value, preferred_element_type=jnp.float32)
     keyval = jnp.concatenate(
         [rotate(projected[:, :head_dim], positions), projected[:, head_dim:]], 1
@@ -133,7 +152,7 @@
     ordered = blocks[::-1]
     back = reach * row_count
     context = attend(
-        queries.reshape(row_count, head_count * head_dim),
+        queries,
         jnp.concatenate(ordered, 0),
         (starts - offset)[:, None],
         back,

time: 91.9 us -> 109 us (1.19)
  local copies, waits for them, and re-layouts: 9.62 us -> 22.5 us
  other arithmetic: 15 us -> 22.7 us
  between operations: 4.21 us -> 2.25 us
  matrix products: 13.9 us -> 12.2 us
    another operation x3 -> x4, local copies, waits for them, and re-layouts: 0.2 us -> 11.2 us  [the longest x2 5.61 us: rotate_lanes(): cosine = jnp.tile(jnp.concatenate([cosine, cosine], 1), (1, repeats))]
    convert_element_type x1, other arithmetic: 0.47 us -> 7.59 us  [body(): (rotate_lanes(queries, positions, head_dim) * head_dim ** (-0.5)).astype(...]
    slice x1 -> x2, local copies, waits for them, and re-layouts: 0.58 us -> 4 us  [rotate_lanes(): jnp.roll(vectors, half_dim, 1)]
    reduce_sum x0 -> x2, other arithmetic: none -> 2.97 us  [the longest x1 1.96 us: body(): jnp.sum((segment_ids < segment_ids[-1]).astype(jnp.int32))]
    sub x1 -> x0, other arithmetic: 2.35 us -> none  [rotate(): first_half * cosine - second_half * sine_part]
    dot_general x1, matrix products: 6.75 us -> 5.04 us  [body(): queries = jnp.dot(normed, w_query, preferred_element_type=jnp.float32)]
    convert_element_type x1 -> x0, local copies, waits for them, and re-layouts: 1.57 us -> none  [body(): (rotate(queries, positions) * head_dim ** (-0.5)).astype(jnp.bfloat16)]
    another operation x7 -> x1, other arithmetic: 3.63 us -> 2.21 us
  transfers between devices with their start and end apart: 4 -> 4, of which waited for: 0 -> 0; matrix products, arithmetic and copies ran while one was open for 28% -> 41% of each run, Pallas kernels for 24% -> 20%
where the time goes in v6:
time: 109 us; the launch traced here: 107 us
  starting transfers between devices  25.8 us (24%)
  other arithmetic  22.7 us (21%)
  local copies, waits for them, and re-layouts  22.5 us (21%)
  Pallas kernels  21.8 us (20%)
  matrix products  12.2 us (11%)
  between operations  2.25 us (2%)
    pallas_call x1, Pallas kernels, attend(): pl.pallas_call(kernel, grid=(row_count // tile,), in_specs=[pl.BlockSpec(...  21.8 us
    all_to_all x1, starting transfers between devices, body(): lax.all_to_all(pages[pick], 'seq', split_axis=0, concat_axis=0, tiled=True)  10.2 us
    all_to_all x1, starting transfers between devices, body(): lax.all_to_all(notes, 'seq', split_axis=0, concat_axis=0, tiled=True)  10.2 us
    convert_element_type x1, other arithmetic, body(): (rotate_lanes(queries, positions, head_dim) * head_dim ** (-0.5)).astype(...  7.59 us
    dot_general x1, matrix products, body(): jnp.dot(context, w_out, preferred_element_type=jnp.float32)  6.56 us
    another operation x2, local copies, waits for them, and re-layouts, rotate_lanes(): cosine = jnp.tile(jnp.concatenate([cosine, cosine], 1), (1, repeats))  5.61 us
    another operation x2, local copies, waits for them, and re-layouts, rotate_lanes(): jnp.tile(jnp.concatenate([-sine_part, sine_part], 1), (1, repeats))  5.58 us
    ppermute x2, starting transfers between devices, passed_along(): return lax.ppermute(value, axis, pairs)  5.35 us
  transfers between devices with their start and end apart: 4, of which 0 were waited for; matrix products, arithmetic and copies ran while one was open for 41% of the time, Pallas kernels for 20%

profile of v6, /device:TPU:32, one launch (start us, length us, event | category | flops | bytes accessed | tf_op | source)
XLA Modules:
  0.0 107.3 jit_solution(1482729016994276468)
XLA Ops:
  0.7 1.3 %slice.41 = s32[1]{0:T(128)} slice(s32[512]{0:T(512)} %param.13), slice={[511:512]} | slice | bytes 8 | tf_op jit(solution)/shard_map/slice | solution.py:131
  2.0 2.0 %convert_reduce_fusion.1 = s32[]{:T(128)} fusion(s32[512]{0:T(512)} %param.13, s32[]{:T(128)} %bitcast), kind=kLoop, calls=%fused_computation.62 | loop fusion | flops 1535 | bytes 2056 | tf_op jit(solution)/shard_map/reduce_sum | solution.py:124
  4.0 0.7 broadcast_add_fusion
  5.3 0.7 select_reduce_fusion
  6.0 1.5 %broadcast_select_fusion.2 = s32[128,1,128]{2,1,0:T(1,128)} fusion(pred[128]{0:T(512)(128)(4,1)S(1)} %iota_compare_fusion.4, pred[128]{0:T(512)(128)(4,1)S(1)} %get-tuple-element.18, pred[128]{0:T(512)(128)(4,1)S(1)} %get-tuple-element.17, s32[]{:T(128)S(6)} %add.89, s32[]{:T(128)} %bitcast, s32[128]{0:T(128)S(1)} %get-tuple-element.5), kind=kLoop, calls=%fused_computation.39 | loop fusion | flops 49152 | bytes 66440 | tf_op jit(solution)/shard_map/jit(_where)/select_n | solution.py:129
  7.5 10.2 %all-to-all-start = ((s32[128,1,128]{2,1,0:T(1,128)}), s32[128,1,128]{2,1,0:T(1,128)S(1)}, u32[]{:S(2)}, u32[]{:S(2)}) async-start(s32[128,1,128]{2,1,0:T(1,128)} %broadcast_select_fusion.2), calls=%async_computation | async-start | bytes 131072 | tf_op jit(solution)/shard_map/all_to_all | solution.py:134
  17.7 1.0 convert_reduce_fusion
  18.8 1.8 %fusion = f32[512]{0:T(512)S(1)} fusion(bf16[512,1536]{1,0:T(8,128)(2,1)} %param.8), kind=kLoop, calls=%fused_computation.4 | loop fusion | flops 2358784 | bytes 1574912 | tf_op jit(solution)/shard_map/reduce_sum | solution.py:142
  20.6 5.0 %fusion.12 = f32[512,1536]{1,0:T(8,128)S(1)} fusion(bf16[1536,1536]{1,0:T(8,128)(2,1)} %param.10, bf16[512,1536]{1,0:T(8,128)(2,1)} %param.8, f32[1536]{0:T(1024)} %param.9, f32[512]{0:T(512)S(1)} %add_rsqrt_fusion), kind=kOutput, calls=%fused_computation.21 | convolution fusion | flops 2419064832 | bytes 9445376 | tf_op jit(solution)/shard_map/dot_general | solution.py:144
  25.7 3.9 %fusion.34 = (f32[512,1472]{1,0:T(8,128)}, f32[512,1472]{1,0:T(8,128)}) fusion(f32[512,1536]{1,0:T(8,128)S(1)} %fusion.12), kind=kLoop, calls=%fused_computation.77 | loop fusion | bytes 12058624 | tf_op jit(solution)/shard_map/jit(_roll_static)/slice | solution.py:57
  29.8 0.6 fusion.10
  30.5 0.8 copy-done.3
  31.5 0.5 constant_dynamic-slice_fusion
  32.8 0.6 fusion.32
  33.4 0.7 broadcast_subtract_fusion
  34.1 2.2 %fusion.20 = (bf16[512,64]{1,0:T(8,128)(2,1)S(1)}, bf16[512,64]{1,0:T(8,128)(2,1)S(1)}, f32[512,64]{1,0:T(8,128)S(1)}, f32[512,64]{1,0:T(8,128)S(1)}, f32[512,64]{1,0:T(8,128)S(1)}) fusion(f32[512,256]{1,0:T(8,128)} %copy-done.3, f32[64]{0:T(128)S(1)} %multiply_power_fusion, f32[512]{0:T(512)S(1)} %get-tuple-element.13), kind=kLoop, calls=%fused_computation.30 | loop fusion | flops 327680 | bytes 788736 | tf_op jit(solution)/shard_map/convert.6
  36.3 0.9 pad_maximum_fusion.2
  37.2 3.4 %collective-permute-start = (bf16[512,256]{1,0:T(8,128)(2,1)}, bf16[512,256]{1,0:T(8,128)(2,1)}, u32[]{:S(2)}, u32[]{:S(2)}) collective-permute-start(bf16[512,256]{1,0:T(8,128)(2,1)} %pad_maximum_fusion.2), channel_id=1, source_target_pairs={{0,2},{1,3},{2,4},{3,5},{4,6},{5,7},{6,8},{7,9},{8,10},{9,11},{10,... | collective-permute-start | bytes 786440 | tf_op jit(solution)/shard_map/ppermute | solution.py:21
  40.6 1.9 %collective-permute-start.1 = (bf16[512,256]{1,0:T(8,128)(2,1)}, bf16[512,256]{1,0:T(8,128)(2,1)}, u32[]{:S(2)}, u32[]{:S(2)}) collective-permute-start(bf16[512,256]{1,0:T(8,128)(2,1)} %pad_maximum_fusion.2), channel_id=1, source_target_pairs={{0,1},{1,2},{2,3},{3,4},{4,5},{5,6},{6,7},{7,8},{8,9},{9,10},{10,1... | collective-permute-start | bytes 786440 | tf_op jit(solution)/shard_map/ppermute | solution.py:21
  42.7 0.2 fusion.23
  43.2 2.1 %tile.20 = f32[512,12,128]{0,2,1:T(8,128)} broadcast(f32[512,128]{0,1:T(8,128)S(1)} %copy.39), dimensions={0,2} | broadcast | bytes 3407872 | tf_op jit(solution)/shard_map/tile | solution.py:54
  45.3 3.5 %copy.40 = f32[512,1536]{1,0:T(8,128)} copy(f32[512,1536]{0,1:T(8,128)} %bitcast.22) | data formatting | bytes 6291456 | tf_op jit(solution)/shard_map/tile | solution.py:54
  49.0 2.1 %tile.8 = f32[512,12,128]{0,2,1:T(8,128)} broadcast(f32[512,128]{0,1:T(8,128)S(1)} %copy.37), dimensions={0,2} | broadcast | bytes 3407872 | tf_op jit(solution)/shard_map/tile | solution.py:53
  51.1 3.6 %copy.38 = f32[512,1536]{1,0:T(8,128)} copy(f32[512,1536]{0,1:T(8,128)} %bitcast.23) | data formatting | bytes 6291456 | tf_op jit(solution)/shard_map/tile | solution.py:53
  54.7 0.9 copy.44.first_ref
  55.7 1.6 %gather_fusion = bf16[128,16,256]{2,1,0:T(8,128)(2,1)} fusion(bf16[33,16,256]{2,1,0:T(8,128)(2,1)S(1)} %fusion.18, s32[1024]{0:T(1024)S(1)} %pad_clamp_fusion.1), kind=kCustom, calls=%fused_computation | custom fusion | bytes 2097664 | tf_op jit(solution)/shard_map/gather | solution.py:167
  57.3 10.2 %all-to-all-start.1 = ((bf16[128,16,256]{2,1,0:T(8,128)(2,1)}), bf16[128,16,256]{2,1,0:T(8,128)(2,1)S(1)}, u32[]{:S(2)}, u32[]{:S(2)}) async-start(bf16[128,16,256]{2,1,0:T(8,128)(2,1)} %gather_fusion), calls=%async_computation.1 | async-start | bytes 2097152 | tf_op jit(solution)/shard_map/all_to_all | solution.py:167
  67.5 7.6 %fusion.6.query_ref = bf16[512,1536]{1,0:T(8,128)(2,1)} fusion(f32[512,1536]{1,0:T(8,128)} %copy.40, f32[512,64]{1,0:T(8,128)S(1)} %get-tuple-element.7, f32[512,1472]{1,0:T(8,128)} %get-tuple-element.9, f32[512,1472]{1,0:T(8,128)} %get-tuple-element.8, f32[512,64]{1,0:T(8,128)S(1)} %get-tuple-element.6, f32[512,1536]{1,0:T(8,128)} %copy-done.1, ...), kind=kLoop, calls=%fused_computation.11 | loop fusion | flops 7864320 | bytes 17315328 | tf_op jit(solution)/shard_map/convert_element_type | solution.py:145
  75.2 2.1 %maximum_maximum_fusion.keyval_ref = bf16[1536,256]{1,0:T(8,128)(2,1)} fusion(bf16[512,128]{1,0:T(8,128)(2,1)S(1)} %slice.76, bf16[512,64]{1,0:T(8,128)(2,1)S(1)} %get-tuple-element.11, bf16[512,64]{1,0:T(8,128)(2,1)S(1)} %get-tuple-element.10, bf16[512,256]{1,0:T(8,128)(2,1)} %collective-permute-done.1, bf16[512,256]{1,0:T(8,128)(2,1)} %collective-permute-done), kind=kLoop, calls=%fused_computation.15 | loop fusion | flops 3932160 | bytes 1572864 | tf_op jit(solution)/shard_map/concatenate | solution.py:156
  77.2 21.8 %shard_map.95 = bf16[512,1536]{1,0:T(8,128)(2,1)} custom-call(bf16[512,1536]{1,0:T(8,128)(2,1)} %fusion.6.query_ref, bf16[1536,256]{1,0:T(8,128)(2,1)} %maximum_maximum_fusion.keyval_ref, s32[512,1]{1,0:T(8,128)} %copy.44.first_ref), custom_call_target="tpu_custom_call" | custom-call | tf_op jit(solution)/shard_map/pallas_call | solution.py:101
  99.1 6.6 %convolution_convert_fusion = bf16[512,1536]{1,0:T(8,128)(2,1)} fusion(bf16[512,1536]{1,0:T(8,128)(2,1)} %shard_map.95, bf16[1536,1536]{1,0:T(8,128)(2,1)} %param.12), kind=kOutput, calls=%fused_computation.13 | convolution fusion | flops 2416705536 | bytes 7864320 | tf_op jit(solution)/shard_map/dot_general | solution.py:160
  105.7 1.6 %gather_fusion.1 = bf16[128,16,256]{2,1,0:T(8,128)(2,1)} fusion(bf16[129,16,256]{2,1,0:T(8,128)(2,1)S(1)} %concatenate.48, s32[1024]{0:T(1024)S(1)} %pad_clamp_fusion), kind=kCustom, calls=%fused_computation.1 | custom fusion | bytes 2097664 | tf_op jit(solution)/shard_map/gather | solution.py:172
  (40 shorter events, 1.6 us)
Async XLA Ops:
  0.6 29.2 %copy-start = (bf16[1536,256]{1,0:T(8,128)(2,1)S(1)}, bf16[1536,256]{1,0:T(8,128)(2,1)}, u32[]{:S(2)}) copy-start(bf16[1536,256]{1,0:T(8,128)(2,1)} %param.11) | copy-start | bytes 2359300
  7.5 23.8 %all-to-all-start = ((s32[128,1,128]{2,1,0:T(1,128)}), s32[128,1,128]{2,1,0:T(1,128)S(1)}, u32[]{:S(2)}, u32[]{:S(2)}) async-start(s32[128,1,128]{2,1,0:T(1,128)} %broadcast_select_fusion.2), calls=%async_computation | async-start | bytes 131072 | tf_op jit(solution)/shard_map/all_to_all | solution.py:134
  25.6 3.9 %copy-start.1 = (f32[512,1536]{1,0:T(8,128)}, f32[512,1536]{1,0:T(8,128)S(1)}, u32[]{:S(2)}) copy-start(f32[512,1536]{1,0:T(8,128)S(1)} %fusion.12) | copy-start | bytes 9437188
  25.6 4.1 %copy-start.5 = (s32[32]{0:T(128)S(1)}, s32[32]{0:T(128)}, u32[]{:S(2)}) copy-start(s32[32]{0:T(128)} %param.14) | copy-start | bytes 388
  25.6 4.2 %copy-start.2 = (bf16[512,1536]{1,0:T(8,128)(2,1)S(1)}, bf16[512,1536]{1,0:T(8,128)(2,1)}, u32[]{:S(2)}) copy-start(bf16[512,1536]{1,0:T(8,128)(2,1)} %param.8) | copy-start | bytes 4718596
  25.6 4.2 %copy-start.6 = (f32[1536]{0:T(1024)S(1)}, f32[1536]{0:T(1024)}, u32[]{:S(2)}) copy-start(f32[1536]{0:T(1024)} %param.9) | copy-start | bytes 18436
  29.5 3.9 %copy-start.4 = (s32[512]{0:T(512)S(1)}, s32[512]{0:T(512)}, u32[]{:S(2)}) copy-start(s32[512]{0:T(512)} %param.13) | copy-start | bytes 6148
  30.5 0.8 copy-start.3
  37.2 38.0 %collective-permute-start = (bf16[512,256]{1,0:T(8,128)(2,1)}, bf16[512,256]{1,0:T(8,128)(2,1)}, u32[]{:S(2)}, u32[]{:S(2)}) collective-permute-start(bf16[512,256]{1,0:T(8,128)(2,1)} %pad_maximum_fusion.2), channel_id=1, source_target_pairs={{0,2},{1,3},{2,4},{3,5},{4,6},{5,7},{6,8},{7,9},{8,10},{9,11},{10,... | collective-permute-start | bytes 786440 | tf_op jit(solution)/shard_map/ppermute | solution.py:21
  40.6 34.5 %collective-permute-start.1 = (bf16[512,256]{1,0:T(8,128)(2,1)}, bf16[512,256]{1,0:T(8,128)(2,1)}, u32[]{:S(2)}, u32[]{:S(2)}) collective-permute-start(bf16[512,256]{1,0:T(8,128)(2,1)} %pad_maximum_fusion.2), channel_id=1, source_target_pairs={{0,1},{1,2},{2,3},{3,4},{4,5},{5,6},{6,7},{7,8},{8,9},{9,10},{10,1... | collective-permute-start | bytes 786440 | tf_op jit(solution)/shard_map/ppermute | solution.py:21
  57.3 48.4 %all-to-all-start.1 = ((bf16[128,16,256]{2,1,0:T(8,128)(2,1)}), bf16[128,16,256]{2,1,0:T(8,128)(2,1)S(1)}, u32[]{:S(2)}, u32[]{:S(2)}) async-start(bf16[128,16,256]{2,1,0:T(8,128)(2,1)} %gather_fusion), calls=%async_computation.1 | async-start | bytes 2097152 | tf_op jit(solution)/shard_map/all_to_all | solution.py:167

commit v7 on v5

--- a/solution.py
+++ b/solution.py
@@ -103,13 +103,17 @@
     head_count = w_query.shape[1] // head_dim
     local_index = jnp.arange(row_count, dtype=jnp.int32)
     global_index = offset + local_index
-    change = jnp.concatenate([jnp.ones((1,), dtype=jnp.bool_), segment_ids[1:] != segment_ids[:-1]])
-    local_start = lax.cummax(jnp.where(change, local_index, 0))
+    local_start = jnp.sum((segment_ids[None, :] < segment_ids[:, None]).astype(jnp.int32), 1)
+    last_first = offset + jnp.sum((segment_ids < segment_ids[-1]).astype(jnp.int32))
     place = lax.axis_index("seq")
     owner_hits = page_owner[:, None] == jnp.arange(devices, dtype=jnp.int32)[None, :]
     slot_to = jnp.sum(jnp.where(owner_hits, page_slot[:, None] + 1, 0), 0)
-    notes = jnp.zeros((devices, 128), jnp.int32)
-    notes = notes.at[:, 0].set(segment_ids[-1]).at[:, 1].set(offset + local_start[-1]).at[:, 2].set(slot_to)
+    column = lax.broadcasted_iota(jnp.int32, (devices, 128), 1)
+    notes = jnp.where(
+        column == 0,
+        segment_ids[-1],
+        jnp.where(column == 1, last_first, jnp.where(column == 2, slot_to[:, None], 0)),
+    )
     heard = lax.all_to_all(notes, "seq", split_axis=0, concat_axis=0, tiled=True)
     source = jnp.arange(devices, dtype=jnp.int32)
     prior_id = jnp.where(place >= 1, heard[jnp.maximum(place - 1, 0), 0], -1)

time: 91.9 us -> 89 us (0.968)
  between operations: 4.21 us -> 2.21 us
  local copies, waits for them, and re-layouts: 9.62 us -> 8.11 us
    reduce_sum x0 -> x2, other arithmetic: none -> 2.97 us  [the longest x1 1.96 us: body(): jnp.sum((segment_ids < segment_ids[-1]).astype(jnp.int32))]
    another operation x7 -> x1, other arithmetic: 3.63 us -> 1.22 us
    select_n x1, other arithmetic: 0.08 us -> 1.48 us  [body(): jnp.where(column == 0, segment_ids[-1], jnp.where(column == 1, last_first...]
  transfers between devices with their start and end apart: 4 -> 4, of which waited for: 0 -> 0; matrix products, arithmetic and copies ran while one was open for 28% -> 30% of each run, Pallas kernels for 24% -> 25%
where the time goes in v7:
time: 89 us; the launch traced here: 87.2 us
  starting transfers between devices  25.5 us (29%)
  Pallas kernels  21.8 us (24%)
  other arithmetic  15.6 us (18%)
  matrix products  13.9 us (16%)
  local copies, waits for them, and re-layouts  8.11 us (9%)
  between operations  2.21 us (2%)
    pallas_call x1, Pallas kernels, attend(): pl.pallas_call(kernel, grid=(row_count // tile,), in_specs=[pl.BlockSpec(...  21.8 us
    all_to_all x1, starting transfers between devices, body(): lax.all_to_all(notes, 'seq', split_axis=0, concat_axis=0, tiled=True)  10.2 us
    all_to_all x1, starting transfers between devices, body(): lax.all_to_all(pages[pick], 'seq', split_axis=0, concat_axis=0, tiled=True)  9.84 us
    dot_general x1, matrix products, body(): jnp.dot(normed, w_query, preferred_element_type=jnp.float32)  6.75 us
    dot_general x1, matrix products, body(): jnp.dot(context, w_out, preferred_element_type=jnp.float32)  6.56 us
    ppermute x2, starting transfers between devices, passed_along(): return lax.ppermute(value, axis, pairs)  5.47 us
    sub x1, other arithmetic, rotate(): first_half * cosine - second_half * sine_part  2.35 us
    reduce_sum x1, other arithmetic, body(): jnp.sum((segment_ids < segment_ids[-1]).astype(jnp.int32))  1.96 us
  transfers between devices with their start and end apart: 4, of which 0 were waited for; matrix products, arithmetic and copies ran while one was open for 30% of the time, Pallas kernels for 25%

profile of v7, /device:TPU:32, one launch (start us, length us, event | category | flops | bytes accessed | tf_op | source)
XLA Modules:
  0.0 87.2 jit_solution(9484767840521539115)
XLA Ops:
  0.7 1.4 %slice.32 = s32[1]{0:T(128)} slice(s32[512]{0:T(512)} %param.13), slice={[511:512]} | slice | bytes 8 | tf_op jit(solution)/shard_map/slice | solution.py:114
  2.1 2.0 %convert_reduce_fusion.1 = s32[]{:T(128)} fusion(s32[512]{0:T(512)} %param.13, s32[]{:T(128)} %bitcast.1), kind=kLoop, calls=%fused_computation.48 | loop fusion | flops 1535 | bytes 2056 | tf_op jit(solution)/shard_map/reduce_sum | solution.py:107
  4.1 0.7 broadcast_add_fusion
  5.4 0.7 select_reduce_fusion
  6.1 1.5 %broadcast_select_fusion.2 = s32[128,1,128]{2,1,0:T(1,128)} fusion(pred[128]{0:T(512)(128)(4,1)S(1)} %iota_compare_fusion.4, pred[128]{0:T(512)(128)(4,1)S(1)} %get-tuple-element.15, pred[128]{0:T(512)(128)(4,1)S(1)} %get-tuple-element.14, s32[]{:T(128)S(6)} %add.82, s32[]{:T(128)} %bitcast.1, s32[128]{0:T(128)S(1)} %get-tuple-element.5), kind=kLoop, calls=%fused_computation.30 | loop fusion | flops 49152 | bytes 66440 | tf_op jit(solution)/shard_map/jit(_where)/select_n | solution.py:112
  7.6 10.2 %all-to-all-start = ((s32[128,1,128]{2,1,0:T(1,128)}), s32[128,1,128]{2,1,0:T(1,128)S(1)}, u32[]{:S(2)}, u32[]{:S(2)}) async-start(s32[128,1,128]{2,1,0:T(1,128)} %broadcast_select_fusion.2), calls=%async_computation | async-start | bytes 131072 | tf_op jit(solution)/shard_map/all_to_all | solution.py:117
  17.9 1.0 %convert_reduce_fusion = s32[512]{0:T(512)S(1)} fusion(s32[512]{0:T(512)} %param.13), kind=kLoop, calls=%fused_computation.12 | loop fusion | flops 785920 | bytes 4096 | tf_op jit(solution)/shard_map/reduce_sum | solution.py:106
  18.9 0.7 fusion.15
  19.6 1.8 %fusion = f32[512]{0:T(512)S(1)} fusion(bf16[512,1536]{1,0:T(8,128)(2,1)} %param.8), kind=kLoop, calls=%fused_computation.4 | loop fusion | flops 2358784 | bytes 1574912 | tf_op jit(solution)/shard_map/reduce_sum | solution.py:125
  21.4 6.7 %fusion.9 = f32[512,1536]{0,1:T(8,128)} fusion(bf16[1536,1536]{1,0:T(8,128)(2,1)} %param.10, bf16[512,1536]{1,0:T(8,128)(2,1)S(1)} %copy-done.1, f32[1536]{0:T(1024)S(1)} %copy-done.3, f32[512]{0:T(512)S(1)} %add_rsqrt_fusion), kind=kOutput, calls=%fused_computation.19 | convolution fusion | flops 2419064832 | bytes 9445376 | tf_op jit(solution)/shard_map/dot_general | solution.py:127
  28.2 0.6 fusion.7
  28.9 0.2 slice_reduce_fusion
  29.1 0.5 constant_dynamic-slice_fusion
  30.4 0.6 fusion.18
  31.0 0.7 broadcast_subtract_fusion
  31.7 1.2 %subtract_convert_fusion = (bf16[512,64]{1,0:T(8,128)(2,1)S(1)}, bf16[512,64]{1,0:T(8,128)(2,1)S(1)}, f32[512,64]{1,0:T(8,128)S(1)}, f32[512,64]{1,0:T(8,128)S(1)}) fusion(f32[512,256]{1,0:T(8,128)S(1)} %fusion.7, f32[64]{0:T(128)S(1)} %multiply_power_fusion, f32[512]{0:T(512)S(1)} %get-tuple-element.11), kind=kLoop, calls=%fused_computation.27 | loop fusion | flops 294912 | bytes 657664 | tf_op jit(solution)/shard_map/convert.6
  32.9 0.1 pad_maximum_fusion
  33.1 2.0 %collective-permute-start.1 = (bf16[512,256]{1,0:T(8,128)(2,1)S(1)}, bf16[512,256]{1,0:T(8,128)(2,1)S(1)}, u32[]{:S(2)}, u32[]{:S(2)}) collective-permute-start(bf16[512,256]{1,0:T(8,128)(2,1)S(1)} %pad_maximum_fusion), channel_id=1, source_target_pairs={{0,1},{1,2},{2,3},{3,4},{4,5},{5,6},{6,7},{7,8},{8,9},{9,10},{10,1... | collective-permute-start | bytes 786440 | tf_op jit(solution)/shard_map/ppermute | solution.py:21
  35.1 3.4 %collective-permute-start = (bf16[512,256]{1,0:T(8,128)(2,1)S(1)}, bf16[512,256]{1,0:T(8,128)(2,1)S(1)}, u32[]{:S(2)}, u32[]{:S(2)}) collective-permute-start(bf16[512,256]{1,0:T(8,128)(2,1)S(1)} %pad_maximum_fusion), channel_id=1, source_target_pairs={{0,2},{1,3},{2,4},{3,5},{4,6},{5,7},{6,8},{7,9},{8,10},{9,11},{10,... | collective-permute-start | bytes 786440 | tf_op jit(solution)/shard_map/ppermute | solution.py:21
  38.5 0.2 compare_reduce_fusion
  38.7 0.2 fusion.13
  39.1 2.3 %multiply_subtract_fusion = (f32[512,12,64]{0,2,1:T(8,128)S(1)}, f32[512,12,64]{0,2,1:T(8,128)S(1)}) fusion(f32[512,12,128]{0,2,1:T(8,128)} %bitcast.23, f32[512,64]{0,1:T(8,128)S(1)} %copy.39, f32[512,64]{0,1:T(8,128)S(1)} %copy.38), kind=kLoop, calls=%fused_computation.11 | loop fusion | flops 2359296 | bytes 6553600 | tf_op jit(solution)/shard_map/sub | solution.py:38
  41.5 0.5 fusion.3
  42.0 1.6 %copy.43.query_ref = bf16[512,1536]{1,0:T(8,128)(2,1)} copy(bf16[512,1536]{0,1:T(8,128)(2,1)S(1)} %bitcast.22) | data formatting | bytes 3145728 | tf_op jit(solution)/shard_map/convert_element_type | solution.py:130
  43.6 0.9 copy.44.first_ref
  44.4 0.1 fusion.12
  44.6 1.6 %gather_fusion = bf16[128,16,256]{2,1,0:T(8,128)(2,1)} fusion(bf16[33,16,256]{2,1,0:T(8,128)(2,1)S(1)} %fusion.12, s32[1024]{0:T(1024)S(1)} %pad_clamp_fusion.1), kind=kCustom, calls=%fused_computation | custom fusion | bytes 2097664 | tf_op jit(solution)/shard_map/gather | solution.py:152
  46.2 9.8 %all-to-all-start.1 = ((bf16[128,16,256]{2,1,0:T(8,128)(2,1)}), bf16[128,16,256]{2,1,0:T(8,128)(2,1)S(1)}, u32[]{:S(2)}, u32[]{:S(2)}) async-start(bf16[128,16,256]{2,1,0:T(8,128)(2,1)} %gather_fusion), calls=%async_computation.1 | async-start | bytes 2097152 | tf_op jit(solution)/shard_map/all_to_all | solution.py:152
  56.1 1.0 %maximum_maximum_fusion.keyval_ref = bf16[1536,256]{1,0:T(8,128)(2,1)} fusion(bf16[512,128]{1,0:T(8,128)(2,1)S(1)} %slice.66, bf16[512,64]{1,0:T(8,128)(2,1)S(1)} %get-tuple-element.9, bf16[512,64]{1,0:T(8,128)(2,1)S(1)} %get-tuple-element.8, bf16[512,256]{1,0:T(8,128)(2,1)S(1)} %collective-permute-done.1, bf16[512,256]{1,0:T(8,128)(2,1)S(1)} %collective-permute-done), kind=kLoop, calls=%fused_computation.13 | loop fusion | flops 3932160 | bytes 1572864 | tf_op jit(solution)/shard_map/concatenate | solution.py:141
  57.1 21.8 %shard_map.95 = bf16[512,1536]{1,0:T(8,128)(2,1)} custom-call(bf16[512,1536]{1,0:T(8,128)(2,1)} %copy.43.query_ref, bf16[1536,256]{1,0:T(8,128)(2,1)} %maximum_maximum_fusion.keyval_ref, s32[512,1]{1,0:T(8,128)} %copy.44.first_ref), custom_call_target="tpu_custom_call" | custom-call | tf_op jit(solution)/shard_map/pallas_call | solution.py:84
  79.0 6.6 %convolution_convert_fusion = bf16[512,1536]{1,0:T(8,128)(2,1)} fusion(bf16[512,1536]{1,0:T(8,128)(2,1)} %shard_map.95, bf16[1536,1536]{1,0:T(8,128)(2,1)} %param.12), kind=kOutput, calls=%fused_computation.9 | convolution fusion | flops 2416705536 | bytes 7864320 | tf_op jit(solution)/shard_map/dot_general | solution.py:145
  85.6 1.6 %gather_fusion.1 = bf16[128,16,256]{2,1,0:T(8,128)(2,1)} fusion(bf16[129,16,256]{2,1,0:T(8,128)(2,1)S(1)} %concatenate.34, s32[1024]{0:T(1024)S(1)} %pad_clamp_fusion), kind=kCustom, calls=%fused_computation.1 | custom fusion | bytes 2097664 | tf_op jit(solution)/shard_map/gather | solution.py:157
  (26 shorter events, 0.5 us)
Async XLA Ops:
  0.6 27.5 %copy-start = (bf16[1536,256]{1,0:T(8,128)(2,1)S(1)}, bf16[1536,256]{1,0:T(8,128)(2,1)}, u32[]{:S(2)}) copy-start(bf16[1536,256]{1,0:T(8,128)(2,1)} %param.11) | copy-start | bytes 2359300
  0.6 20.8 %copy-start.1 = (bf16[512,1536]{1,0:T(8,128)(2,1)S(1)}, bf16[512,1536]{1,0:T(8,128)(2,1)}, u32[]{:S(2)}) copy-start(bf16[512,1536]{1,0:T(8,128)(2,1)} %param.8) | copy-start | bytes 4718596
  0.7 20.8 %copy-start.3 = (f32[1536]{0:T(1024)S(1)}, f32[1536]{0:T(1024)}, u32[]{:S(2)}) copy-start(f32[1536]{0:T(1024)} %param.9) | copy-start | bytes 18436
  7.6 21.3 %all-to-all-start = ((s32[128,1,128]{2,1,0:T(1,128)}), s32[128,1,128]{2,1,0:T(1,128)S(1)}, u32[]{:S(2)}, u32[]{:S(2)}) async-start(s32[128,1,128]{2,1,0:T(1,128)} %broadcast_select_fusion.2), calls=%async_computation | async-start | bytes 131072 | tf_op jit(solution)/shard_map/all_to_all | solution.py:117
  28.2 2.8 %copy-start.2 = (s32[512]{0:T(512)S(1)}, s32[512]{0:T(512)}, u32[]{:S(2)}) copy-start(s32[512]{0:T(512)} %param.13) | copy-start | bytes 6148
  33.1 23.0 %collective-permute-start.1 = (bf16[512,256]{1,0:T(8,128)(2,1)S(1)}, bf16[512,256]{1,0:T(8,128)(2,1)S(1)}, u32[]{:S(2)}, u32[]{:S(2)}) collective-permute-start(bf16[512,256]{1,0:T(8,128)(2,1)S(1)} %pad_maximum_fusion), channel_id=1, source_target_pairs={{0,1},{1,2},{2,3},{3,4},{4,5},{5,6},{6,7},{7,8},{8,9},{9,10},{10,1... | collective-permute-start | bytes 786440 | tf_op jit(solution)/shard_map/ppermute | solution.py:21
  35.1 21.0 %collective-permute-start = (bf16[512,256]{1,0:T(8,128)(2,1)S(1)}, bf16[512,256]{1,0:T(8,128)(2,1)S(1)}, u32[]{:S(2)}, u32[]{:S(2)}) collective-permute-start(bf16[512,256]{1,0:T(8,128)(2,1)S(1)} %pad_maximum_fusion), channel_id=1, source_target_pairs={{0,2},{1,3},{2,4},{3,5},{4,6},{5,7},{6,8},{7,9},{8,10},{9,11},{10,... | collective-permute-start | bytes 786440 | tf_op jit(solution)/shard_map/ppermute | solution.py:21
  46.2 39.4 %all-to-all-start.1 = ((bf16[128,16,256]{2,1,0:T(8,128)(2,1)}), bf16[128,16,256]{2,1,0:T(8,128)(2,1)S(1)}, u32[]{:S(2)}, u32[]{:S(2)}) async-start(bf16[128,16,256]{2,1,0:T(8,128)(2,1)} %gather_fusion), calls=%async_computation.1 | async-start | bytes 2097152 | tf_op jit(solution)/shard_map/all_to_all | solution.py:152

commit v8 on v7

--- a/solution.py
+++ b/solution.py
@@ -42,7 +42,9 @@
     )
 
 
-def attend_kernel(query_ref, keyval_ref, first_ref, out_ref, *, tile, back, head_count, head_dim):
+def attend_kernel(
+    query_ref, keyval_ref, first_ref, weight_ref, out_ref, *, tile, back, head_count, head_dim
+):
     step = pl.program_id(0)
     span = tile + WINDOW
     key_first = pl.multiple_of(step * tile + back - WINDOW, tile)
@@ -65,13 +67,19 @@
     context = jnp.dot(
         probs.reshape(head_count * tile, span), values, preferred_element_type=jnp.float32
     )
-    for head in range(head_count):
-        out_ref[:, head * head_dim : (head + 1) * head_dim] = context[
-            head * tile : (head + 1) * tile
-        ].astype(out_ref.dtype)
+    context = jnp.concatenate(
+        [
+            context[head * tile : (head + 1) * tile].astype(jnp.bfloat16)
+            for head in range(head_count)
+        ],
+        1,
+    )
+    out_ref[...] = jnp.dot(
+        context, weight_ref[...], preferred_element_type=jnp.float32
+    ).astype(out_ref.dtype)
 
 
-def attend(queries, keyval_rows, first_rel, back, tile=128):
+def attend(queries, keyval_rows, first_rel, weight, back, tile=128):
     row_count, width = queries.shape
     head_dim = keyval_rows.shape[1] // 2
     kernel = functools.partial(
@@ -88,11 +96,12 @@
             pl.BlockSpec((tile, width), lambda i: (i, 0)),
             pl.BlockSpec(keyval_rows.shape, lambda i: (0, 0)),
             pl.BlockSpec((tile, 1), lambda i: (i, 0)),
+            pl.BlockSpec(weight.shape, lambda i: (0, 0)),
         ],
-        out_specs=pl.BlockSpec((tile, width), lambda i: (i, 0)),
-        out_shape=jax.ShapeDtypeStruct((row_count, width), jnp.bfloat16),
+        out_specs=pl.BlockSpec((tile, weight.shape[1]), lambda i: (i, 0)),
+        out_shape=jax.ShapeDtypeStruct((row_count, weight.shape[1]), jnp.bfloat16),
         compiler_params=pltpu.CompilerParams(vmem_limit_bytes=60 * 1024 * 1024),
-    )(queries, keyval_rows, first_rel)
+    )(queries, keyval_rows, first_rel, weight)
 
 
 def body(tokens, norm_gain, w_query, w_key_value, w_out, segment_ids, page_owner, page_slot):
@@ -136,13 +145,13 @@
     blocks = [keyval] + [passed_along(keyval, "seq", hop) for hop in range(1, reach + 1)]
     ordered = blocks[::-1]
     back = reach * row_count
-    context = attend(
+    attn_out = attend(
         queries.reshape(row_count, head_count * head_dim),
         jnp.concatenate(ordered, 0),
         (starts - offset)[:, None],
+        w_out,
         back,
     )
-    attn_out = jnp.dot(context, w_out, preferred_element_type=jnp.float32).astype(jnp.bfloat16)
     page_count = row_count // PAGE
     pages = keyval.reshape(page_count, PAGE, 2 * head_dim)
     pages = jnp.concatenate([pages, jnp.zeros((1, PAGE, 2 * head_dim), pages.dtype)], 0)

time: 89 us -> 88.1 us (0.990)
  matrix products: 13.9 us -> 7.37 us
  Pallas kernels: 21.8 us -> 25.6 us
  other arithmetic: 15.6 us -> 17.4 us
    dot_general x1 -> x0, matrix products: 6.56 us -> none  [body(): jnp.dot(context, w_out, preferred_element_type=jnp.float32)]
    pallas_call x1, Pallas kernels: 21.8 us -> 25.6 us  [attend(): pl.pallas_call(kernel, grid=(row_count // tile,), in_specs=[pl.BlockSpec(...]
    concatenate x1, other arithmetic: 1.04 us -> 2.21 us  [body(): jnp.concatenate(ordered, 0)]
  transfers between devices with their start and end apart: 4 -> 4, of which waited for: 0 -> 0; matrix products, arithmetic and copies ran while one was open for 30% -> 24% of each run, Pallas kernels for 25% -> 30%
where the time goes in v8:
time: 88.1 us; the launch traced here: 86.4 us
  Pallas kernels  25.6 us (29%)
  starting transfers between devices  25.5 us (29%)
  other arithmetic  17.4 us (20%)
  local copies, waits for them, and re-layouts  8.14 us (9%)
  matrix products  7.37 us (8%)
  between operations  2.23 us (3%)
    pallas_call x1, Pallas kernels, attend(): pl.pallas_call(kernel, grid=(row_count // tile,), in_specs=[pl.BlockSpec(...  25.6 us
    all_to_all x1, starting transfers between devices, body(): lax.all_to_all(notes, 'seq', split_axis=0, concat_axis=0, tiled=True)  10.2 us
    all_to_all x1, starting transfers between devices, body(): lax.all_to_all(pages[pick], 'seq', split_axis=0, concat_axis=0, tiled=True)  9.84 us
    dot_general x1, matrix products, body(): jnp.dot(normed, w_query, preferred_element_type=jnp.float32)  6.75 us
    ppermute x2, starting transfers between devices, passed_along(): return lax.ppermute(value, axis, pairs)  5.46 us
    sub x1, other arithmetic, rotate(): first_half * cosine - second_half * sine_part  2.35 us
    concatenate x1, other arithmetic, body(): jnp.concatenate(ordered, 0)  2.21 us
    reduce_sum x1, other arithmetic, body(): jnp.sum((segment_ids < segment_ids[-1]).astype(jnp.int32))  1.96 us
  transfers between devices with their start and end apart: 4, of which 0 were waited for; matrix products, arithmetic and copies ran while one was open for 24% of the time, Pallas kernels for 30%

profile of v8, /device:TPU:32, one launch (start us, length us, event | category | flops | bytes accessed | tf_op | source)
XLA Modules:
  0.0 86.4 jit_solution(15019574761359714104)
XLA Ops:
  0.7 1.4 %slice.32 = s32[1]{0:T(128)} slice(s32[512]{0:T(512)} %param.13), slice={[511:512]} | slice | bytes 8 | tf_op jit(solution)/shard_map/slice | solution.py:123
  2.1 2.0 %convert_reduce_fusion.1 = s32[]{:T(128)} fusion(s32[512]{0:T(512)} %param.13, s32[]{:T(128)} %bitcast.1), kind=kLoop, calls=%fused_computation.47 | loop fusion | flops 1535 | bytes 2056 | tf_op jit(solution)/shard_map/reduce_sum | solution.py:116
  4.1 0.7 broadcast_add_fusion
  5.4 0.7 select_reduce_fusion
  6.1 1.5 %broadcast_select_fusion.2 = s32[128,1,128]{2,1,0:T(1,128)} fusion(pred[128]{0:T(512)(128)(4,1)S(1)} %iota_compare_fusion.4, pred[128]{0:T(512)(128)(4,1)S(1)} %get-tuple-element.15, pred[128]{0:T(512)(128)(4,1)S(1)} %get-tuple-element.14, s32[]{:T(128)S(6)} %add.82, s32[]{:T(128)} %bitcast.1, s32[128]{0:T(128)S(1)} %get-tuple-element.5), kind=kLoop, calls=%fused_computation.29 | loop fusion | flops 49152 | bytes 66440 | tf_op jit(solution)/shard_map/jit(_where)/select_n | solution.py:121
  7.6 10.2 %all-to-all-start = ((s32[128,1,128]{2,1,0:T(1,128)}), s32[128,1,128]{2,1,0:T(1,128)S(1)}, u32[]{:S(2)}, u32[]{:S(2)}) async-start(s32[128,1,128]{2,1,0:T(1,128)} %broadcast_select_fusion.2), calls=%async_computation | async-start | bytes 131072 | tf_op jit(solution)/shard_map/all_to_all | solution.py:126
  17.9 1.0 %convert_reduce_fusion = s32[512]{0:T(512)S(1)} fusion(s32[512]{0:T(512)} %param.13), kind=kLoop, calls=%fused_computation.11 | loop fusion | flops 785920 | bytes 4096 | tf_op jit(solution)/shard_map/reduce_sum | solution.py:115
  18.9 0.7 fusion.15
  19.6 1.8 %fusion = f32[512]{0:T(512)S(1)} fusion(bf16[512,1536]{1,0:T(8,128)(2,1)} %param.8), kind=kLoop, calls=%fused_computation.4 | loop fusion | flops 2358784 | bytes 1574912 | tf_op jit(solution)/shard_map/reduce_sum | solution.py:134
  21.4 6.7 %fusion.9 = f32[512,1536]{0,1:T(8,128)} fusion(bf16[1536,1536]{1,0:T(8,128)(2,1)} %param.10, bf16[512,1536]{1,0:T(8,128)(2,1)S(1)} %copy-done.3, f32[1536]{0:T(1024)S(1)} %copy-done.5, f32[512]{0:T(512)S(1)} %add_rsqrt_fusion), kind=kOutput, calls=%fused_computation.18 | convolution fusion | flops 2419064832 | bytes 9445376 | tf_op jit(solution)/shard_map/dot_general | solution.py:136
  28.2 0.6 fusion.7
  28.9 0.2 slice_reduce_fusion
  29.1 0.5 constant_dynamic-slice_fusion
  30.4 0.6 fusion.18
  31.0 0.7 broadcast_subtract_fusion
  31.7 1.2 %subtract_convert_fusion = (bf16[512,64]{1,0:T(8,128)(2,1)S(1)}, bf16[512,64]{1,0:T(8,128)(2,1)S(1)}, f32[512,64]{1,0:T(8,128)S(1)}, f32[512,64]{1,0:T(8,128)S(1)}) fusion(f32[512,256]{1,0:T(8,128)S(1)} %fusion.7, f32[64]{0:T(128)S(1)} %multiply_power_fusion, f32[512]{0:T(512)S(1)} %get-tuple-element.11), kind=kLoop, calls=%fused_computation.26 | loop fusion | flops 294912 | bytes 657664 | tf_op jit(solution)/shard_map/convert.6
  32.9 0.9 pad_maximum_fusion
  33.8 2.0 %collective-permute-start.1 = (bf16[512,256]{1,0:T(8,128)(2,1)}, bf16[512,256]{1,0:T(8,128)(2,1)}, u32[]{:S(2)}, u32[]{:S(2)}) collective-permute-start(bf16[512,256]{1,0:T(8,128)(2,1)} %pad_maximum_fusion), channel_id=1, source_target_pairs={{0,1},{1,2},{2,3},{3,4},{4,5},{5,6},{6,7},{7,8},{8,9},{9,10},{10,1... | collective-permute-start | bytes 786440 | tf_op jit(solution)/shard_map/ppermute | solution.py:21
  35.8 3.4 %collective-permute-start = (bf16[512,256]{1,0:T(8,128)(2,1)}, bf16[512,256]{1,0:T(8,128)(2,1)}, u32[]{:S(2)}, u32[]{:S(2)}) collective-permute-start(bf16[512,256]{1,0:T(8,128)(2,1)} %pad_maximum_fusion), channel_id=1, source_target_pairs={{0,2},{1,3},{2,4},{3,5},{4,6},{5,7},{6,8},{7,9},{8,10},{9,11},{10,... | collective-permute-start | bytes 786440 | tf_op jit(solution)/shard_map/ppermute | solution.py:21
  39.2 0.1 copy.39
  39.5 0.1 fusion.12
  39.6 1.6 %gather_fusion = bf16[128,16,256]{2,1,0:T(8,128)(2,1)} fusion(bf16[33,16,256]{2,1,0:T(8,128)(2,1)S(1)} %fusion.12, s32[1024]{0:T(1024)S(1)} %pad_clamp_fusion.1), kind=kCustom, calls=%fused_computation | custom fusion | bytes 2097664 | tf_op jit(solution)/shard_map/gather | solution.py:161
  41.3 9.8 %all-to-all-start.1 = ((bf16[128,16,256]{2,1,0:T(8,128)(2,1)}), bf16[128,16,256]{2,1,0:T(8,128)(2,1)S(1)}, u32[]{:S(2)}, u32[]{:S(2)}) async-start(bf16[128,16,256]{2,1,0:T(8,128)(2,1)} %gather_fusion), calls=%async_computation.1 | async-start | bytes 2097152 | tf_op jit(solution)/shard_map/all_to_all | solution.py:161
  51.1 2.3 %multiply_subtract_fusion = (f32[512,12,64]{0,2,1:T(8,128)S(1)}, f32[512,12,64]{0,2,1:T(8,128)S(1)}) fusion(f32[512,12,128]{0,2,1:T(8,128)} %bitcast.21, f32[512,64]{0,1:T(8,128)S(1)} %copy.39, f32[512,64]{0,1:T(8,128)S(1)} %copy.38), kind=kLoop, calls=%fused_computation.10 | loop fusion | flops 2359296 | bytes 6553600 | tf_op jit(solution)/shard_map/sub | solution.py:38
  53.5 0.5 fusion.3
  53.9 1.6 %copy.43.query_ref = bf16[512,1536]{1,0:T(8,128)(2,1)} copy(bf16[512,1536]{0,1:T(8,128)(2,1)S(1)} %bitcast.20) | data formatting | bytes 3145728 | tf_op jit(solution)/shard_map/convert_element_type | solution.py:139
  55.5 0.9 copy.44.first_ref
  56.4 0.2 compare_reduce_fusion
  56.6 0.2 fusion.13
  56.8 2.2 %maximum_maximum_fusion.keyval_ref = bf16[1536,256]{1,0:T(8,128)(2,1)} fusion(bf16[512,128]{1,0:T(8,128)(2,1)} %copy-done.2, bf16[512,64]{1,0:T(8,128)(2,1)} %copy-done.1, bf16[512,64]{1,0:T(8,128)(2,1)S(1)} %get-tuple-element.8, bf16[512,256]{1,0:T(8,128)(2,1)} %collective-permute-done.1, bf16[512,256]{1,0:T(8,128)(2,1)} %collective-permute-done), kind=kLoop, calls=%fused_computation.12 | loop fusion | flops 3932160 | bytes 1572864 | tf_op jit(solution)/shard_map/concatenate | solution.py:150
  59.0 25.6 %shard_map.95 = bf16[512,1536]{1,0:T(8,128)(2,1)} custom-call(bf16[512,1536]{1,0:T(8,128)(2,1)} %copy.43.query_ref, bf16[1536,256]{1,0:T(8,128)(2,1)} %maximum_maximum_fusion.keyval_ref, s32[512,1]{1,0:T(8,128)} %copy.44.first_ref, bf16[1536,1536]{1,0:T(8,128)(2,1)} %weight_ref.1), custom_call_target="tpu_custom_call" | custom-call | tf_op jit(solution)/shard_map/pallas_call | solution.py:92
  84.7 1.6 %gather_fusion.1 = bf16[128,16,256]{2,1,0:T(8,128)(2,1)} fusion(bf16[129,16,256]{2,1,0:T(8,128)(2,1)S(1)} %concatenate.34, s32[1024]{0:T(1024)S(1)} %pad_clamp_fusion), kind=kCustom, calls=%fused_computation.1 | custom fusion | bytes 2097664 | tf_op jit(solution)/shard_map/gather | solution.py:166
  (29 shorter events, 0.4 us)
Async XLA Ops:
  0.6 27.5 %copy-start = (bf16[1536,256]{1,0:T(8,128)(2,1)S(1)}, bf16[1536,256]{1,0:T(8,128)(2,1)}, u32[]{:S(2)}) copy-start(bf16[1536,256]{1,0:T(8,128)(2,1)} %param.11) | copy-start | bytes 2359300
  0.6 20.8 %copy-start.3 = (bf16[512,1536]{1,0:T(8,128)(2,1)S(1)}, bf16[512,1536]{1,0:T(8,128)(2,1)}, u32[]{:S(2)}) copy-start(bf16[512,1536]{1,0:T(8,128)(2,1)} %param.8) | copy-start | bytes 4718596
  0.7 20.8 %copy-start.5 = (f32[1536]{0:T(1024)S(1)}, f32[1536]{0:T(1024)}, u32[]{:S(2)}) copy-start(f32[1536]{0:T(1024)} %param.9) | copy-start | bytes 18436
  7.6 21.3 %all-to-all-start = ((s32[128,1,128]{2,1,0:T(1,128)}), s32[128,1,128]{2,1,0:T(1,128)S(1)}, u32[]{:S(2)}, u32[]{:S(2)}) async-start(s32[128,1,128]{2,1,0:T(1,128)} %broadcast_select_fusion.2), calls=%async_computation | async-start | bytes 131072 | tf_op jit(solution)/shard_map/all_to_all | solution.py:126
  28.2 2.8 %copy-start.4 = (s32[512]{0:T(512)S(1)}, s32[512]{0:T(512)}, u32[]{:S(2)}) copy-start(s32[512]{0:T(512)} %param.13) | copy-start | bytes 6148
  28.8 10.8 %copy-start.2 = (bf16[512,128]{1,0:T(8,128)(2,1)}, bf16[512,128]{1,0:T(8,128)(2,1)S(1)}, u32[]{:S(2)}) copy-start(bf16[512,128]{1,0:T(8,128)(2,1)S(1)} %slice.66) | copy-start | bytes 393220
  32.9 8.4 %copy-start.1 = (bf16[512,64]{1,0:T(8,128)(2,1)}, bf16[512,64]{1,0:T(8,128)(2,1)S(1)}, u32[]{:S(2)}) copy-start(bf16[512,64]{1,0:T(8,128)(2,1)S(1)} %get-tuple-element.9) | copy-start | bytes 196612
  33.8 23.0 %collective-permute-start.1 = (bf16[512,256]{1,0:T(8,128)(2,1)}, bf16[512,256]{1,0:T(8,128)(2,1)}, u32[]{:S(2)}, u32[]{:S(2)}) collective-permute-start(bf16[512,256]{1,0:T(8,128)(2,1)} %pad_maximum_fusion), channel_id=1, source_target_pairs={{0,1},{1,2},{2,3},{3,4},{4,5},{5,6},{6,7},{7,8},{8,9},{9,10},{10,1... | collective-permute-start | bytes 786440 | tf_op jit(solution)/shard_map/ppermute | solution.py:21
  35.8 21.0 %collective-permute-start = (bf16[512,256]{1,0:T(8,128)(2,1)}, bf16[512,256]{1,0:T(8,128)(2,1)}, u32[]{:S(2)}, u32[]{:S(2)}) collective-permute-start(bf16[512,256]{1,0:T(8,128)(2,1)} %pad_maximum_fusion), channel_id=1, source_target_pairs={{0,2},{1,3},{2,4},{3,5},{4,6},{5,7},{6,8},{7,9},{8,10},{9,11},{10,... | collective-permute-start | bytes 786440 | tf_op jit(solution)/shard_map/ppermute | solution.py:21
  41.3 43.4 %all-to-all-start.1 = ((bf16[128,16,256]{2,1,0:T(8,128)(2,1)}), bf16[128,16,256]{2,1,0:T(8,128)(2,1)S(1)}, u32[]{:S(2)}, u32[]{:S(2)}) async-start(bf16[128,16,256]{2,1,0:T(8,128)(2,1)} %gather_fusion), calls=%async_computation.1 | async-start | bytes 2097152 | tf_op jit(solution)/shard_map/all_to_all | solution.py:161

commit v9 on v8

--- a/solution.py
+++ b/solution.py
@@ -43,7 +43,19 @@
 
 
 def attend_kernel(
-    query_ref, keyval_ref, first_ref, weight_ref, out_ref, *, tile, back, head_count, head_dim
+    query_ref,
+    keyval_ref,
+    first_ref,
+    weight_ref,
+    out_ref,
+    bias_ref,
+    scores_ref,
+    *,
+    tile,
+    back,
+    head_count,
+    head_dim,
+    chunk,
 ):
     step = pl.program_id(0)
     span = tile + WINDOW
@@ -54,18 +66,24 @@
     query_at = step * tile + lax.broadcasted_iota(jnp.int32, (tile, span), 0)
     key_at = key_first - back + lax.broadcasted_iota(jnp.int32, (tile, span), 1)
     valid = (key_at >= first_ref[...]) & (key_at <= query_at) & (query_at - key_at < WINDOW)
+    bias_ref[...] = jnp.where(valid, 0.0, -1e30).astype(jnp.float32)
     stacked = jnp.concatenate(
         [query_ref[:, head * head_dim : (head + 1) * head_dim] for head in range(head_count)], 0
     )
-    scores = lax.dot_general(
+    scores_ref[...] = lax.dot_general(
         stacked, keys, (((1,), (1,)), ((), ())), preferred_element_type=jnp.float32
-    ).reshape(head_count, tile, span)
-    scores = jnp.where(valid[None], scores, -1e30)
-    peak = jnp.max(scores, 2, keepdims=True)
-    exponent = jnp.exp(scores - peak)
-    probs = (exponent / jnp.sum(exponent, 2, keepdims=True)).astype(jnp.bfloat16)
+    )
+
+    for head in range(head_count):
+        for part in range(tile // chunk):
+            row = head * tile + part * chunk
+            scores = scores_ref[row : row + chunk, :] + bias_ref[part * chunk : (part + 1) * chunk, :]
+            peak = jnp.max(scores, 1, keepdims=True)
+            exponent = jnp.exp(scores - peak)
+            probs = exponent / jnp.sum(exponent, 1, keepdims=True)
+            scores_ref[row : row + chunk, :] = probs
     context = jnp.dot(
-        probs.reshape(head_count * tile, span), values, preferred_element_type=jnp.float32
+        scores_ref[...].astype(jnp.bfloat16), values, preferred_element_type=jnp.float32
     )
     context = jnp.concatenate(
         [
@@ -79,7 +97,7 @@
     ).astype(out_ref.dtype)
 
 
-def attend(queries, keyval_rows, first_rel, weight, back, tile=128):
+def attend(queries, keyval_rows, first_rel, weight, back, tile=128, chunk=32):
     row_count, width = queries.shape
     head_dim = keyval_rows.shape[1] // 2
     kernel = functools.partial(
@@ -88,6 +106,7 @@
         back=back,
         head_count=width // head_dim,
         head_dim=head_dim,
+        chunk=chunk,
     )
     return pl.pallas_call(
         kernel,
@@ -100,6 +119,10 @@
         ],
         out_specs=pl.BlockSpec((tile, weight.shape[1]), lambda i: (i, 0)),
         out_shape=jax.ShapeDtypeStruct((row_count, weight.shape[1]), jnp.bfloat16),
+        scratch_shapes=[
+            pltpu.VMEM((tile, tile + WINDOW), jnp.float32),
+            pltpu.VMEM((width // head_dim * tile, tile + WINDOW), jnp.float32),
+        ],
         compiler_params=pltpu.CompilerParams(vmem_limit_bytes=60 * 1024 * 1024),
     )(queries, keyval_rows, first_rel, weight)
 

time: 88.1 us -> 87.2 us (0.990)
  transfers between devices with their start and end apart: 4 -> 4, of which waited for: 0 -> 0; matrix products, arithmetic and copies ran while one was open for 24% -> 24% of each run, Pallas kernels for 30% -> 29%
where the time goes in v9:
time: 87.2 us; the launch traced here: 85.5 us
  starting transfers between devices  25.5 us (29%)
  Pallas kernels  24.8 us (28%)
  other arithmetic  17.4 us (20%)
  local copies, waits for them, and re-layouts  8.14 us (9%)
  matrix products  7.37 us (8%)
  between operations  2.23 us (3%)
    pallas_call x1, Pallas kernels, attend(): pl.pallas_call(kernel, grid=(row_count // tile,), in_specs=[pl.BlockSpec(...  24.8 us
    all_to_all x1, starting transfers between devices, body(): lax.all_to_all(notes, 'seq', split_axis=0, concat_axis=0, tiled=True)  10.2 us
    all_to_all x1, starting transfers between devices, body(): lax.all_to_all(pages[pick], 'seq', split_axis=0, concat_axis=0, tiled=True)  9.84 us
    dot_general x1, matrix products, body(): jnp.dot(normed, w_query, preferred_element_type=jnp.float32)  6.75 us
    ppermute x2, starting transfers between devices, passed_along(): return lax.ppermute(value, axis, pairs)  5.46 us
    sub x1, other arithmetic, rotate(): first_half * cosine - second_half * sine_part  2.35 us
    concatenate x1, other arithmetic, body(): jnp.concatenate(ordered, 0)  2.21 us
    reduce_sum x1, other arithmetic, body(): jnp.sum((segment_ids < segment_ids[-1]).astype(jnp.int32))  1.96 us
  transfers between devices with their start and end apart: 4, of which 0 were waited for; matrix products, arithmetic and copies ran while one was open for 24% of the time, Pallas kernels for 29%

profile of v9, /device:TPU:32, one launch (start us, length us, event | category | flops | bytes accessed | tf_op | source)
XLA Modules:
  0.0 85.5 jit_solution(3176162930265658613)
XLA Ops:
  0.7 1.4 %slice.32 = s32[1]{0:T(128)} slice(s32[512]{0:T(512)} %param.13), slice={[511:512]} | slice | bytes 8 | tf_op jit(solution)/shard_map/slice | solution.py:146
  2.1 2.0 %convert_reduce_fusion.1 = s32[]{:T(128)} fusion(s32[512]{0:T(512)} %param.13, s32[]{:T(128)} %bitcast.1), kind=kLoop, calls=%fused_computation.47 | loop fusion | flops 1535 | bytes 2056 | tf_op jit(solution)/shard_map/reduce_sum | solution.py:139
  4.1 0.7 broadcast_add_fusion
  5.4 0.7 select_reduce_fusion
  6.1 1.5 %broadcast_select_fusion.2 = s32[128,1,128]{2,1,0:T(1,128)} fusion(pred[128]{0:T(512)(128)(4,1)S(1)} %iota_compare_fusion.4, pred[128]{0:T(512)(128)(4,1)S(1)} %get-tuple-element.15, pred[128]{0:T(512)(128)(4,1)S(1)} %get-tuple-element.14, s32[]{:T(128)S(6)} %add.82, s32[]{:T(128)} %bitcast.1, s32[128]{0:T(128)S(1)} %get-tuple-element.5), kind=kLoop, calls=%fused_computation.29 | loop fusion | flops 49152 | bytes 66440 | tf_op jit(solution)/shard_map/jit(_where)/select_n | solution.py:144
  7.6 10.2 %all-to-all-start = ((s32[128,1,128]{2,1,0:T(1,128)}), s32[128,1,128]{2,1,0:T(1,128)S(1)}, u32[]{:S(2)}, u32[]{:S(2)}) async-start(s32[128,1,128]{2,1,0:T(1,128)} %broadcast_select_fusion.2), calls=%async_computation | async-start | bytes 131072 | tf_op jit(solution)/shard_map/all_to_all | solution.py:149
  17.9 1.0 %convert_reduce_fusion = s32[512]{0:T(512)S(1)} fusion(s32[512]{0:T(512)} %param.13), kind=kLoop, calls=%fused_computation.11 | loop fusion | flops 785920 | bytes 4096 | tf_op jit(solution)/shard_map/reduce_sum | solution.py:138
  18.9 0.7 fusion.15
  19.6 1.8 %fusion = f32[512]{0:T(512)S(1)} fusion(bf16[512,1536]{1,0:T(8,128)(2,1)} %param.8), kind=kLoop, calls=%fused_computation.4 | loop fusion | flops 2358784 | bytes 1574912 | tf_op jit(solution)/shard_map/reduce_sum | solution.py:157
  21.4 6.7 %fusion.9 = f32[512,1536]{0,1:T(8,128)} fusion(bf16[1536,1536]{1,0:T(8,128)(2,1)} %param.10, bf16[512,1536]{1,0:T(8,128)(2,1)S(1)} %copy-done.3, f32[1536]{0:T(1024)S(1)} %copy-done.5, f32[512]{0:T(512)S(1)} %add_rsqrt_fusion), kind=kOutput, calls=%fused_computation.18 | convolution fusion | flops 2419064832 | bytes 9445376 | tf_op jit(solution)/shard_map/dot_general | solution.py:159
  28.2 0.6 fusion.7
  28.9 0.2 slice_reduce_fusion
  29.1 0.5 constant_dynamic-slice_fusion
  30.4 0.6 fusion.18
  31.0 0.7 broadcast_subtract_fusion
  31.7 1.2 %subtract_convert_fusion = (bf16[512,64]{1,0:T(8,128)(2,1)S(1)}, bf16[512,64]{1,0:T(8,128)(2,1)S(1)}, f32[512,64]{1,0:T(8,128)S(1)}, f32[512,64]{1,0:T(8,128)S(1)}) fusion(f32[512,256]{1,0:T(8,128)S(1)} %fusion.7, f32[64]{0:T(128)S(1)} %multiply_power_fusion, f32[512]{0:T(512)S(1)} %get-tuple-element.11), kind=kLoop, calls=%fused_computation.26 | loop fusion | flops 294912 | bytes 657664 | tf_op jit(solution)/shard_map/convert.6
  32.9 0.9 %pad_maximum_fusion = bf16[512,256]{1,0:T(8,128)(2,1)} fusion(bf16[512,128]{1,0:T(8,128)(2,1)S(1)} %slice.66, bf16[512,64]{1,0:T(8,128)(2,1)S(1)} %get-tuple-element.9, bf16[512,64]{1,0:T(8,128)(2,1)S(1)} %get-tuple-element.8), kind=kLoop, calls=%fused_computation.24 | loop fusion | flops 786432 | bytes 524288 | tf_op jit(solution)/shard_map/concatenate | solution.py:164
  33.8 2.0 %collective-permute-start.1 = (bf16[512,256]{1,0:T(8,128)(2,1)}, bf16[512,256]{1,0:T(8,128)(2,1)}, u32[]{:S(2)}, u32[]{:S(2)}) collective-permute-start(bf16[512,256]{1,0:T(8,128)(2,1)} %pad_maximum_fusion), channel_id=1, source_target_pairs={{0,1},{1,2},{2,3},{3,4},{4,5},{5,6},{6,7},{7,8},{8,9},{9,10},{10,1... | collective-permute-start | bytes 786440 | tf_op jit(solution)/shard_map/ppermute | solution.py:21
  35.8 3.4 %collective-permute-start = (bf16[512,256]{1,0:T(8,128)(2,1)}, bf16[512,256]{1,0:T(8,128)(2,1)}, u32[]{:S(2)}, u32[]{:S(2)}) collective-permute-start(bf16[512,256]{1,0:T(8,128)(2,1)} %pad_maximum_fusion), channel_id=1, source_target_pairs={{0,2},{1,3},{2,4},{3,5},{4,6},{5,7},{6,8},{7,9},{8,10},{9,11},{10,... | collective-permute-start | bytes 786440 | tf_op jit(solution)/shard_map/ppermute | solution.py:21
  39.2 0.1 copy.39
  39.5 0.1 fusion.12
  39.6 1.6 %gather_fusion = bf16[128,16,256]{2,1,0:T(8,128)(2,1)} fusion(bf16[33,16,256]{2,1,0:T(8,128)(2,1)S(1)} %fusion.12, s32[1024]{0:T(1024)S(1)} %pad_clamp_fusion.1), kind=kCustom, calls=%fused_computation | custom fusion | bytes 2097664 | tf_op jit(solution)/shard_map/gather | solution.py:184
  41.3 9.8 %all-to-all-start.1 = ((bf16[128,16,256]{2,1,0:T(8,128)(2,1)}), bf16[128,16,256]{2,1,0:T(8,128)(2,1)S(1)}, u32[]{:S(2)}, u32[]{:S(2)}) async-start(bf16[128,16,256]{2,1,0:T(8,128)(2,1)} %gather_fusion), calls=%async_computation.1 | async-start | bytes 2097152 | tf_op jit(solution)/shard_map/all_to_all | solution.py:184
  51.1 2.3 %multiply_subtract_fusion = (f32[512,12,64]{0,2,1:T(8,128)S(1)}, f32[512,12,64]{0,2,1:T(8,128)S(1)}) fusion(f32[512,12,128]{0,2,1:T(8,128)} %bitcast.21, f32[512,64]{0,1:T(8,128)S(1)} %copy.39, f32[512,64]{0,1:T(8,128)S(1)} %copy.38), kind=kLoop, calls=%fused_computation.10 | loop fusion | flops 2359296 | bytes 6553600 | tf_op jit(solution)/shard_map/sub | solution.py:38
  53.5 0.5 fusion.3
  53.9 1.6 %copy.43.query_ref = bf16[512,1536]{1,0:T(8,128)(2,1)} copy(bf16[512,1536]{0,1:T(8,128)(2,1)S(1)} %bitcast.20) | data formatting | bytes 3145728 | tf_op jit(solution)/shard_map/convert_element_type | solution.py:162
  55.5 0.9 %copy.44.first_ref = s32[512,1]{1,0:T(8,128)} copy(s32[512,1]{0,1:T(1,128)S(1)} %bitcast.28) | data formatting | bytes 4096 | tf_op jit(solution)/shard_map/broadcast_in_dim | solution.py:174
  56.4 0.2 compare_reduce_fusion
  56.6 0.2 fusion.13
  56.8 2.2 %maximum_maximum_fusion.keyval_ref = bf16[1536,256]{1,0:T(8,128)(2,1)} fusion(bf16[512,128]{1,0:T(8,128)(2,1)} %copy-done.2, bf16[512,64]{1,0:T(8,128)(2,1)} %copy-done.1, bf16[512,64]{1,0:T(8,128)(2,1)S(1)} %get-tuple-element.8, bf16[512,256]{1,0:T(8,128)(2,1)} %collective-permute-done.1, bf16[512,256]{1,0:T(8,128)(2,1)} %collective-permute-done), kind=kLoop, calls=%fused_computation.12 | loop fusion | flops 3932160 | bytes 1572864 | tf_op jit(solution)/shard_map/concatenate | solution.py:173
  59.0 24.8 %shard_map.95 = bf16[512,1536]{1,0:T(8,128)(2,1)} custom-call(bf16[512,1536]{1,0:T(8,128)(2,1)} %copy.43.query_ref, bf16[1536,256]{1,0:T(8,128)(2,1)} %maximum_maximum_fusion.keyval_ref, s32[512,1]{1,0:T(8,128)} %copy.44.first_ref, bf16[1536,1536]{1,0:T(8,128)(2,1)} %weight_ref.1), custom_call_target="tpu_custom_call" | custom-call | tf_op jit(solution)/shard_map/pallas_call | solution.py:111
  83.9 1.6 %gather_fusion.1 = bf16[128,16,256]{2,1,0:T(8,128)(2,1)} fusion(bf16[129,16,256]{2,1,0:T(8,128)(2,1)S(1)} %concatenate.34, s32[1024]{0:T(1024)S(1)} %pad_clamp_fusion), kind=kCustom, calls=%fused_computation.1 | custom fusion | bytes 2097664 | tf_op jit(solution)/shard_map/gather | solution.py:189
  (29 shorter events, 0.4 us)
Async XLA Ops:
  0.6 27.5 %copy-start = (bf16[1536,256]{1,0:T(8,128)(2,1)S(1)}, bf16[1536,256]{1,0:T(8,128)(2,1)}, u32[]{:S(2)}) copy-start(bf16[1536,256]{1,0:T(8,128)(2,1)} %param.11) | copy-start | bytes 2359300
  0.6 20.8 %copy-start.3 = (bf16[512,1536]{1,0:T(8,128)(2,1)S(1)}, bf16[512,1536]{1,0:T(8,128)(2,1)}, u32[]{:S(2)}) copy-start(bf16[512,1536]{1,0:T(8,128)(2,1)} %param.8) | copy-start | bytes 4718596
  0.7 20.8 %copy-start.5 = (f32[1536]{0:T(1024)S(1)}, f32[1536]{0:T(1024)}, u32[]{:S(2)}) copy-start(f32[1536]{0:T(1024)} %param.9) | copy-start | bytes 18436
  7.6 21.3 %all-to-all-start = ((s32[128,1,128]{2,1,0:T(1,128)}), s32[128,1,128]{2,1,0:T(1,128)S(1)}, u32[]{:S(2)}, u32[]{:S(2)}) async-start(s32[128,1,128]{2,1,0:T(1,128)} %broadcast_select_fusion.2), calls=%async_computation | async-start | bytes 131072 | tf_op jit(solution)/shard_map/all_to_all | solution.py:149
  28.2 2.8 %copy-start.4 = (s32[512]{0:T(512)S(1)}, s32[512]{0:T(512)}, u32[]{:S(2)}) copy-start(s32[512]{0:T(512)} %param.13) | copy-start | bytes 6148
  28.8 10.8 %copy-start.2 = (bf16[512,128]{1,0:T(8,128)(2,1)}, bf16[512,128]{1,0:T(8,128)(2,1)S(1)}, u32[]{:S(2)}) copy-start(bf16[512,128]{1,0:T(8,128)(2,1)S(1)} %slice.66) | copy-start | bytes 393220
  32.9 8.4 %copy-start.1 = (bf16[512,64]{1,0:T(8,128)(2,1)}, bf16[512,64]{1,0:T(8,128)(2,1)S(1)}, u32[]{:S(2)}) copy-start(bf16[512,64]{1,0:T(8,128)(2,1)S(1)} %get-tuple-element.9) | copy-start | bytes 196612
  33.8 23.0 %collective-permute-start.1 = (bf16[512,256]{1,0:T(8,128)(2,1)}, bf16[512,256]{1,0:T(8,128)(2,1)}, u32[]{:S(2)}, u32[]{:S(2)}) collective-permute-start(bf16[512,256]{1,0:T(8,128)(2,1)} %pad_maximum_fusion), channel_id=1, source_target_pairs={{0,1},{1,2},{2,3},{3,4},{4,5},{5,6},{6,7},{7,8},{8,9},{9,10},{10,1... | collective-permute-start | bytes 786440 | tf_op jit(solution)/shard_map/ppermute | solution.py:21
  35.8 21.0 %collective-permute-start = (bf16[512,256]{1,0:T(8,128)(2,1)}, bf16[512,256]{1,0:T(8,128)(2,1)}, u32[]{:S(2)}, u32[]{:S(2)}) collective-permute-start(bf16[512,256]{1,0:T(8,128)(2,1)} %pad_maximum_fusion), channel_id=1, source_target_pairs={{0,2},{1,3},{2,4},{3,5},{4,6},{5,7},{6,8},{7,9},{8,10},{9,11},{10,... | collective-permute-start | bytes 786440 | tf_op jit(solution)/shard_map/ppermute | solution.py:21
  41.3 42.6 %all-to-all-start.1 = ((bf16[128,16,256]{2,1,0:T(8,128)(2,1)}), bf16[128,16,256]{2,1,0:T(8,128)(2,1)S(1)}, u32[]{:S(2)}, u32[]{:S(2)}) async-start(bf16[128,16,256]{2,1,0:T(8,128)(2,1)} %gather_fusion), calls=%async_computation.1 | async-start | bytes 2097152 | tf_op jit(solution)/shard_map/all_to_all | solution.py:184

commit v10 on v9

--- a/solution.py
+++ b/solution.py
@@ -44,10 +44,13 @@
 
 def attend_kernel(
     query_ref,
-    keyval_ref,
-    first_ref,
+    table_ref,
+    early_ref,
+    middle_ref,
+    own_ref,
     weight_ref,
     out_ref,
+    rows_ref,
     bias_ref,
     scores_ref,
     *,
@@ -58,22 +61,36 @@
     chunk,
 ):
     step = pl.program_id(0)
+    block = own_ref.shape[0]
+
+    @pl.when(step == 0)
+    def _():
+        rows_ref[0:block, :] = early_ref[...]
+        rows_ref[block : 2 * block, :] = middle_ref[...]
+        rows_ref[2 * block : 3 * block, :] = own_ref[...]
+
     span = tile + WINDOW
     key_first = pl.multiple_of(step * tile + back - WINDOW, tile)
-    rows = keyval_ref[pl.ds(key_first, span), :]
+    rows = rows_ref[pl.ds(key_first, span), :]
     keys = rows[:, :head_dim]
     values = rows[:, head_dim:]
+    cosine = table_ref[:, 0:head_dim]
+    sine_part = table_ref[:, head_dim : 2 * head_dim]
+    first = table_ref[:, 2 * head_dim : 2 * head_dim + 1].astype(jnp.int32)
     query_at = step * tile + lax.broadcasted_iota(jnp.int32, (tile, span), 0)
     key_at = key_first - back + lax.broadcasted_iota(jnp.int32, (tile, span), 1)
-    valid = (key_at >= first_ref[...]) & (key_at <= query_at) & (query_at - key_at < WINDOW)
+    valid = (key_at >= first) & (key_at <= query_at) & (query_at - key_at < WINDOW)
     bias_ref[...] = jnp.where(valid, 0.0, -1e30).astype(jnp.float32)
-    stacked = jnp.concatenate(
-        [query_ref[:, head * head_dim : (head + 1) * head_dim] for head in range(head_count)], 0
-    )
+    pieces = []
+    for head in range(head_count):
+        vectors = query_ref[:, head * head_dim : (head + 1) * head_dim]
+        swapped = pltpu.roll(vectors, head_dim // 2, 1)
+        turned = vectors * cosine + swapped * sine_part
+        pieces.append((turned * head_dim ** (-0.5)).astype(jnp.bfloat16))
+    stacked = jnp.concatenate(pieces, 0)
     scores_ref[...] = lax.dot_general(
         stacked, keys, (((1,), (1,)), ((), ())), preferred_element_type=jnp.float32
     )
-
     for head in range(head_count):
         for part in range(tile // chunk):
             row = head * tile + part * chunk
@@ -97,9 +114,9 @@
     ).astype(out_ref.dtype)
 
 
-def attend(queries, keyval_rows, first_rel, weight, back, tile=128, chunk=32):
-    row_count, width = queries.shape
-    head_dim = keyval_rows.shape[1] // 2
+def attend(projected, table, blocks, weight, back, tile=128, chunk=32):
+    row_count, width = projected.shape
+    head_dim = blocks[0].shape[1] // 2
     kernel = functools.partial(
         attend_kernel,
         tile=tile,
@@ -108,23 +125,27 @@
         head_dim=head_dim,
         chunk=chunk,
     )
+    whole = pl.BlockSpec(blocks[0].shape, lambda i: (0, 0))
     return pl.pallas_call(
         kernel,
         grid=(row_count // tile,),
         in_specs=[
             pl.BlockSpec((tile, width), lambda i: (i, 0)),
-            pl.BlockSpec(keyval_rows.shape, lambda i: (0, 0)),
-            pl.BlockSpec((tile, 1), lambda i: (i, 0)),
+            pl.BlockSpec((tile, table.shape[1]), lambda i: (i, 0)),
+            whole,
+            whole,
+            whole,
             pl.BlockSpec(weight.shape, lambda i: (0, 0)),
         ],
         out_specs=pl.BlockSpec((tile, weight.shape[1]), lambda i: (i, 0)),
         out_shape=jax.ShapeDtypeStruct((row_count, weight.shape[1]), jnp.bfloat16),
         scratch_shapes=[
+            pltpu.VMEM((len(blocks) * row_count, 2 * head_dim), blocks[0].dtype),
             pltpu.VMEM((tile, tile + WINDOW), jnp.float32),
             pltpu.VMEM((width // head_dim * tile, tile + WINDOW), jnp.float32),
         ],
         compiler_params=pltpu.CompilerParams(vmem_limit_bytes=60 * 1024 * 1024),
-    )(queries, keyval_rows, first_rel, weight)
+    )(projected, table, *blocks, weight)
 
 
 def body(tokens, norm_gain, w_query, w_key_value, w_out, segment_ids, page_owner, page_slot):
@@ -156,10 +177,20 @@
     wide = tokens.astype(jnp.float32)
     mean_square = jnp.mean(wide * wide, -1, keepdims=True)
     normed = (wide * lax.rsqrt(mean_square + EPS) * norm_gain).astype(jnp.bfloat16)
-    queries = jnp.dot(normed, w_query, preferred_element_type=jnp.float32).reshape(
-        row_count, head_count, head_dim
-    )
-    queries = (rotate(queries, positions) * head_dim ** (-0.5)).astype(jnp.bfloat16)
+    queries = jnp.dot(normed, w_query, preferred_element_type=jnp.float32)
+    pair_index = jnp.arange(head_dim // 2, dtype=jnp.float32)
+    frequency = ROPE_BASE ** (-2.0 * pair_index / head_dim)
+    angles = positions.astype(jnp.float32)[:, None] * frequency[None, :]
+    table = jnp.concatenate(
+        [
+            jnp.cos(angles),
+            jnp.cos(angles),
+            -jnp.sin(angles),
+            jnp.sin(angles),
+            jnp.broadcast_to((starts - offset).astype(jnp.float32)[:, None], (row_count, head_dim)),
+        ],
+        1,
+    )
     projected = jnp.dot(normed, w_key_value, preferred_element_type=jnp.float32)
     keyval = jnp.concatenate(
         [rotate(projected[:, :head_dim], positions), projected[:, head_dim:]], 1
@@ -167,14 +198,7 @@
     reach = WINDOW // row_count
     blocks = [keyval] + [passed_along(keyval, "seq", hop) for hop in range(1, reach + 1)]
     ordered = blocks[::-1]
-    back = reach * row_count
-    attn_out = attend(
-        queries.reshape(row_count, head_count * head_dim),
-        jnp.concatenate(ordered, 0),
-        (starts - offset)[:, None],
-        w_out,
-        back,
-    )
+    attn_out = attend(queries, table, ordered, w_out, reach * row_count)
     page_count = row_count // PAGE
     pages = keyval.reshape(page_count, PAGE, 2 * head_dim)
     pages = jnp.concatenate([pages, jnp.zeros((1, PAGE, 2 * head_dim), pages.dtype)], 0)

time: 87.2 us -> 91.6 us (1.050); the launches traced: 85.5 us -> 91.1 us
  waiting for transfers between devices: 0.01 us -> 13.9 us
  other arithmetic: 17.4 us -> 11.7 us
  starting transfers between devices: 25.5 us -> 22 us
  matrix products: 7.37 us -> 9.18 us
  local copies, waits for them, and re-layouts: 8.14 us -> 6.58 us
    ppermute x2, waiting for transfers between devices: 0.01 us -> 10.6 us  [passed_along(): return lax.ppermute(value, axis, pairs)]
    all_to_all x1, starting transfers between devices: 9.84 us -> 6.45 us  [body(): lax.all_to_all(pages[pick], 'seq', split_axis=0, concat_axis=0, tiled=True)]
    all_to_all x1, waiting for transfers between devices: 0.01 us -> 3.32 us  [body(): lax.all_to_all(notes, 'seq', split_axis=0, concat_axis=0, tiled=True)]
    sub x2 -> x0, other arithmetic: 3 us -> none  [the longest x1 2.35 us: rotate(): first_half * cosine - second_half * sine_part]
    concatenate x1 -> x0, other arithmetic: 2.21 us -> none  [body(): jnp.concatenate(ordered, 0)]
    convert_element_type x1 -> x0, local copies, waits for them, and re-layouts: 1.6 us -> none  [body(): (rotate(queries, positions) * head_dim ** (-0.5)).astype(jnp.bfloat16)]
    dot_general x1, matrix products: 0.63 us -> 2.04 us  [body(): projected = jnp.dot(normed, w_key_value, preferred_element_type=jnp.float32)]
    concatenate x0 -> x1, local copies, waits for them, and re-layouts: none -> 1.09 us  [body(): jnp.concatenate([jnp.cos(angles), jnp.cos(angles), -jnp.sin(angles), jnp....]
  transfers between devices with their start and end apart: 4 -> 4, of which waited for: 0 -> 3; matrix products, arithmetic and copies ran while one was open for 24% -> 16% of each run, Pallas kernels for 29% -> 28%
where the time goes in v10:
time: 91.6 us; the launch traced here: 91.1 us
  Pallas kernels  25.5 us (28%)
  starting transfers between devices  22 us (24%)
  waiting for transfers between devices  13.9 us (15%)
  other arithmetic  11.7 us (13%)
  matrix products  9.18 us (10%)
  local copies, waits for them, and re-layouts  6.58 us (7%)
  between operations  2.16 us (2%)
    pallas_call x1, Pallas kernels, attend(): pl.pallas_call(kernel, grid=(row_count // tile,), in_specs=[pl.BlockSpec(...  25.5 us
    ppermute x2, waiting for transfers between devices, passed_along(): return lax.ppermute(value, axis, pairs)  10.6 us
    all_to_all x1, starting transfers between devices, body(): lax.all_to_all(notes, 'seq', split_axis=0, concat_axis=0, tiled=True)  10.2 us
    dot_general x1, matrix products, body(): queries = jnp.dot(normed, w_query, preferred_element_type=jnp.float32)  7.13 us
    all_to_all x1, starting transfers between devices, body(): lax.all_to_all(pages[pick], 'seq', split_axis=0, concat_axis=0, tiled=True)  6.45 us
    ppermute x2, starting transfers between devices, passed_along(): return lax.ppermute(value, axis, pairs)  5.36 us
    all_to_all x1, waiting for transfers between devices, body(): lax.all_to_all(notes, 'seq', split_axis=0, concat_axis=0, tiled=True)  3.32 us
    dot_general x1, matrix products, body(): projected = jnp.dot(normed, w_key_value, preferred_element_type=jnp.float32)  2.04 us
  transfers between devices with their start and end apart: 4, of which 3 were waited for; matrix products, arithmetic and copies ran while one was open for 16% of the time, Pallas kernels for 28%

profile of v10, /device:TPU:32, one launch (start us, length us, event | category | flops | bytes accessed | tf_op | source)
XLA Modules:
  0.0 91.1 jit_solution(9499447982646316366)
XLA Ops:
  0.7 1.3 %slice.25 = s32[1]{0:T(128)} slice(s32[512]{0:T(512)} %param.13), slice={[511:512]} | slice | bytes 8 | tf_op jit(solution)/shard_map/slice | solution.py:167
  2.0 2.0 %convert_reduce_fusion.1 = s32[]{:T(128)} fusion(s32[512]{0:T(512)} %param.13, s32[]{:T(128)} %bitcast), kind=kLoop, calls=%fused_computation.48 | loop fusion | flops 1535 | bytes 2056 | tf_op jit(solution)/shard_map/reduce_sum | solution.py:160
  4.0 0.7 broadcast_add_fusion
  5.3 0.7 select_reduce_fusion
  6.0 1.5 %broadcast_select_fusion.2 = s32[128,1,128]{2,1,0:T(1,128)} fusion(pred[128]{0:T(512)(128)(4,1)S(1)} %iota_compare_fusion.4, pred[128]{0:T(512)(128)(4,1)S(1)} %get-tuple-element.14, pred[128]{0:T(512)(128)(4,1)S(1)} %get-tuple-element.13, s32[]{:T(128)S(6)} %add.79, s32[]{:T(128)} %bitcast, s32[128]{0:T(128)S(1)} %get-tuple-element.5), kind=kLoop, calls=%fused_computation.29 | loop fusion | flops 49152 | bytes 66440 | tf_op jit(solution)/shard_map/jit(_where)/select_n | solution.py:165
  7.5 10.2 %all-to-all-start = ((s32[128,1,128]{2,1,0:T(1,128)}), s32[128,1,128]{2,1,0:T(1,128)S(1)}, u32[]{:S(2)}, u32[]{:S(2)}) async-start(s32[128,1,128]{2,1,0:T(1,128)} %broadcast_select_fusion.2), calls=%async_computation | async-start | bytes 131072 | tf_op jit(solution)/shard_map/all_to_all | solution.py:170
  17.7 1.0 %convert_reduce_fusion = s32[512]{0:T(512)S(1)} fusion(s32[512]{0:T(512)} %param.13), kind=kLoop, calls=%fused_computation.7 | loop fusion | flops 785920 | bytes 4096 | tf_op jit(solution)/shard_map/reduce_sum | solution.py:159
  18.7 0.7 fusion.21
  19.5 1.8 %fusion = f32[512]{0:T(512)S(1)} fusion(bf16[512,1536]{1,0:T(8,128)(2,1)} %param.8), kind=kLoop, calls=%fused_computation.4 | loop fusion | flops 2358784 | bytes 1574912 | tf_op jit(solution)/shard_map/reduce_sum | solution.py:178
  21.3 2.0 %fusion.6 = f32[512,256]{1,0:T(8,128)S(1)} fusion(bf16[1536,256]{1,0:T(8,128)(2,1)S(1)} %copy-done, bf16[512,1536]{1,0:T(8,128)(2,1)} %param.8, f32[1536]{0:T(1024)} %param.9, f32[512]{0:T(512)S(1)} %add_rsqrt_fusion), kind=kOutput, calls=%fused_computation.12 | convolution fusion | flops 405798912 | bytes 2891776 | tf_op jit(solution)/shard_map/dot_general | solution.py:194
  23.4 3.3 %all-to-all-done = s32[128,1,128]{2,1,0:T(1,128)S(1)} async-done(((s32[128,1,128]{2,1,0:T(1,128)}), s32[128,1,128]{2,1,0:T(1,128)S(1)}, u32[]{:S(2)}, u32[]{:S(2)}) %all-to-all-start) | async-done | bytes 65568 | tf_op jit(solution)/shard_map/all_to_all | solution.py:170
  26.8 0.2 slice_reduce_fusion
  26.9 0.5 constant_dynamic-slice_fusion
  28.1 0.1 fusion.20
  28.2 0.6 fusion.24
  28.9 0.7 subtract_convert_fusion
  29.5 1.2 %fusion.16 = (bf16[512,64]{1,0:T(8,128)(2,1)S(1)}, bf16[512,64]{1,0:T(8,128)(2,1)S(1)}, f32[512,64]{1,0:T(8,128)S(1)}, f32[512,64]{1,0:T(8,128)S(1)}, f32[512,64]{1,0:T(8,128)S(1)}) fusion(f32[512,256]{1,0:T(8,128)S(1)} %fusion.6, f32[64]{0:T(128)S(1)} %multiply_power_fusion, f32[512]{0:T(512)S(1)} %get-tuple-element.9), kind=kLoop, calls=%fused_computation.22 | loop fusion | flops 327680 | bytes 788736 | tf_op jit(solution)/shard_map/convert.6
  30.8 0.1 fusion.14
  30.9 1.6 %gather_fusion = bf16[128,16,256]{2,1,0:T(8,128)(2,1)} fusion(bf16[33,16,256]{2,1,0:T(8,128)(2,1)S(1)} %fusion.14, s32[1024]{0:T(1024)S(1)} %pad_clamp_fusion.1), kind=kCustom, calls=%fused_computation | custom fusion | bytes 2097664 | tf_op jit(solution)/shard_map/gather | solution.py:208
  32.5 6.5 %all-to-all-start.1 = ((bf16[128,16,256]{2,1,0:T(8,128)(2,1)}), bf16[128,16,256]{2,1,0:T(8,128)(2,1)S(1)}, u32[]{:S(2)}, u32[]{:S(2)}) async-start(bf16[128,16,256]{2,1,0:T(8,128)(2,1)} %gather_fusion), calls=%async_computation.1 | async-start | bytes 2097152 | tf_op jit(solution)/shard_map/all_to_all | solution.py:208
  39.0 7.1 %fusion.8.query_ref = f32[512,1536]{1,0:T(8,128)} fusion(bf16[1536,1536]{1,0:T(8,128)(2,1)} %param.10, bf16[512,1536]{1,0:T(8,128)(2,1)} %param.8, f32[1536]{0:T(1024)S(1)} %copy-done.4, f32[512]{0:T(512)S(1)} %add_rsqrt_fusion), kind=kOutput, calls=%fused_computation.13 | convolution fusion | flops 2419064832 | bytes 9445376 | tf_op jit(solution)/shard_map/dot_general | solution.py:180
  46.1 0.1 pad_maximum_fusion.own_ref
  46.3 3.4 %collective-permute-start = (bf16[512,256]{1,0:T(8,128)(2,1)S(1)}, bf16[512,256]{1,0:T(8,128)(2,1)S(1)}, u32[]{:S(2)}, u32[]{:S(2)}) collective-permute-start(bf16[512,256]{1,0:T(8,128)(2,1)S(1)} %pad_maximum_fusion.own_ref), channel_id=1, source_target_pairs={{0,2},{1,3},{2,4},{3,5},{4,6},{5,7},{6,8},{7,9},{8,10},{9,11},{10,... | collective-permute-start | bytes 786440 | tf_op jit(solution)/shard_map/ppermute | solution.py:21
  49.8 1.9 %collective-permute-start.1 = (bf16[512,256]{1,0:T(8,128)(2,1)S(1)}, bf16[512,256]{1,0:T(8,128)(2,1)}, u32[]{:S(2)}, u32[]{:S(2)}) collective-permute-start(bf16[512,256]{1,0:T(8,128)(2,1)S(1)} %pad_maximum_fusion.own_ref), channel_id=1, source_target_pairs={{0,1},{1,2},{2,3},{3,4},{4,5},{5,6},{6,7},{7,8},{8,9},{9,10},{10,1... | collective-permute-start | bytes 786440 | tf_op jit(solution)/shard_map/ppermute | solution.py:21
  51.7 0.1 broadcast_in_dim.90
  51.8 1.1 %concatenate.23.table_ref = f32[512,384]{1,0:T(8,128)} concatenate(f32[512,64]{1,0:T(8,128)S(1)} %get-tuple-element.12, f32[512,64]{1,0:T(8,128)S(1)} %get-tuple-element.12, f32[512,64]{1,0:T(8,128)S(1)} %get-tuple-element.11, f32[512,64]{1,0:T(8,128)S(1)} %get-tuple-element.10, f32[512,128]{1,0:T(8,128)S(1)} %broadcast_in_dim.90), dimensions={1} | concatenate | bytes 1572864 | tf_op jit(solution)/shard_map/concatenate | solution.py:184
  52.9 0.2 compare_reduce_fusion
  53.1 0.2 fusion.19
  53.3 8.3 %collective-permute-done.early_ref = bf16[512,256]{1,0:T(8,128)(2,1)S(1)} collective-permute-done((bf16[512,256]{1,0:T(8,128)(2,1)S(1)}, bf16[512,256]{1,0:T(8,128)(2,1)S(1)}, u32[]{:S(2)}, u32[]{:S(2)}) %collective-permute-start) | collective-permute-done | bytes 262176 | tf_op jit(solution)/shard_map/ppermute | solution.py:21
  61.6 2.3 %collective-permute-done.1.middle_ref = bf16[512,256]{1,0:T(8,128)(2,1)} collective-permute-done((bf16[512,256]{1,0:T(8,128)(2,1)S(1)}, bf16[512,256]{1,0:T(8,128)(2,1)}, u32[]{:S(2)}, u32[]{:S(2)}) %collective-permute-start.1) | collective-permute-done | bytes 262176 | tf_op jit(solution)/shard_map/ppermute | solution.py:21
  63.9 25.5 %shard_map.95 = bf16[512,1536]{1,0:T(8,128)(2,1)} custom-call(f32[512,1536]{1,0:T(8,128)} %fusion.8.query_ref, f32[512,384]{1,0:T(8,128)} %concatenate.23.table_ref, bf16[512,256]{1,0:T(8,128)(2,1)} %copy-done.2, bf16[512,256]{1,0:T(8,128)(2,1)} %collective-permute-done.1.middle_ref, bf16[512,256]{1,0:T(8,128)(2,1)} %copy-done.1, bf16[1536,1536]{1,0:T(8,128)(2,1)} %weight_ref.1), custom_call_target="tpu_custom_call" | custom-call | tf_op jit(solution)/shard_map/pallas_call | solution.py:129
  89.5 1.6 %gather_fusion.1 = bf16[128,16,256]{2,1,0:T(8,128)(2,1)} fusion(bf16[129,16,256]{2,1,0:T(8,128)(2,1)S(1)} %concatenate.30, s32[1024]{0:T(1024)S(1)} %pad_clamp_fusion), kind=kCustom, calls=%fused_computation.1 | custom fusion | bytes 2097664 | tf_op jit(solution)/shard_map/gather | solution.py:213
  (22 shorter events, 0.2 us)
Async XLA Ops:
  0.6 20.7 %copy-start = (bf16[1536,256]{1,0:T(8,128)(2,1)S(1)}, bf16[1536,256]{1,0:T(8,128)(2,1)}, u32[]{:S(2)}) copy-start(bf16[1536,256]{1,0:T(8,128)(2,1)} %param.11) | copy-start | bytes 2359300
  7.5 19.2 %all-to-all-start = ((s32[128,1,128]{2,1,0:T(1,128)}), s32[128,1,128]{2,1,0:T(1,128)S(1)}, u32[]{:S(2)}, u32[]{:S(2)}) async-start(s32[128,1,128]{2,1,0:T(1,128)} %broadcast_select_fusion.2), calls=%async_computation | async-start | bytes 131072 | tf_op jit(solution)/shard_map/all_to_all | solution.py:170
  19.5 9.4 %copy-start.3 = (s32[512]{0:T(512)S(1)}, s32[512]{0:T(512)}, u32[]{:S(2)}) copy-start(s32[512]{0:T(512)} %param.13) | copy-start | bytes 6148
  29.5 9.5 %copy-start.4 = (f32[1536]{0:T(1024)S(1)}, f32[1536]{0:T(1024)}, u32[]{:S(2)}) copy-start(f32[1536]{0:T(1024)} %param.9) | copy-start | bytes 18436
  32.5 56.9 %all-to-all-start.1 = ((bf16[128,16,256]{2,1,0:T(8,128)(2,1)}), bf16[128,16,256]{2,1,0:T(8,128)(2,1)S(1)}, u32[]{:S(2)}, u32[]{:S(2)}) async-start(bf16[128,16,256]{2,1,0:T(8,128)(2,1)} %gather_fusion), calls=%async_computation.1 | async-start | bytes 2097152 | tf_op jit(solution)/shard_map/all_to_all | solution.py:208
  46.3 17.6 %copy-start.1 = (bf16[512,256]{1,0:T(8,128)(2,1)}, bf16[512,256]{1,0:T(8,128)(2,1)S(1)}, u32[]{:S(2)}) copy-start(bf16[512,256]{1,0:T(8,128)(2,1)S(1)} %pad_maximum_fusion.own_ref) | copy-start | bytes 786436
  46.3 15.3 %collective-permute-start = (bf16[512,256]{1,0:T(8,128)(2,1)S(1)}, bf16[512,256]{1,0:T(8,128)(2,1)S(1)}, u32[]{:S(2)}, u32[]{:S(2)}) collective-permute-start(bf16[512,256]{1,0:T(8,128)(2,1)S(1)} %pad_maximum_fusion.own_ref), channel_id=1, source_target_pairs={{0,2},{1,3},{2,4},{3,5},{4,6},{5,7},{6,8},{7,9},{8,10},{9,11},{10,... | collective-permute-start | bytes 786440 | tf_op jit(solution)/shard_map/ppermute | solution.py:21
  49.8 14.2 %collective-permute-start.1 = (bf16[512,256]{1,0:T(8,128)(2,1)S(1)}, bf16[512,256]{1,0:T(8,128)(2,1)}, u32[]{:S(2)}, u32[]{:S(2)}) collective-permute-start(bf16[512,256]{1,0:T(8,128)(2,1)S(1)} %pad_maximum_fusion.own_ref), channel_id=1, source_target_pairs={{0,1},{1,2},{2,3},{3,4},{4,5},{5,6},{6,7},{7,8},{8,9},{9,10},{10,1... | collective-permute-start | bytes 786440 | tf_op jit(solution)/shard_map/ppermute | solution.py:21
  61.6 2.3 %copy-start.2 = (bf16[512,256]{1,0:T(8,128)(2,1)}, bf16[512,256]{1,0:T(8,128)(2,1)S(1)}, u32[]{:S(2)}) copy-start(bf16[512,256]{1,0:T(8,128)(2,1)S(1)} %collective-permute-done.early_ref) | copy-start | bytes 786436

commit v11 on v10

--- a/solution.py
+++ b/solution.py
@@ -148,12 +148,11 @@
     )(projected, table, *blocks, weight)
 
 
-def body(tokens, norm_gain, w_query, w_key_value, w_out, segment_ids, page_owner, page_slot):
+def layer(tokens, norm_gain, w_query, w_key_value, w_out, segment_ids, page_owner, page_slot):
     row_count = tokens.shape[0]
     devices = lax.axis_size("seq")
     offset = lax.axis_index("seq") * row_count
     head_dim = w_key_value.shape[1] // 2
-    head_count = w_query.shape[1] // head_dim
     local_index = jnp.arange(row_count, dtype=jnp.int32)
     global_index = offset + local_index
     local_start = jnp.sum((segment_ids[None, :] < segment_ids[:, None]).astype(jnp.int32), 1)
@@ -217,7 +216,7 @@
 def solution(mesh):
     placed = (P("seq", None), P(), P(), P(), P(), P("seq"), P("seq"), P("seq"))
     return jax.shard_map(
-        body,
+        layer,
         mesh=mesh,
         in_specs=placed,
         out_specs=(P("seq", None), P("seq", None)),

time: 91.6 us -> 91.6 us (level)
  no operation moved by 1% of the time
where the time goes in v11:
time: 91.6 us; the launch traced here: 91.1 us
  Pallas kernels  25.5 us (28%)
  starting transfers between devices  22 us (24%)
  waiting for transfers between devices  13.9 us (15%)
  other arithmetic  11.7 us (13%)
  matrix products  9.18 us (10%)
  local copies, waits for them, and re-layouts  6.58 us (7%)
  between operations  2.16 us (2%)
    pallas_call x1, Pallas kernels, attend(): pl.pallas_call(kernel, grid=(row_count // tile,), in_specs=[pl.BlockSpec(...  25.5 us
    ppermute x2, waiting for transfers between devices, passed_along(): return lax.ppermute(value, axis, pairs)  10.6 us
    all_to_all x1, starting transfers between devices, layer(): lax.all_to_all(notes, 'seq', split_axis=0, concat_axis=0, tiled=True)  10.2 us
    dot_general x1, matrix products, layer(): queries = jnp.dot(normed, w_query, preferred_element_type=jnp.float32)  7.13 us
    all_to_all x1, starting transfers between devices, layer(): lax.all_to_all(pages[pick], 'seq', split_axis=0, concat_axis=0, tiled=True)  6.45 us
    ppermute x2, starting transfers between devices, passed_along(): return lax.ppermute(value, axis, pairs)  5.36 us
    all_to_all x1, waiting for transfers between devices, layer(): lax.all_to_all(notes, 'seq', split_axis=0, concat_axis=0, tiled=True)  3.32 us
    dot_general x1, matrix products, layer(): projected = jnp.dot(normed, w_key_value, preferred_element_type=jnp.float32)  2.04 us
  transfers between devices with their start and end apart: 4, of which 3 were waited for; matrix products, arithmetic and copies ran while one was open for 16% of the time, Pallas kernels for 28%

profile of v11, /device:TPU:32, one launch (start us, length us, event | category | flops | bytes accessed | tf_op | source)
XLA Modules:
  0.0 91.1 jit_solution(9499447982646316366)
XLA Ops:
  0.7 1.3 %slice.25 = s32[1]{0:T(128)} slice(s32[512]{0:T(512)} %param.13), slice={[511:512]} | slice | bytes 8 | tf_op jit(solution)/shard_map/slice | solution.py:166
  2.0 2.0 %convert_reduce_fusion.1 = s32[]{:T(128)} fusion(s32[512]{0:T(512)} %param.13, s32[]{:T(128)} %bitcast), kind=kLoop, calls=%fused_computation.48 | loop fusion | flops 1535 | bytes 2056 | tf_op jit(solution)/shard_map/reduce_sum | solution.py:159
  4.0 0.7 broadcast_add_fusion
  5.3 0.7 select_reduce_fusion
  6.0 1.5 %broadcast_select_fusion.2 = s32[128,1,128]{2,1,0:T(1,128)} fusion(pred[128]{0:T(512)(128)(4,1)S(1)} %iota_compare_fusion.4, pred[128]{0:T(512)(128)(4,1)S(1)} %get-tuple-element.14, pred[128]{0:T(512)(128)(4,1)S(1)} %get-tuple-element.13, s32[]{:T(128)S(6)} %add.79, s32[]{:T(128)} %bitcast, s32[128]{0:T(128)S(1)} %get-tuple-element.5), kind=kLoop, calls=%fused_computation.29 | loop fusion | flops 49152 | bytes 66440 | tf_op jit(solution)/shard_map/jit(_where)/select_n | solution.py:164
  7.5 10.2 %all-to-all-start = ((s32[128,1,128]{2,1,0:T(1,128)}), s32[128,1,128]{2,1,0:T(1,128)S(1)}, u32[]{:S(2)}, u32[]{:S(2)}) async-start(s32[128,1,128]{2,1,0:T(1,128)} %broadcast_select_fusion.2), calls=%async_computation | async-start | bytes 131072 | tf_op jit(solution)/shard_map/all_to_all | solution.py:169
  17.7 1.0 %convert_reduce_fusion = s32[512]{0:T(512)S(1)} fusion(s32[512]{0:T(512)} %param.13), kind=kLoop, calls=%fused_computation.7 | loop fusion | flops 785920 | bytes 4096 | tf_op jit(solution)/shard_map/reduce_sum | solution.py:158
  18.7 0.7 fusion.21
  19.5 1.8 %fusion = f32[512]{0:T(512)S(1)} fusion(bf16[512,1536]{1,0:T(8,128)(2,1)} %param.8), kind=kLoop, calls=%fused_computation.4 | loop fusion | flops 2358784 | bytes 1574912 | tf_op jit(solution)/shard_map/reduce_sum | solution.py:177
  21.3 2.0 %fusion.6 = f32[512,256]{1,0:T(8,128)S(1)} fusion(bf16[1536,256]{1,0:T(8,128)(2,1)S(1)} %copy-done, bf16[512,1536]{1,0:T(8,128)(2,1)} %param.8, f32[1536]{0:T(1024)} %param.9, f32[512]{0:T(512)S(1)} %add_rsqrt_fusion), kind=kOutput, calls=%fused_computation.12 | convolution fusion | flops 405798912 | bytes 2891776 | tf_op jit(solution)/shard_map/dot_general | solution.py:193
  23.4 3.3 %all-to-all-done = s32[128,1,128]{2,1,0:T(1,128)S(1)} async-done(((s32[128,1,128]{2,1,0:T(1,128)}), s32[128,1,128]{2,1,0:T(1,128)S(1)}, u32[]{:S(2)}, u32[]{:S(2)}) %all-to-all-start) | async-done | bytes 65568 | tf_op jit(solution)/shard_map/all_to_all | solution.py:169
  26.8 0.2 slice_reduce_fusion
  26.9 0.5 constant_dynamic-slice_fusion
  28.1 0.1 fusion.20
  28.2 0.6 fusion.24
  28.9 0.7 subtract_convert_fusion
  29.5 1.2 %fusion.16 = (bf16[512,64]{1,0:T(8,128)(2,1)S(1)}, bf16[512,64]{1,0:T(8,128)(2,1)S(1)}, f32[512,64]{1,0:T(8,128)S(1)}, f32[512,64]{1,0:T(8,128)S(1)}, f32[512,64]{1,0:T(8,128)S(1)}) fusion(f32[512,256]{1,0:T(8,128)S(1)} %fusion.6, f32[64]{0:T(128)S(1)} %multiply_power_fusion, f32[512]{0:T(512)S(1)} %get-tuple-element.9), kind=kLoop, calls=%fused_computation.22 | loop fusion | flops 327680 | bytes 788736 | tf_op jit(solution)/shard_map/convert.6
  30.8 0.1 fusion.14
  30.9 1.6 %gather_fusion = bf16[128,16,256]{2,1,0:T(8,128)(2,1)} fusion(bf16[33,16,256]{2,1,0:T(8,128)(2,1)S(1)} %fusion.14, s32[1024]{0:T(1024)S(1)} %pad_clamp_fusion.1), kind=kCustom, calls=%fused_computation | custom fusion | bytes 2097664 | tf_op jit(solution)/shard_map/gather | solution.py:207
  32.5 6.5 %all-to-all-start.1 = ((bf16[128,16,256]{2,1,0:T(8,128)(2,1)}), bf16[128,16,256]{2,1,0:T(8,128)(2,1)S(1)}, u32[]{:S(2)}, u32[]{:S(2)}) async-start(bf16[128,16,256]{2,1,0:T(8,128)(2,1)} %gather_fusion), calls=%async_computation.1 | async-start | bytes 2097152 | tf_op jit(solution)/shard_map/all_to_all | solution.py:207
  39.0 7.1 %fusion.8.query_ref = f32[512,1536]{1,0:T(8,128)} fusion(bf16[1536,1536]{1,0:T(8,128)(2,1)} %param.10, bf16[512,1536]{1,0:T(8,128)(2,1)} %param.8, f32[1536]{0:T(1024)S(1)} %copy-done.4, f32[512]{0:T(512)S(1)} %add_rsqrt_fusion), kind=kOutput, calls=%fused_computation.13 | convolution fusion | flops 2419064832 | bytes 9445376 | tf_op jit(solution)/shard_map/dot_general | solution.py:179
  46.1 0.1 pad_maximum_fusion.own_ref
  46.3 3.4 %collective-permute-start = (bf16[512,256]{1,0:T(8,128)(2,1)S(1)}, bf16[512,256]{1,0:T(8,128)(2,1)S(1)}, u32[]{:S(2)}, u32[]{:S(2)}) collective-permute-start(bf16[512,256]{1,0:T(8,128)(2,1)S(1)} %pad_maximum_fusion.own_ref), channel_id=1, source_target_pairs={{0,2},{1,3},{2,4},{3,5},{4,6},{5,7},{6,8},{7,9},{8,10},{9,11},{10,... | collective-permute-start | bytes 786440 | tf_op jit(solution)/shard_map/ppermute | solution.py:21
  49.8 1.9 %collective-permute-start.1 = (bf16[512,256]{1,0:T(8,128)(2,1)S(1)}, bf16[512,256]{1,0:T(8,128)(2,1)}, u32[]{:S(2)}, u32[]{:S(2)}) collective-permute-start(bf16[512,256]{1,0:T(8,128)(2,1)S(1)} %pad_maximum_fusion.own_ref), channel_id=1, source_target_pairs={{0,1},{1,2},{2,3},{3,4},{4,5},{5,6},{6,7},{7,8},{8,9},{9,10},{10,1... | collective-permute-start | bytes 786440 | tf_op jit(solution)/shard_map/ppermute | solution.py:21
  51.7 0.1 broadcast_in_dim.90
  51.8 1.1 %concatenate.23.table_ref = f32[512,384]{1,0:T(8,128)} concatenate(f32[512,64]{1,0:T(8,128)S(1)} %get-tuple-element.12, f32[512,64]{1,0:T(8,128)S(1)} %get-tuple-element.12, f32[512,64]{1,0:T(8,128)S(1)} %get-tuple-element.11, f32[512,64]{1,0:T(8,128)S(1)} %get-tuple-element.10, f32[512,128]{1,0:T(8,128)S(1)} %broadcast_in_dim.90), dimensions={1} | concatenate | bytes 1572864 | tf_op jit(solution)/shard_map/concatenate | solution.py:183
  52.9 0.2 compare_reduce_fusion
  53.1 0.2 fusion.19
  53.3 8.3 %collective-permute-done.early_ref = bf16[512,256]{1,0:T(8,128)(2,1)S(1)} collective-permute-done((bf16[512,256]{1,0:T(8,128)(2,1)S(1)}, bf16[512,256]{1,0:T(8,128)(2,1)S(1)}, u32[]{:S(2)}, u32[]{:S(2)}) %collective-permute-start) | collective-permute-done | bytes 262176 | tf_op jit(solution)/shard_map/ppermute | solution.py:21
  61.6 2.3 %collective-permute-done.1.middle_ref = bf16[512,256]{1,0:T(8,128)(2,1)} collective-permute-done((bf16[512,256]{1,0:T(8,128)(2,1)S(1)}, bf16[512,256]{1,0:T(8,128)(2,1)}, u32[]{:S(2)}, u32[]{:S(2)}) %collective-permute-start.1) | collective-permute-done | bytes 262176 | tf_op jit(solution)/shard_map/ppermute | solution.py:21
  63.9 25.5 %shard_map.95 = bf16[512,1536]{1,0:T(8,128)(2,1)} custom-call(f32[512,1536]{1,0:T(8,128)} %fusion.8.query_ref, f32[512,384]{1,0:T(8,128)} %concatenate.23.table_ref, bf16[512,256]{1,0:T(8,128)(2,1)} %copy-done.2, bf16[512,256]{1,0:T(8,128)(2,1)} %collective-permute-done.1.middle_ref, bf16[512,256]{1,0:T(8,128)(2,1)} %copy-done.1, bf16[1536,1536]{1,0:T(8,128)(2,1)} %weight_ref.1), custom_call_target="tpu_custom_call" | custom-call | tf_op jit(solution)/shard_map/pallas_call | solution.py:129
  89.5 1.6 %gather_fusion.1 = bf16[128,16,256]{2,1,0:T(8,128)(2,1)} fusion(bf16[129,16,256]{2,1,0:T(8,128)(2,1)S(1)} %concatenate.30, s32[1024]{0:T(1024)S(1)} %pad_clamp_fusion), kind=kCustom, calls=%fused_computation.1 | custom fusion | bytes 2097664 | tf_op jit(solution)/shard_map/gather | solution.py:212
  (22 shorter events, 0.2 us)
Async XLA Ops:
  0.6 20.7 %copy-start = (bf16[1536,256]{1,0:T(8,128)(2,1)S(1)}, bf16[1536,256]{1,0:T(8,128)(2,1)}, u32[]{:S(2)}) copy-start(bf16[1536,256]{1,0:T(8,128)(2,1)} %param.11) | copy-start | bytes 2359300
  7.5 19.2 %all-to-all-start = ((s32[128,1,128]{2,1,0:T(1,128)}), s32[128,1,128]{2,1,0:T(1,128)S(1)}, u32[]{:S(2)}, u32[]{:S(2)}) async-start(s32[128,1,128]{2,1,0:T(1,128)} %broadcast_select_fusion.2), calls=%async_computation | async-start | bytes 131072 | tf_op jit(solution)/shard_map/all_to_all | solution.py:169
  19.5 9.4 %copy-start.3 = (s32[512]{0:T(512)S(1)}, s32[512]{0:T(512)}, u32[]{:S(2)}) copy-start(s32[512]{0:T(512)} %param.13) | copy-start | bytes 6148
  29.5 9.5 %copy-start.4 = (f32[1536]{0:T(1024)S(1)}, f32[1536]{0:T(1024)}, u32[]{:S(2)}) copy-start(f32[1536]{0:T(1024)} %param.9) | copy-start | bytes 18436
  32.5 56.9 %all-to-all-start.1 = ((bf16[128,16,256]{2,1,0:T(8,128)(2,1)}), bf16[128,16,256]{2,1,0:T(8,128)(2,1)S(1)}, u32[]{:S(2)}, u32[]{:S(2)}) async-start(bf16[128,16,256]{2,1,0:T(8,128)(2,1)} %gather_fusion), calls=%async_computation.1 | async-start | bytes 2097152 | tf_op jit(solution)/shard_map/all_to_all | solution.py:207
  46.3 17.6 %copy-start.1 = (bf16[512,256]{1,0:T(8,128)(2,1)}, bf16[512,256]{1,0:T(8,128)(2,1)S(1)}, u32[]{:S(2)}) copy-start(bf16[512,256]{1,0:T(8,128)(2,1)S(1)} %pad_maximum_fusion.own_ref) | copy-start | bytes 786436
  46.3 15.3 %collective-permute-start = (bf16[512,256]{1,0:T(8,128)(2,1)S(1)}, bf16[512,256]{1,0:T(8,128)(2,1)S(1)}, u32[]{:S(2)}, u32[]{:S(2)}) collective-permute-start(bf16[512,256]{1,0:T(8,128)(2,1)S(1)} %pad_maximum_fusion.own_ref), channel_id=1, source_target_pairs={{0,2},{1,3},{2,4},{3,5},{4,6},{5,7},{6,8},{7,9},{8,10},{9,11},{10,... | collective-permute-start | bytes 786440 | tf_op jit(solution)/shard_map/ppermute | solution.py:21
  49.8 14.2 %collective-permute-start.1 = (bf16[512,256]{1,0:T(8,128)(2,1)S(1)}, bf16[512,256]{1,0:T(8,128)(2,1)}, u32[]{:S(2)}, u32[]{:S(2)}) collective-permute-start(bf16[512,256]{1,0:T(8,128)(2,1)S(1)} %pad_maximum_fusion.own_ref), channel_id=1, source_target_pairs={{0,1},{1,2},{2,3},{3,4},{4,5},{5,6},{6,7},{7,8},{8,9},{9,10},{10,1... | collective-permute-start | bytes 786440 | tf_op jit(solution)/shard_map/ppermute | solution.py:21
  61.6 2.3 %copy-start.2 = (bf16[512,256]{1,0:T(8,128)(2,1)}, bf16[512,256]{1,0:T(8,128)(2,1)S(1)}, u32[]{:S(2)}) copy-start(bf16[512,256]{1,0:T(8,128)(2,1)S(1)} %collective-permute-done.early_ref) | copy-start | bytes 786436

commit v12 on v11

--- a/solution.py
+++ b/solution.py
@@ -156,21 +156,22 @@
     local_index = jnp.arange(row_count, dtype=jnp.int32)
     global_index = offset + local_index
     local_start = jnp.sum((segment_ids[None, :] < segment_ids[:, None]).astype(jnp.int32), 1)
-    last_first = offset + jnp.sum((segment_ids < segment_ids[-1]).astype(jnp.int32))
     place = lax.axis_index("seq")
+    page_count = row_count // PAGE
+    row = jnp.concatenate(
+        [segment_ids, page_owner, page_slot, jnp.zeros((128 - 2 * page_count,), jnp.int32)]
+    )
+    notes = jnp.broadcast_to(row[None, :], (devices, row.shape[0]))
+    heard = lax.all_to_all(notes, "seq", split_axis=0, concat_axis=0, tiled=True)
     owner_hits = page_owner[:, None] == jnp.arange(devices, dtype=jnp.int32)[None, :]
-    slot_to = jnp.sum(jnp.where(owner_hits, page_slot[:, None] + 1, 0), 0)
-    column = lax.broadcasted_iota(jnp.int32, (devices, 128), 1)
-    notes = jnp.where(
-        column == 0,
-        segment_ids[-1],
-        jnp.where(column == 1, last_first, jnp.where(column == 2, slot_to[:, None], 0)),
-    )
-    heard = lax.all_to_all(notes, "seq", split_axis=0, concat_axis=0, tiled=True)
     source = jnp.arange(devices, dtype=jnp.int32)
-    prior_id = jnp.where(place >= 1, heard[jnp.maximum(place - 1, 0), 0], -1)
-    earlier_same = (source < place) & (heard[:, 0] == prior_id)
-    prior_first = jnp.min(jnp.where(earlier_same, heard[:, 1], offset))
+    every_id = heard[:, :row_count]
+    owned_here = heard[:, row_count : row_count + page_count] == place
+    slot_from = jnp.sum(
+        jnp.where(owned_here, heard[:, row_count + page_count : row_count + 2 * page_count] + 1, 0), 1
+    )
+    prior_id = jnp.where(place >= 1, every_id[jnp.maximum(place - 1, 0), row_count - 1], -1)
+    prior_first = jnp.sum((every_id < prior_id).astype(jnp.int32))
     starts = jnp.where(segment_ids == prior_id, prior_first, offset + local_start)
     positions = global_index - starts
     wide = tokens.astype(jnp.float32)
@@ -198,7 +199,6 @@
     blocks = [keyval] + [passed_along(keyval, "seq", hop) for hop in range(1, reach + 1)]
     ordered = blocks[::-1]
     attn_out = attend(queries, table, ordered, w_out, reach * row_count)
-    page_count = row_count // PAGE
     pages = keyval.reshape(page_count, PAGE, 2 * head_dim)
     pages = jnp.concatenate([pages, jnp.zeros((1, PAGE, 2 * head_dim), pages.dtype)], 0)
     page_index = jnp.arange(page_count, dtype=jnp.int32)[:, None]
@@ -206,7 +206,7 @@
     pick = jnp.where(jnp.any(owner_hits, 0), pick, page_count)
     got = lax.all_to_all(pages[pick], "seq", split_axis=0, concat_axis=0, tiled=True)
     got = jnp.concatenate([got, jnp.zeros((1, PAGE, 2 * head_dim), got.dtype)], 0)
-    landed = heard[:, 2][None, :] == source[:, None] + 1
+    landed = slot_from[None, :] == source[:, None] + 1
     from_source = jnp.sum(jnp.where(landed, source[None, :], 0), 1)
     from_source = jnp.where(jnp.any(landed, 1), from_source, devices)
     cache = got[from_source]

time: 91.6 us -> 87.5 us (0.955)
  other arithmetic: 11.7 us -> 8.47 us
  starting transfers between devices: 22 us -> 20.5 us
  waiting for transfers between devices: 13.9 us -> 14.9 us
    all_to_all x1, waiting for transfers between devices: 3.32 us -> 5.45 us  [layer(): lax.all_to_all(notes, 'seq', split_axis=0, concat_axis=0, tiled=True)]
    all_to_all x1, starting transfers between devices: 6.45 us -> 4.9 us  [layer(): lax.all_to_all(pages[pick], 'seq', split_axis=0, concat_axis=0, tiled=True)]
    slice x2 -> x1, local copies, waits for them, and re-layouts: 1.51 us -> 0.02 us  [layer(): every_id = heard[:, :row_count]]
    select_n x1 -> x0, other arithmetic: 1.48 us -> none  [layer(): jnp.where(column == 0, segment_ids[-1], jnp.where(column == 1, last_first...]
    ppermute x2, waiting for transfers between devices: 10.6 us -> 9.43 us  [passed_along(): return lax.ppermute(value, axis, pairs)]
    reduce_sum x1 -> x2, other arithmetic: 1.96 us -> 0.87 us  [the longest x1 0.7 us: layer(): prior_first = jnp.sum((every_id < prior_id).astype(jnp.int32))]
    concatenate x1, local copies, waits for them, and re-layouts: 1.09 us -> 2.1 us  [layer(): jnp.concatenate([jnp.cos(angles), jnp.cos(angles), -jnp.sin(angles), jnp....]
  transfers between devices with their start and end apart: 4 -> 4, of which waited for: 3 -> 3; matrix products, arithmetic and copies ran while one was open for 16% -> 18% of each run, Pallas kernels for 28% -> 29%
where the time goes in v12:
time: 87.5 us; the launch traced here: 87.1 us
  Pallas kernels  25.5 us (29%)
  starting transfers between devices  20.5 us (23%)
  waiting for transfers between devices  14.9 us (17%)
  matrix products  9.18 us (10%)
  other arithmetic  8.47 us (10%)
  local copies, waits for them, and re-layouts  7.09 us (8%)
  between operations  1.51 us (2%)
    pallas_call x1, Pallas kernels, attend(): pl.pallas_call(kernel, grid=(row_count // tile,), in_specs=[pl.BlockSpec(...  25.5 us
    all_to_all x1, starting transfers between devices, layer(): lax.all_to_all(notes, 'seq', split_axis=0, concat_axis=0, tiled=True)  10.2 us
    ppermute x2, waiting for transfers between devices, passed_along(): return lax.ppermute(value, axis, pairs)  9.43 us
    dot_general x1, matrix products, layer(): queries = jnp.dot(normed, w_query, preferred_element_type=jnp.float32)  7.14 us
    all_to_all x1, waiting for transfers between devices, layer(): lax.all_to_all(notes, 'seq', split_axis=0, concat_axis=0, tiled=True)  5.45 us
    ppermute x2, starting transfers between devices, passed_along(): return lax.ppermute(value, axis, pairs)  5.36 us
    all_to_all x1, starting transfers between devices, layer(): lax.all_to_all(pages[pick], 'seq', split_axis=0, concat_axis=0, tiled=True)  4.9 us
    concatenate x1, local copies, waits for them, and re-layouts, layer(): jnp.concatenate([jnp.cos(angles), jnp.cos(angles), -jnp.sin(angles), jnp....  2.1 us
  transfers between devices with their start and end apart: 4, of which 3 were waited for; matrix products, arithmetic and copies ran while one was open for 18% of the time, Pallas kernels for 29%

profile of v12, /device:TPU:32, one launch (start us, length us, event | category | flops | bytes accessed | tf_op | source)
XLA Modules:
  0.0 87.1 jit_solution(2192318225403458659)
XLA Ops:
  0.6 0.0 copy-start
  0.7 0.9 pad_add_fusion
  1.5 0.9 %broadcast_in_dim.46 = s32[128,1,640]{2,1,0:T(1,128)} broadcast(s32[640]{0:T(1024)S(1)} %pad_add_fusion), dimensions={2} | broadcast | bytes 330240 | tf_op jit(solution)/shard_map/broadcast_in_dim | solution.py:164
  2.4 10.2 %all-to-all-start = ((s32[128,1,640]{2,1,0:T(1,128)}), s32[128,1,640]{2,1,0:T(1,128)S(1)}, u32[]{:S(2)}, u32[]{:S(2)}) async-start(s32[128,1,640]{2,1,0:T(1,128)} %broadcast_in_dim.46), calls=%async_computation | async-start | bytes 655360 | tf_op jit(solution)/shard_map/all_to_all | solution.py:165
  12.6 0.0 copy-start.2
  12.7 0.7 fusion.22
  13.4 0.7 select_reduce_fusion
  14.1 1.8 %fusion = f32[512]{0:T(512)S(1)} fusion(bf16[512,1536]{1,0:T(8,128)(2,1)} %param.8), kind=kLoop, calls=%fused_computation.4 | loop fusion | flops 2358784 | bytes 1574912 | tf_op jit(solution)/shard_map/reduce_sum | solution.py:178
  16.0 2.0 %fusion.6 = f32[512,256]{1,0:T(8,128)S(1)} fusion(bf16[1536,256]{1,0:T(8,128)(2,1)S(1)} %copy-done, bf16[512,1536]{1,0:T(8,128)(2,1)} %param.8, f32[1536]{0:T(1024)} %param.9, f32[512]{0:T(512)S(1)} %add_rsqrt_fusion), kind=kOutput, calls=%fused_computation.12 | convolution fusion | flops 405798912 | bytes 2891776 | tf_op jit(solution)/shard_map/dot_general | solution.py:194
  18.1 0.2 convert_reduce_fusion
  18.3 5.4 %all-to-all-done = s32[128,1,640]{2,1,0:T(1,128)S(1)} async-done(((s32[128,1,640]{2,1,0:T(1,128)}), s32[128,1,640]{2,1,0:T(1,128)S(1)}, u32[]{:S(2)}, u32[]{:S(2)}) %all-to-all-start) | async-done | bytes 327712 | tf_op jit(solution)/shard_map/all_to_all | solution.py:165
  23.8 0.6 constant_dynamic-slice_fusion
  25.1 0.7 convert_reduce_fusion.1
  25.8 0.7 subtract_convert_fusion
  26.5 1.9 %fusion.16 = (bf16[512,64]{1,0:T(8,128)(2,1)S(1)}, bf16[512,64]{1,0:T(8,128)(2,1)S(1)}, f32[512,64]{1,0:T(8,128)S(1)}, f32[512,64]{1,0:T(8,128)}, f32[512,64]{1,0:T(8,128)S(1)}) fusion(f32[512,256]{1,0:T(8,128)S(1)} %fusion.6, f32[64]{0:T(128)S(1)} %multiply_power_fusion, f32[512]{0:T(512)S(1)} %get-tuple-element.5), kind=kLoop, calls=%fused_computation.23 | loop fusion | flops 327680 | bytes 788736 | tf_op jit(solution)/shard_map/convert.6
  28.3 0.1 fusion.14
  28.5 1.6 %gather_fusion = bf16[128,16,256]{2,1,0:T(8,128)(2,1)} fusion(bf16[33,16,256]{2,1,0:T(8,128)(2,1)S(1)} %fusion.14, s32[1024]{0:T(1024)S(1)} %pad_clamp_fusion.1), kind=kCustom, calls=%fused_computation | custom fusion | bytes 2097664 | tf_op jit(solution)/shard_map/gather | solution.py:207
  30.1 4.9 %all-to-all-start.1 = ((bf16[128,16,256]{2,1,0:T(8,128)(2,1)}), bf16[128,16,256]{2,1,0:T(8,128)(2,1)S(1)}, u32[]{:S(2)}, u32[]{:S(2)}) async-start(bf16[128,16,256]{2,1,0:T(8,128)(2,1)} %gather_fusion), calls=%async_computation.1 | async-start | bytes 2097152 | tf_op jit(solution)/shard_map/all_to_all | solution.py:207
  35.0 7.1 %fusion.8.query_ref = f32[512,1536]{1,0:T(8,128)} fusion(bf16[1536,1536]{1,0:T(8,128)(2,1)} %param.10, bf16[512,1536]{1,0:T(8,128)(2,1)} %param.8, f32[1536]{0:T(1024)S(1)} %copy-done.3, f32[512]{0:T(512)S(1)} %add_rsqrt_fusion), kind=kOutput, calls=%fused_computation.13 | convolution fusion | flops 2419064832 | bytes 9445376 | tf_op jit(solution)/shard_map/dot_general | solution.py:180
  42.2 0.1 pad_maximum_fusion.own_ref
  42.3 3.4 %collective-permute-start = (bf16[512,256]{1,0:T(8,128)(2,1)S(1)}, bf16[512,256]{1,0:T(8,128)(2,1)}, u32[]{:S(2)}, u32[]{:S(2)}) collective-permute-start(bf16[512,256]{1,0:T(8,128)(2,1)S(1)} %pad_maximum_fusion.own_ref), channel_id=1, source_target_pairs={{0,2},{1,3},{2,4},{3,5},{4,6},{5,7},{6,8},{7,9},{8,10},{9,11},{10,... | collective-permute-start | bytes 786440 | tf_op jit(solution)/shard_map/ppermute | solution.py:21
  45.8 1.9 %collective-permute-start.1 = (bf16[512,256]{1,0:T(8,128)(2,1)S(1)}, bf16[512,256]{1,0:T(8,128)(2,1)}, u32[]{:S(2)}, u32[]{:S(2)}) collective-permute-start(bf16[512,256]{1,0:T(8,128)(2,1)S(1)} %pad_maximum_fusion.own_ref), channel_id=1, source_target_pairs={{0,1},{1,2},{2,3},{3,4},{4,5},{5,6},{6,7},{7,8},{8,9},{9,10},{10,1... | collective-permute-start | bytes 786440 | tf_op jit(solution)/shard_map/ppermute | solution.py:21
  47.7 0.1 broadcast_in_dim.73
  47.8 2.1 %concatenate.27.table_ref = f32[512,384]{1,0:T(8,128)} concatenate(f32[512,64]{1,0:T(8,128)S(1)} %get-tuple-element.8, f32[512,64]{1,0:T(8,128)S(1)} %get-tuple-element.8, f32[512,64]{1,0:T(8,128)} %get-tuple-element.7, f32[512,64]{1,0:T(8,128)S(1)} %get-tuple-element.6, f32[512,128]{1,0:T(8,128)S(1)} %broadcast_in_dim.73), dimensions={1} | concatenate | bytes 1572864 | tf_op jit(solution)/shard_map/concatenate | solution.py:184
  49.9 0.2 fusion.21
  50.1 0.2 compare_reduce_fusion
  50.3 0.2 fusion.19
  50.5 7.2 %collective-permute-done.early_ref = bf16[512,256]{1,0:T(8,128)(2,1)} collective-permute-done((bf16[512,256]{1,0:T(8,128)(2,1)S(1)}, bf16[512,256]{1,0:T(8,128)(2,1)}, u32[]{:S(2)}, u32[]{:S(2)}) %collective-permute-start) | collective-permute-done | bytes 262176 | tf_op jit(solution)/shard_map/ppermute | solution.py:21
  57.7 2.2 %collective-permute-done.1.middle_ref = bf16[512,256]{1,0:T(8,128)(2,1)} collective-permute-done((bf16[512,256]{1,0:T(8,128)(2,1)S(1)}, bf16[512,256]{1,0:T(8,128)(2,1)}, u32[]{:S(2)}, u32[]{:S(2)}) %collective-permute-start.1) | collective-permute-done | bytes 262176 | tf_op jit(solution)/shard_map/ppermute | solution.py:21
  59.9 25.5 %shard_map.95 = bf16[512,1536]{1,0:T(8,128)(2,1)} custom-call(f32[512,1536]{1,0:T(8,128)} %fusion.8.query_ref, f32[512,384]{1,0:T(8,128)} %concatenate.27.table_ref, bf16[512,256]{1,0:T(8,128)(2,1)} %collective-permute-done.early_ref, bf16[512,256]{1,0:T(8,128)(2,1)} %collective-permute-done.1.middle_ref, bf16[512,256]{1,0:T(8,128)(2,1)} %copy-done.1, ...), custom_call_target="tpu_custom_call" | custom-call | tf_op jit(solution)/shard_map/pallas_call | solution.py:129
  85.4 0.1 concatenate.34
  85.5 1.6 %gather_fusion.1 = bf16[128,16,256]{2,1,0:T(8,128)(2,1)} fusion(bf16[129,16,256]{2,1,0:T(8,128)(2,1)S(1)} %concatenate.34, s32[1024]{0:T(1024)S(1)} %pad_clamp_fusion), kind=kCustom, calls=%fused_computation.1 | custom fusion | bytes 2097664 | tf_op jit(solution)/shard_map/gather | solution.py:212
  (18 shorter events, 0.1 us)
Async XLA Ops:
  0.6 15.3 %copy-start = (bf16[1536,256]{1,0:T(8,128)(2,1)S(1)}, bf16[1536,256]{1,0:T(8,128)(2,1)}, u32[]{:S(2)}) copy-start(bf16[1536,256]{1,0:T(8,128)(2,1)} %param.11) | copy-start | bytes 2359300
  2.4 21.4 %all-to-all-start = ((s32[128,1,640]{2,1,0:T(1,128)}), s32[128,1,640]{2,1,0:T(1,128)S(1)}, u32[]{:S(2)}, u32[]{:S(2)}) async-start(s32[128,1,640]{2,1,0:T(1,128)} %broadcast_in_dim.46), calls=%async_computation | async-start | bytes 655360 | tf_op jit(solution)/shard_map/all_to_all | solution.py:165
  12.6 5.4 %copy-start.2 = (s32[512]{0:T(512)S(1)}, s32[512]{0:T(512)}, u32[]{:S(2)}) copy-start(s32[512]{0:T(512)} %param.13) | copy-start | bytes 6148
  26.4 8.6 %copy-start.3 = (f32[1536]{0:T(1024)S(1)}, f32[1536]{0:T(1024)}, u32[]{:S(2)}) copy-start(f32[1536]{0:T(1024)} %param.9) | copy-start | bytes 18436
  30.1 55.3 %all-to-all-start.1 = ((bf16[128,16,256]{2,1,0:T(8,128)(2,1)}), bf16[128,16,256]{2,1,0:T(8,128)(2,1)S(1)}, u32[]{:S(2)}, u32[]{:S(2)}) async-start(bf16[128,16,256]{2,1,0:T(8,128)(2,1)} %gather_fusion), calls=%async_computation.1 | async-start | bytes 2097152 | tf_op jit(solution)/shard_map/all_to_all | solution.py:207
  42.3 17.6 %copy-start.1 = (bf16[512,256]{1,0:T(8,128)(2,1)}, bf16[512,256]{1,0:T(8,128)(2,1)S(1)}, u32[]{:S(2)}) copy-start(bf16[512,256]{1,0:T(8,128)(2,1)S(1)} %pad_maximum_fusion.own_ref) | copy-start | bytes 786436
  42.3 15.4 %collective-permute-start = (bf16[512,256]{1,0:T(8,128)(2,1)S(1)}, bf16[512,256]{1,0:T(8,128)(2,1)}, u32[]{:S(2)}, u32[]{:S(2)}) collective-permute-start(bf16[512,256]{1,0:T(8,128)(2,1)S(1)} %pad_maximum_fusion.own_ref), channel_id=1, source_target_pairs={{0,2},{1,3},{2,4},{3,5},{4,6},{5,7},{6,8},{7,9},{8,10},{9,11},{10,... | collective-permute-start | bytes 786440 | tf_op jit(solution)/shard_map/ppermute | solution.py:21
  45.8 14.2 %collective-permute-start.1 = (bf16[512,256]{1,0:T(8,128)(2,1)S(1)}, bf16[512,256]{1,0:T(8,128)(2,1)}, u32[]{:S(2)}, u32[]{:S(2)}) collective-permute-start(bf16[512,256]{1,0:T(8,128)(2,1)S(1)} %pad_maximum_fusion.own_ref), channel_id=1, source_target_pairs={{0,1},{1,2},{2,3},{3,4},{4,5},{5,6},{6,7},{7,8},{8,9},{9,10},{10,1... | collective-permute-start | bytes 786440 | tf_op jit(solution)/shard_map/ppermute | solution.py:21

commit v13 on v12

--- a/solution.py
+++ b/solution.py
@@ -53,6 +53,7 @@
     rows_ref,
     bias_ref,
     scores_ref,
+    probs_ref,
     *,
     tile,
     back,
@@ -98,10 +99,8 @@
             peak = jnp.max(scores, 1, keepdims=True)
             exponent = jnp.exp(scores - peak)
             probs = exponent / jnp.sum(exponent, 1, keepdims=True)
-            scores_ref[row : row + chunk, :] = probs
-    context = jnp.dot(
-        scores_ref[...].astype(jnp.bfloat16), values, preferred_element_type=jnp.float32
-    )
+            probs_ref[row : row + chunk, :] = probs.astype(jnp.bfloat16)
+    context = jnp.dot(probs_ref[...], values, preferred_element_type=jnp.float32)
     context = jnp.concatenate(
         [
             context[head * tile : (head + 1) * tile].astype(jnp.bfloat16)
@@ -143,6 +142,7 @@
             pltpu.VMEM((len(blocks) * row_count, 2 * head_dim), blocks[0].dtype),
             pltpu.VMEM((tile, tile + WINDOW), jnp.float32),
             pltpu.VMEM((width // head_dim * tile, tile + WINDOW), jnp.float32),
+            pltpu.VMEM((width // head_dim * tile, tile + WINDOW), jnp.bfloat16),
         ],
         compiler_params=pltpu.CompilerParams(vmem_limit_bytes=60 * 1024 * 1024),
     )(projected, table, *blocks, weight)
@@ -157,19 +157,19 @@
     global_index = offset + local_index
     local_start = jnp.sum((segment_ids[None, :] < segment_ids[:, None]).astype(jnp.int32), 1)
     place = lax.axis_index("seq")
-    page_count = row_count // PAGE
-    row = jnp.concatenate(
-        [segment_ids, page_owner, page_slot, jnp.zeros((128 - 2 * page_count,), jnp.int32)]
-    )
-    notes = jnp.broadcast_to(row[None, :], (devices, row.shape[0]))
+    owner_hits = page_owner[:, None] == jnp.arange(devices, dtype=jnp.int32)[None, :]
+    slot_to = jnp.sum(jnp.where(owner_hits, page_slot[:, None] + 1, 0), 0)
+    notes = jnp.concatenate(
+        [
+            jnp.broadcast_to(segment_ids[None, :], (devices, row_count)),
+            jnp.broadcast_to(slot_to[:, None], (devices, 128)),
+        ],
+        1,
+    )
     heard = lax.all_to_all(notes, "seq", split_axis=0, concat_axis=0, tiled=True)
-    owner_hits = page_owner[:, None] == jnp.arange(devices, dtype=jnp.int32)[None, :]
     source = jnp.arange(devices, dtype=jnp.int32)
     every_id = heard[:, :row_count]
-    owned_here = heard[:, row_count : row_count + page_count] == place
-    slot_from = jnp.sum(
-        jnp.where(owned_here, heard[:, row_count + page_count : row_count + 2 * page_count] + 1, 0), 1
-    )
+    slot_from = heard[:, row_count]
     prior_id = jnp.where(place >= 1, every_id[jnp.maximum(place - 1, 0), row_count - 1], -1)
     prior_first = jnp.sum((every_id < prior_id).astype(jnp.int32))
     starts = jnp.where(segment_ids == prior_id, prior_first, offset + local_start)
@@ -199,6 +199,7 @@
     blocks = [keyval] + [passed_along(keyval, "seq", hop) for hop in range(1, reach + 1)]
     ordered = blocks[::-1]
     attn_out = attend(queries, table, ordered, w_out, reach * row_count)
+    page_count = row_count // PAGE
     pages = keyval.reshape(page_count, PAGE, 2 * head_dim)
     pages = jnp.concatenate([pages, jnp.zeros((1, PAGE, 2 * head_dim), pages.dtype)], 0)
     page_index = jnp.arange(page_count, dtype=jnp.int32)[:, None]

time: 87.5 us -> 90.7 us (1.037)
  local copies, waits for them, and re-layouts: 7.09 us -> 8.73 us
  waiting for transfers between devices: 14.9 us -> 16.4 us
  matrix products: 9.18 us -> 7.77 us
    all_to_all x1, waiting for transfers between devices: 5.45 us -> 6.88 us  [layer(): lax.all_to_all(notes, 'seq', split_axis=0, concat_axis=0, tiled=True)]
    dot_general x1, matrix products: 2.04 us -> 0.63 us  [layer(): projected = jnp.dot(normed, w_key_value, preferred_element_type=jnp.float32)]
    another operation x1, other arithmetic: 1.88 us -> 2.84 us
    all_to_all x0 -> x1, local copies, waits for them, and re-layouts: none -> 0.95 us  [layer(): lax.all_to_all(notes, 'seq', split_axis=0, concat_axis=0, tiled=True)]
  transfers between devices with their start and end apart: 4 -> 4, of which waited for: 3 -> 3; matrix products, arithmetic and copies ran while one was open for 18% -> 15% of each run, Pallas kernels for 29% -> 29%
where the time goes in v13:
time: 90.7 us; the launch traced here: 90.3 us
  Pallas kernels  26.1 us (29%)
  starting transfers between devices  20.5 us (23%)
  waiting for transfers between devices  16.4 us (18%)
  other arithmetic  9.24 us (10%)
  local copies, waits for them, and re-layouts  8.73 us (10%)
  matrix products  7.77 us (9%)
  between operations  1.52 us (2%)
    pallas_call x1, Pallas kernels, attend(): pl.pallas_call(kernel, grid=(row_count // tile,), in_specs=[pl.BlockSpec(...  26.1 us
    all_to_all x1, starting transfers between devices, layer(): lax.all_to_all(notes, 'seq', split_axis=0, concat_axis=0, tiled=True)  10.2 us
    ppermute x2, waiting for transfers between devices, passed_along(): return lax.ppermute(value, axis, pairs)  9.51 us
    dot_general x1, matrix products, layer(): queries = jnp.dot(normed, w_query, preferred_element_type=jnp.float32)  7.14 us
    all_to_all x1, waiting for transfers between devices, layer(): lax.all_to_all(notes, 'seq', split_axis=0, concat_axis=0, tiled=True)  6.88 us
    ppermute x2, starting transfers between devices, passed_along(): return lax.ppermute(value, axis, pairs)  5.36 us
    all_to_all x1, starting transfers between devices, layer(): lax.all_to_all(pages[pick], 'seq', split_axis=0, concat_axis=0, tiled=True)  4.9 us
    another operation x1, other arithmetic  2.84 us
  transfers between devices with their start and end apart: 4, of which 3 were waited for; matrix products, arithmetic and copies ran while one was open for 15% of the time, Pallas kernels for 29%

profile of v13, /device:TPU:32, one launch (start us, length us, event | category | flops | bytes accessed | tf_op | source)
XLA Modules:
  0.0 90.3 jit_solution(13062490836833517430)
XLA Ops:
  0.7 0.8 broadcast_add_fusion
  1.5 0.7 select_reduce_fusion
  2.2 0.7 pad.8.clone
  2.9 0.1 broadcast_in_dim.78
  3.0 0.9 %all_to_all.11 = s32[128,1,640]{2,1,0:T(1,128)} reshape(s32[128,640]{1,0:T(8,128)S(1)} %pad_add_fusion) | data formatting | bytes 655360 | tf_op jit(solution)/shard_map/all_to_all | solution.py:169
  4.0 10.2 %all-to-all-start = ((s32[128,1,640]{2,1,0:T(1,128)}), s32[128,1,640]{2,1,0:T(1,128)S(1)}, u32[]{:S(2)}, u32[]{:S(2)}) async-start(s32[128,1,640]{2,1,0:T(1,128)} %all_to_all.11), calls=%async_computation | async-start | bytes 655360 | tf_op jit(solution)/shard_map/all_to_all | solution.py:169
  14.2 0.7 fusion.20
  15.0 1.8 %fusion = f32[512]{0:T(512)S(1)} fusion(bf16[512,1536]{1,0:T(8,128)(2,1)} %param.8), kind=kLoop, calls=%fused_computation.4 | loop fusion | flops 2358784 | bytes 1574912 | tf_op jit(solution)/shard_map/reduce_sum | solution.py:178
  16.8 0.6 fusion.6
  17.5 0.7 copy-done.3
  18.2 0.2 convert_reduce_fusion
  18.5 6.9 %all-to-all-done = s32[128,1,640]{2,1,0:T(1,128)S(1)} async-done(((s32[128,1,640]{2,1,0:T(1,128)}), s32[128,1,640]{2,1,0:T(1,128)S(1)}, u32[]{:S(2)}, u32[]{:S(2)}) %all-to-all-start) | async-done | bytes 327712 | tf_op jit(solution)/shard_map/all_to_all | solution.py:169
  25.4 0.6 constant_dynamic-slice_fusion
  26.6 0.7 convert_reduce_fusion.1
  27.3 0.7 subtract_convert_fusion
  28.0 2.8 %fusion.16 = (bf16[512,64]{1,0:T(8,128)(2,1)S(1)}, bf16[512,64]{1,0:T(8,128)(2,1)S(1)}, f32[512,64]{1,0:T(8,128)S(1)}, f32[512,64]{1,0:T(8,128)}, f32[512,64]{1,0:T(8,128)S(1)}) fusion(f32[512,256]{1,0:T(8,128)} %copy-done.3, f32[64]{0:T(128)S(1)} %multiply_power_fusion, f32[512]{0:T(512)S(1)} %get-tuple-element.7), kind=kLoop, calls=%fused_computation.24 | loop fusion | flops 327680 | bytes 788736 | tf_op jit(solution)/shard_map/convert.6
  30.8 0.1 fusion.14
  31.0 1.6 %gather_fusion = bf16[128,16,256]{2,1,0:T(8,128)(2,1)} fusion(bf16[33,16,256]{2,1,0:T(8,128)(2,1)S(1)} %fusion.14, s32[1024]{0:T(1024)S(1)} %pad_clamp_fusion.1), kind=kCustom, calls=%fused_computation | custom fusion | bytes 2097664 | tf_op jit(solution)/shard_map/gather | solution.py:208
  32.6 4.9 %all-to-all-start.1 = ((bf16[128,16,256]{2,1,0:T(8,128)(2,1)}), bf16[128,16,256]{2,1,0:T(8,128)(2,1)S(1)}, u32[]{:S(2)}, u32[]{:S(2)}) async-start(bf16[128,16,256]{2,1,0:T(8,128)(2,1)} %gather_fusion), calls=%async_computation.1 | async-start | bytes 2097152 | tf_op jit(solution)/shard_map/all_to_all | solution.py:208
  37.5 7.1 %fusion.8.query_ref = f32[512,1536]{1,0:T(8,128)} fusion(bf16[1536,1536]{1,0:T(8,128)(2,1)} %param.10, bf16[512,1536]{1,0:T(8,128)(2,1)} %param.8, f32[1536]{0:T(1024)S(1)} %copy-done.5, f32[512]{0:T(512)S(1)} %add_rsqrt_fusion), kind=kOutput, calls=%fused_computation.13 | convolution fusion | flops 2419064832 | bytes 9445376 | tf_op jit(solution)/shard_map/dot_general | solution.py:180
  44.6 0.1 pad_maximum_fusion.own_ref
  44.8 3.4 %collective-permute-start = (bf16[512,256]{1,0:T(8,128)(2,1)S(1)}, bf16[512,256]{1,0:T(8,128)(2,1)}, u32[]{:S(2)}, u32[]{:S(2)}) collective-permute-start(bf16[512,256]{1,0:T(8,128)(2,1)S(1)} %pad_maximum_fusion.own_ref), channel_id=1, source_target_pairs={{0,2},{1,3},{2,4},{3,5},{4,6},{5,7},{6,8},{7,9},{8,10},{9,11},{10,... | collective-permute-start | bytes 786440 | tf_op jit(solution)/shard_map/ppermute | solution.py:21
  48.2 1.9 %collective-permute-start.1 = (bf16[512,256]{1,0:T(8,128)(2,1)S(1)}, bf16[512,256]{1,0:T(8,128)(2,1)}, u32[]{:S(2)}, u32[]{:S(2)}) collective-permute-start(bf16[512,256]{1,0:T(8,128)(2,1)S(1)} %pad_maximum_fusion.own_ref), channel_id=1, source_target_pairs={{0,1},{1,2},{2,3},{3,4},{4,5},{5,6},{6,7},{7,8},{8,9},{9,10},{10,1... | collective-permute-start | bytes 786440 | tf_op jit(solution)/shard_map/ppermute | solution.py:21
  50.2 0.1 broadcast_in_dim.80
  50.3 2.1 %concatenate.27.table_ref = f32[512,384]{1,0:T(8,128)} concatenate(f32[512,64]{1,0:T(8,128)S(1)} %get-tuple-element.10, f32[512,64]{1,0:T(8,128)S(1)} %get-tuple-element.10, f32[512,64]{1,0:T(8,128)} %get-tuple-element.9, f32[512,64]{1,0:T(8,128)S(1)} %get-tuple-element.8, f32[512,128]{1,0:T(8,128)S(1)} %broadcast_in_dim.80), dimensions={1} | concatenate | bytes 1572864 | tf_op jit(solution)/shard_map/concatenate | solution.py:184
  52.4 0.1 slice_reduce_fusion
  52.5 0.2 compare_reduce_fusion
  52.7 0.2 fusion.19
  52.9 7.3 %collective-permute-done.early_ref = bf16[512,256]{1,0:T(8,128)(2,1)} collective-permute-done((bf16[512,256]{1,0:T(8,128)(2,1)S(1)}, bf16[512,256]{1,0:T(8,128)(2,1)}, u32[]{:S(2)}, u32[]{:S(2)}) %collective-permute-start) | collective-permute-done | bytes 262176 | tf_op jit(solution)/shard_map/ppermute | solution.py:21
  60.2 2.2 %collective-permute-done.1.middle_ref = bf16[512,256]{1,0:T(8,128)(2,1)} collective-permute-done((bf16[512,256]{1,0:T(8,128)(2,1)S(1)}, bf16[512,256]{1,0:T(8,128)(2,1)}, u32[]{:S(2)}, u32[]{:S(2)}) %collective-permute-start.1) | collective-permute-done | bytes 262176 | tf_op jit(solution)/shard_map/ppermute | solution.py:21
  62.4 26.1 %shard_map.95 = bf16[512,1536]{1,0:T(8,128)(2,1)} custom-call(f32[512,1536]{1,0:T(8,128)} %fusion.8.query_ref, f32[512,384]{1,0:T(8,128)} %concatenate.27.table_ref, bf16[512,256]{1,0:T(8,128)(2,1)} %collective-permute-done.early_ref, bf16[512,256]{1,0:T(8,128)(2,1)} %collective-permute-done.1.middle_ref, bf16[512,256]{1,0:T(8,128)(2,1)} %copy-done.2, ...), custom_call_target="tpu_custom_call" | custom-call | tf_op jit(solution)/shard_map/pallas_call | solution.py:128
  88.6 1.6 %gather_fusion.1 = bf16[128,16,256]{2,1,0:T(8,128)(2,1)} fusion(bf16[129,16,256]{2,1,0:T(8,128)(2,1)S(1)} %concatenate.34, s32[1024]{0:T(1024)S(1)} %pad_clamp_fusion), kind=kCustom, calls=%fused_computation.1 | custom fusion | bytes 2097664 | tf_op jit(solution)/shard_map/gather | solution.py:213
  (24 shorter events, 0.2 us)
Async XLA Ops:
  0.6 16.1 %copy-start = (bf16[1536,256]{1,0:T(8,128)(2,1)S(1)}, bf16[1536,256]{1,0:T(8,128)(2,1)}, u32[]{:S(2)}) copy-start(bf16[1536,256]{1,0:T(8,128)(2,1)} %param.11) | copy-start | bytes 2359300
  0.6 16.1 %copy-start.1 = (bf16[512,1536]{1,0:T(8,128)(2,1)S(1)}, bf16[512,1536]{1,0:T(8,128)(2,1)}, u32[]{:S(2)}) copy-start(bf16[512,1536]{1,0:T(8,128)(2,1)} %param.8) | copy-start | bytes 4718596
  0.7 16.1 %copy-start.5 = (f32[1536]{0:T(1024)S(1)}, f32[1536]{0:T(1024)}, u32[]{:S(2)}) copy-start(f32[1536]{0:T(1024)} %param.9) | copy-start | bytes 18436
  4.0 21.4 %all-to-all-start = ((s32[128,1,640]{2,1,0:T(1,128)}), s32[128,1,640]{2,1,0:T(1,128)S(1)}, u32[]{:S(2)}, u32[]{:S(2)}) async-start(s32[128,1,640]{2,1,0:T(1,128)} %all_to_all.11), calls=%async_computation | async-start | bytes 655360 | tf_op jit(solution)/shard_map/all_to_all | solution.py:169
  14.2 4.0 %copy-start.4 = (s32[512]{0:T(512)S(1)}, s32[512]{0:T(512)}, u32[]{:S(2)}) copy-start(s32[512]{0:T(512)} %param.13) | copy-start | bytes 6148
  17.4 0.8 copy-start.3
  32.6 56.0 %all-to-all-start.1 = ((bf16[128,16,256]{2,1,0:T(8,128)(2,1)}), bf16[128,16,256]{2,1,0:T(8,128)(2,1)S(1)}, u32[]{:S(2)}, u32[]{:S(2)}) async-start(bf16[128,16,256]{2,1,0:T(8,128)(2,1)} %gather_fusion), calls=%async_computation.1 | async-start | bytes 2097152 | tf_op jit(solution)/shard_map/all_to_all | solution.py:208
  44.8 17.6 %copy-start.2 = (bf16[512,256]{1,0:T(8,128)(2,1)}, bf16[512,256]{1,0:T(8,128)(2,1)S(1)}, u32[]{:S(2)}) copy-start(bf16[512,256]{1,0:T(8,128)(2,1)S(1)} %pad_maximum_fusion.own_ref) | copy-start | bytes 786436
  44.8 15.4 %collective-permute-start = (bf16[512,256]{1,0:T(8,128)(2,1)S(1)}, bf16[512,256]{1,0:T(8,128)(2,1)}, u32[]{:S(2)}, u32[]{:S(2)}) collective-permute-start(bf16[512,256]{1,0:T(8,128)(2,1)S(1)} %pad_maximum_fusion.own_ref), channel_id=1, source_target_pairs={{0,2},{1,3},{2,4},{3,5},{4,6},{5,7},{6,8},{7,9},{8,10},{9,11},{10,... | collective-permute-start | bytes 786440 | tf_op jit(solution)/shard_map/ppermute | solution.py:21
  48.2 14.2 %collective-permute-start.1 = (bf16[512,256]{1,0:T(8,128)(2,1)S(1)}, bf16[512,256]{1,0:T(8,128)(2,1)}, u32[]{:S(2)}, u32[]{:S(2)}) collective-permute-start(bf16[512,256]{1,0:T(8,128)(2,1)S(1)} %pad_maximum_fusion.own_ref), channel_id=1, source_target_pairs={{0,1},{1,2},{2,3},{3,4},{4,5},{5,6},{6,7},{7,8},{8,9},{9,10},{10,1... | collective-permute-start | bytes 786440 | tf_op jit(solution)/shard_map/ppermute | solution.py:21

commit v14 on v13

--- a/solution.py
+++ b/solution.py
@@ -53,7 +53,6 @@
     rows_ref,
     bias_ref,
     scores_ref,
-    probs_ref,
     *,
     tile,
     back,
@@ -99,8 +98,10 @@
             peak = jnp.max(scores, 1, keepdims=True)
             exponent = jnp.exp(scores - peak)
             probs = exponent / jnp.sum(exponent, 1, keepdims=True)
-            probs_ref[row : row + chunk, :] = probs.astype(jnp.bfloat16)
-    context = jnp.dot(probs_ref[...], values, preferred_element_type=jnp.float32)
+            scores_ref[row : row + chunk, :] = probs
+    context = jnp.dot(
+        scores_ref[...].astype(jnp.bfloat16), values, preferred_element_type=jnp.float32
+    )
     context = jnp.concatenate(
         [
             context[head * tile : (head + 1) * tile].astype(jnp.bfloat16)
@@ -113,7 +114,7 @@
     ).astype(out_ref.dtype)
 
 
-def attend(projected, table, blocks, weight, back, tile=128, chunk=32):
+def attend(projected, table, blocks, weight, back, tile=64, chunk=32):
     row_count, width = projected.shape
     head_dim = blocks[0].shape[1] // 2
     kernel = functools.partial(
@@ -142,7 +143,6 @@
             pltpu.VMEM((len(blocks) * row_count, 2 * head_dim), blocks[0].dtype),
             pltpu.VMEM((tile, tile + WINDOW), jnp.float32),
             pltpu.VMEM((width // head_dim * tile, tile + WINDOW), jnp.float32),
-            pltpu.VMEM((width // head_dim * tile, tile + WINDOW), jnp.bfloat16),
         ],
         compiler_params=pltpu.CompilerParams(vmem_limit_bytes=60 * 1024 * 1024),
     )(projected, table, *blocks, weight)

time: 90.7 us -> 95.8 us (1.056)
  Pallas kernels: 26.1 us -> 31.2 us
    pallas_call x1, Pallas kernels: 26.1 us -> 31.2 us  [attend(): pl.pallas_call(kernel, grid=(row_count // tile,), in_specs=[pl.BlockSpec(...]
  transfers between devices with their start and end apart: 4 -> 4, of which waited for: 3 -> 3; matrix products, arithmetic and copies ran while one was open for 15% -> 14% of each run, Pallas kernels for 29% -> 33%
where the time goes in v14:
time: 95.8 us; the launch traced here: 95.3 us
  Pallas kernels  31.2 us (33%)
  starting transfers between devices  20.5 us (21%)
  waiting for transfers between devices  16.4 us (17%)
  other arithmetic  9.24 us (10%)
  local copies, waits for them, and re-layouts  8.73 us (9%)
  matrix products  7.77 us (8%)
  between operations  1.52 us (2%)
    pallas_call x1, Pallas kernels, attend(): pl.pallas_call(kernel, grid=(row_count // tile,), in_specs=[pl.BlockSpec(...  31.2 us
    all_to_all x1, starting transfers between devices, layer(): lax.all_to_all(notes, 'seq', split_axis=0, concat_axis=0, tiled=True)  10.2 us
    ppermute x2, waiting for transfers between devices, passed_along(): return lax.ppermute(value, axis, pairs)  9.51 us
    dot_general x1, matrix products, layer(): queries = jnp.dot(normed, w_query, preferred_element_type=jnp.float32)  7.14 us
    all_to_all x1, waiting for transfers between devices, layer(): lax.all_to_all(notes, 'seq', split_axis=0, concat_axis=0, tiled=True)  6.88 us
    ppermute x2, starting transfers between devices, passed_along(): return lax.ppermute(value, axis, pairs)  5.36 us
    all_to_all x1, starting transfers between devices, layer(): lax.all_to_all(pages[pick], 'seq', split_axis=0, concat_axis=0, tiled=True)  4.9 us
    another operation x1, other arithmetic  2.84 us
  transfers between devices with their start and end apart: 4, of which 3 were waited for; matrix products, arithmetic and copies ran while one was open for 14% of the time, Pallas kernels for 33%

profile of v14, /device:TPU:32, one launch (start us, length us, event | category | flops | bytes accessed | tf_op | source)
XLA Modules:
  0.0 95.3 jit_solution(5577254290572614226)
XLA Ops:
  0.7 0.8 broadcast_add_fusion
  1.5 0.7 select_reduce_fusion
  2.2 0.7 pad.8.clone
  2.9 0.1 broadcast_in_dim.78
  3.0 0.9 all_to_all.11
  4.0 10.2 %all-to-all-start = ((s32[128,1,640]{2,1,0:T(1,128)}), s32[128,1,640]{2,1,0:T(1,128)S(1)}, u32[]{:S(2)}, u32[]{:S(2)}) async-start(s32[128,1,640]{2,1,0:T(1,128)} %all_to_all.11), calls=%async_computation | async-start | bytes 655360 | tf_op jit(solution)/shard_map/all_to_all | solution.py:169
  14.2 0.7 fusion.20
  15.0 1.8 %fusion = f32[512]{0:T(512)S(1)} fusion(bf16[512,1536]{1,0:T(8,128)(2,1)} %param.8), kind=kLoop, calls=%fused_computation.4 | loop fusion | flops 2358784 | bytes 1574912 | tf_op jit(solution)/shard_map/reduce_sum | solution.py:178
  16.8 0.6 fusion.6
  17.5 0.7 copy-done.3
  18.2 0.2 convert_reduce_fusion
  18.5 6.9 %all-to-all-done = s32[128,1,640]{2,1,0:T(1,128)S(1)} async-done(((s32[128,1,640]{2,1,0:T(1,128)}), s32[128,1,640]{2,1,0:T(1,128)S(1)}, u32[]{:S(2)}, u32[]{:S(2)}) %all-to-all-start) | async-done | bytes 327712 | tf_op jit(solution)/shard_map/all_to_all | solution.py:169
  25.4 0.6 constant_dynamic-slice_fusion
  26.6 0.7 convert_reduce_fusion.1
  27.3 0.7 subtract_convert_fusion
  28.0 2.8 %fusion.16 = (bf16[512,64]{1,0:T(8,128)(2,1)S(1)}, bf16[512,64]{1,0:T(8,128)(2,1)S(1)}, f32[512,64]{1,0:T(8,128)S(1)}, f32[512,64]{1,0:T(8,128)}, f32[512,64]{1,0:T(8,128)S(1)}) fusion(f32[512,256]{1,0:T(8,128)} %copy-done.3, f32[64]{0:T(128)S(1)} %multiply_power_fusion, f32[512]{0:T(512)S(1)} %get-tuple-element.7), kind=kLoop, calls=%fused_computation.24 | loop fusion | flops 327680 | bytes 788736 | tf_op jit(solution)/shard_map/convert.6
  30.8 0.1 fusion.14
  31.0 1.6 %gather_fusion = bf16[128,16,256]{2,1,0:T(8,128)(2,1)} fusion(bf16[33,16,256]{2,1,0:T(8,128)(2,1)S(1)} %fusion.14, s32[1024]{0:T(1024)S(1)} %pad_clamp_fusion.1), kind=kCustom, calls=%fused_computation | custom fusion | bytes 2097664 | tf_op jit(solution)/shard_map/gather | solution.py:208
  32.6 4.9 %all-to-all-start.1 = ((bf16[128,16,256]{2,1,0:T(8,128)(2,1)}), bf16[128,16,256]{2,1,0:T(8,128)(2,1)S(1)}, u32[]{:S(2)}, u32[]{:S(2)}) async-start(bf16[128,16,256]{2,1,0:T(8,128)(2,1)} %gather_fusion), calls=%async_computation.1 | async-start | bytes 2097152 | tf_op jit(solution)/shard_map/all_to_all | solution.py:208
  37.5 7.1 %fusion.8.query_ref = f32[512,1536]{1,0:T(8,128)} fusion(bf16[1536,1536]{1,0:T(8,128)(2,1)} %param.10, bf16[512,1536]{1,0:T(8,128)(2,1)} %param.8, f32[1536]{0:T(1024)S(1)} %copy-done.5, f32[512]{0:T(512)S(1)} %add_rsqrt_fusion), kind=kOutput, calls=%fused_computation.13 | convolution fusion | flops 2419064832 | bytes 9445376 | tf_op jit(solution)/shard_map/dot_general | solution.py:180
  44.6 0.1 pad_maximum_fusion.own_ref
  44.8 3.4 %collective-permute-start = (bf16[512,256]{1,0:T(8,128)(2,1)S(1)}, bf16[512,256]{1,0:T(8,128)(2,1)}, u32[]{:S(2)}, u32[]{:S(2)}) collective-permute-start(bf16[512,256]{1,0:T(8,128)(2,1)S(1)} %pad_maximum_fusion.own_ref), channel_id=1, source_target_pairs={{0,2},{1,3},{2,4},{3,5},{4,6},{5,7},{6,8},{7,9},{8,10},{9,11},{10,... | collective-permute-start | bytes 786440 | tf_op jit(solution)/shard_map/ppermute | solution.py:21
  48.2 1.9 %collective-permute-start.1 = (bf16[512,256]{1,0:T(8,128)(2,1)S(1)}, bf16[512,256]{1,0:T(8,128)(2,1)}, u32[]{:S(2)}, u32[]{:S(2)}) collective-permute-start(bf16[512,256]{1,0:T(8,128)(2,1)S(1)} %pad_maximum_fusion.own_ref), channel_id=1, source_target_pairs={{0,1},{1,2},{2,3},{3,4},{4,5},{5,6},{6,7},{7,8},{8,9},{9,10},{10,1... | collective-permute-start | bytes 786440 | tf_op jit(solution)/shard_map/ppermute | solution.py:21
  50.2 0.1 broadcast_in_dim.80
  50.3 2.1 %concatenate.27.table_ref = f32[512,384]{1,0:T(8,128)} concatenate(f32[512,64]{1,0:T(8,128)S(1)} %get-tuple-element.10, f32[512,64]{1,0:T(8,128)S(1)} %get-tuple-element.10, f32[512,64]{1,0:T(8,128)} %get-tuple-element.9, f32[512,64]{1,0:T(8,128)S(1)} %get-tuple-element.8, f32[512,128]{1,0:T(8,128)S(1)} %broadcast_in_dim.80), dimensions={1} | concatenate | bytes 1572864 | tf_op jit(solution)/shard_map/concatenate | solution.py:184
  52.4 0.1 slice_reduce_fusion
  52.5 0.2 compare_reduce_fusion
  52.7 0.2 fusion.19
  52.9 7.3 %collective-permute-done.early_ref = bf16[512,256]{1,0:T(8,128)(2,1)} collective-permute-done((bf16[512,256]{1,0:T(8,128)(2,1)S(1)}, bf16[512,256]{1,0:T(8,128)(2,1)}, u32[]{:S(2)}, u32[]{:S(2)}) %collective-permute-start) | collective-permute-done | bytes 262176 | tf_op jit(solution)/shard_map/ppermute | solution.py:21
  60.2 2.2 %collective-permute-done.1.middle_ref = bf16[512,256]{1,0:T(8,128)(2,1)} collective-permute-done((bf16[512,256]{1,0:T(8,128)(2,1)S(1)}, bf16[512,256]{1,0:T(8,128)(2,1)}, u32[]{:S(2)}, u32[]{:S(2)}) %collective-permute-start.1) | collective-permute-done | bytes 262176 | tf_op jit(solution)/shard_map/ppermute | solution.py:21
  62.4 31.2 %shard_map.95 = bf16[512,1536]{1,0:T(8,128)(2,1)} custom-call(f32[512,1536]{1,0:T(8,128)} %fusion.8.query_ref, f32[512,384]{1,0:T(8,128)} %concatenate.27.table_ref, bf16[512,256]{1,0:T(8,128)(2,1)} %collective-permute-done.early_ref, bf16[512,256]{1,0:T(8,128)(2,1)} %collective-permute-done.1.middle_ref, bf16[512,256]{1,0:T(8,128)(2,1)} %copy-done.2, ...), custom_call_target="tpu_custom_call" | custom-call | tf_op jit(solution)/shard_map/pallas_call | solution.py:129
  93.7 1.6 %gather_fusion.1 = bf16[128,16,256]{2,1,0:T(8,128)(2,1)} fusion(bf16[129,16,256]{2,1,0:T(8,128)(2,1)S(1)} %concatenate.34, s32[1024]{0:T(1024)S(1)} %pad_clamp_fusion), kind=kCustom, calls=%fused_computation.1 | custom fusion | bytes 2097664 | tf_op jit(solution)/shard_map/gather | solution.py:213
  (24 shorter events, 0.2 us)
Async XLA Ops:
  0.6 16.1 %copy-start = (bf16[1536,256]{1,0:T(8,128)(2,1)S(1)}, bf16[1536,256]{1,0:T(8,128)(2,1)}, u32[]{:S(2)}) copy-start(bf16[1536,256]{1,0:T(8,128)(2,1)} %param.11) | copy-start | bytes 2359300
  0.6 16.1 %copy-start.1 = (bf16[512,1536]{1,0:T(8,128)(2,1)S(1)}, bf16[512,1536]{1,0:T(8,128)(2,1)}, u32[]{:S(2)}) copy-start(bf16[512,1536]{1,0:T(8,128)(2,1)} %param.8) | copy-start | bytes 4718596
  0.7 16.1 %copy-start.5 = (f32[1536]{0:T(1024)S(1)}, f32[1536]{0:T(1024)}, u32[]{:S(2)}) copy-start(f32[1536]{0:T(1024)} %param.9) | copy-start | bytes 18436
  4.0 21.4 %all-to-all-start = ((s32[128,1,640]{2,1,0:T(1,128)}), s32[128,1,640]{2,1,0:T(1,128)S(1)}, u32[]{:S(2)}, u32[]{:S(2)}) async-start(s32[128,1,640]{2,1,0:T(1,128)} %all_to_all.11), calls=%async_computation | async-start | bytes 655360 | tf_op jit(solution)/shard_map/all_to_all | solution.py:169
  14.2 4.0 %copy-start.4 = (s32[512]{0:T(512)S(1)}, s32[512]{0:T(512)}, u32[]{:S(2)}) copy-start(s32[512]{0:T(512)} %param.13) | copy-start | bytes 6148
  17.4 0.8 copy-start.3
  32.6 61.1 %all-to-all-start.1 = ((bf16[128,16,256]{2,1,0:T(8,128)(2,1)}), bf16[128,16,256]{2,1,0:T(8,128)(2,1)S(1)}, u32[]{:S(2)}, u32[]{:S(2)}) async-start(bf16[128,16,256]{2,1,0:T(8,128)(2,1)} %gather_fusion), calls=%async_computation.1 | async-start | bytes 2097152 | tf_op jit(solution)/shard_map/all_to_all | solution.py:208
  44.8 17.6 %copy-start.2 = (bf16[512,256]{1,0:T(8,128)(2,1)}, bf16[512,256]{1,0:T(8,128)(2,1)S(1)}, u32[]{:S(2)}) copy-start(bf16[512,256]{1,0:T(8,128)(2,1)S(1)} %pad_maximum_fusion.own_ref) | copy-start | bytes 786436
  44.8 15.4 %collective-permute-start = (bf16[512,256]{1,0:T(8,128)(2,1)S(1)}, bf16[512,256]{1,0:T(8,128)(2,1)}, u32[]{:S(2)}, u32[]{:S(2)}) collective-permute-start(bf16[512,256]{1,0:T(8,128)(2,1)S(1)} %pad_maximum_fusion.own_ref), channel_id=1, source_target_pairs={{0,2},{1,3},{2,4},{3,5},{4,6},{5,7},{6,8},{7,9},{8,10},{9,11},{10,... | collective-permute-start | bytes 786440 | tf_op jit(solution)/shard_map/ppermute | solution.py:21
  48.2 14.2 %collective-permute-start.1 = (bf16[512,256]{1,0:T(8,128)(2,1)S(1)}, bf16[512,256]{1,0:T(8,128)(2,1)}, u32[]{:S(2)}, u32[]{:S(2)}) collective-permute-start(bf16[512,256]{1,0:T(8,128)(2,1)S(1)} %pad_maximum_fusion.own_ref), channel_id=1, source_target_pairs={{0,1},{1,2},{2,3},{3,4},{4,5},{5,6},{6,7},{7,8},{8,9},{9,10},{10,1... | collective-permute-start | bytes 786440 | tf_op jit(solution)/shard_map/ppermute | solution.py:21
